TPU v7x, 256 devices: a whole 4x4x8 slice. The times are simulated.
256 devices in a mesh: space: 128 (over z, y, x), vel: 2 (over core).
Axes of the slice: x: 4, y: 4, z: 8, core: 2. Of those that a mesh axis runs over, the one named last changes fastest.
Arguments:
- adjoint: bfloat16 [4096, 512, 256], P('vel', 'space'), may hold values from -15 to 15
- collision: float32 [512, 256], P('space'), may hold values from 0.5 to 2
- solid: int32 [512, 256], P('space'), may hold values 0 or 1
- codes: int32 [512, 256], P('space'), may hold values from 0 to 3
Outputs:
- corrected: bfloat16 [4096, 512, 256], P('vel', 'space')
- synthetic: float32 [13, 512, 256], P(None, 'space')
All inputs are finite; a program needn't handle non-finite values. No bound on the sum of `solid` on one device may be relied on, other than what follows from the above.
Results may differ from a plain program's by a relative error of at most 0.0053.
Values may be sent and summed in bfloat16 or wider, within the bound.
No kernel may reach another device: no remote copies, remote signals or barrier semaphores. Data moves between devices by JAX's collectives and lax.ppermute only.
A program may use at most 128 MiB of HBM per device.

v0:
```python
import math

import jax
import jax.numpy as jnp
from jax import lax
from jax.sharding import PartitionSpec as P

NV1 = 16
NM = 13
NY = 16
NZ = 16
SWEEPS = 3


TIME_STEP = 0.06


def with_halo(cells, sides, width):
    for axis, dim in sides:
        count = lax.axis_size(axis)
        ends = count - 1
        head = lax.slice_in_dim(cells, 0, width, axis=dim)
        tail = lax.slice_in_dim(cells, cells.shape[dim] - width, cells.shape[dim], axis=dim)
        cells = jnp.concatenate(
            [
                lax.ppermute(tail, axis, [(i, (i + 1) % count) for i in range(ends)]),
                cells,
                lax.ppermute(head, axis, [((i + 1) % count, i) for i in range(ends)]),
            ],
            axis=dim,
        )
    return cells


def velocity_axes(start, count):
    index = start + jnp.arange(count, dtype=jnp.int32)
    spacing = 9.0 / NV1
    centre = (NV1 - 1) / 2.0
    along_x = ((index % NV1).astype(jnp.float32) - centre) * spacing
    along_z = ((index // NV1 % NV1).astype(jnp.float32) - centre) * spacing
    along_y = ((index // (NV1 * NV1)).astype(jnp.float32) - centre) * spacing
    return (along_x, along_y, along_z)


def tables(start, count):
    along_x, along_y, along_z = velocity_axes(start, count)
    speed = along_x * along_x + along_y * along_y + along_z * along_z
    unity = jnp.ones_like(along_x)
    basis = jnp.stack(
        [
            unity,
            along_x,
            along_y,
            along_z,
            (speed - 3.0) / math.sqrt(6.0),
            along_x * along_y,
            along_x * along_z,
            along_y * along_z,
            (along_x * along_x - along_y * along_y) / math.sqrt(2.0),
            (along_x * along_x + along_y * along_y - 2.0 * along_z * along_z) / math.sqrt(6.0),
            along_x * (speed - 5.0) / math.sqrt(10.0),
            along_y * (speed - 5.0) / math.sqrt(10.0),
            along_z * (speed - 5.0) / math.sqrt(10.0),
        ]
    )
    every_x, every_y, every_z = velocity_axes(0, NV1**3)
    total = jnp.sum(jnp.exp(-0.5 * (every_x * every_x + every_y * every_y + every_z * every_z)))
    weigh = (basis * jnp.exp(-0.5 * speed) / total).astype(jnp.bfloat16)
    lift = jnp.transpose(0.1 * basis * jnp.exp(-0.25 * speed)).astype(jnp.bfloat16)
    return (along_x, along_y, along_z, weigh, lift)


def wall_level(codes):
    return (
        0.5 * (codes == 1).astype(jnp.float32)
        + 1.5 * (codes == 2).astype(jnp.float32)
        + 4.0 * (codes == 3).astype(jnp.float32)
    )


def plane_around(fields):
    count, rows, plane = fields.shape
    cube = fields.reshape(count, rows, NY, NZ)
    padded = jnp.pad(cube, ((0, 0), (0, 0), (1, 1), (1, 1)))
    summed = (
        padded[:, :, 2:, 1:-1]
        + padded[:, :, :-2, 1:-1]
        + padded[:, :, 1:-1, 2:]
        + padded[:, :, 1:-1, :-2]
    )
    return summed.reshape(count, rows, plane)


def sweep_each(fields, source, inverse):
    widened = with_halo(fields.astype(jnp.bfloat16), (("space", 1),), 1).astype(fields.dtype)
    beside_all = widened[:, 2:] + widened[:, :-2] + plane_around(fields)
    return inverse * (source + beside_all)


def on_device(adjoint, collision, solid, codes):
    local_vel, width, plane = adjoint.shape
    start = lax.axis_index("vel") * local_vel
    speed_x, speed_y, speed_z, weigh, lift = tables(start, local_vel)
    half = NV1 // 2
    groups = local_vel // NV1
    grid = adjoint.reshape(groups, NV1, width, plane)
    widened = with_halo(adjoint, (("space", 1),), 1).reshape(groups, NV1, width + 2, plane)
    left_rim = widened[:, :half, 0]
    right_rim = widened[:, half:, width + 1]
    lower = grid[:, :half].astype(jnp.float32)
    upper = grid[:, half:].astype(jnp.float32)
    before = jnp.concatenate([left_rim[:, :, None].astype(jnp.float32), lower[:, :, :-1]], axis=2)
    after = jnp.concatenate([upper[:, :, 1:], right_rim[:, :, None].astype(jnp.float32)], axis=2)
    shaped_x = speed_x.reshape(groups, NV1, 1, 1)
    term_x = jnp.concatenate(
        [shaped_x[:, :half] * (lower - before), shaped_x[:, half:] * (after - upper)], axis=1
    )
    term_x = term_x.reshape(local_vel, width, plane)
    flat = adjoint.astype(jnp.float32)
    cube = flat.reshape(local_vel, width, NY, NZ)
    padded = jnp.pad(cube, ((0, 0), (0, 0), (1, 1), (1, 1)))
    shaped_y = speed_y[:, None, None, None]
    shaped_z = speed_z[:, None, None, None]
    term_y = jnp.maximum(shaped_y, 0.0) * (padded[:, :, 2:, 1:-1] - cube) + jnp.minimum(
        shaped_y, 0.0
    ) * (cube - padded[:, :, :-2, 1:-1])
    term_z = jnp.maximum(shaped_z, 0.0) * (padded[:, :, 1:-1, 2:] - cube) + jnp.minimum(
        shaped_z, 0.0
    ) * (cube - padded[:, :, 1:-1, :-2])
    advect = (
        term_x + term_y.reshape(local_vel, width, plane) + term_z.reshape(local_vel, width, plane)
    )
    fluid = (1 - solid).astype(jnp.float32)
    starred = (fluid[None] * (flat + TIME_STEP * (advect - collision[None] * flat))).astype(
        jnp.bfloat16
    )
    starred_flat = starred.reshape(local_vel, width * plane)
    partial_value = jnp.dot(weigh, starred_flat, preferred_element_type=jnp.float32)
    moments = lax.psum(partial_value, "vel").reshape(NM, width, plane)
    cells_all = width * lax.axis_size("space") * plane
    squares = lax.psum(jnp.sum(moments[0] * moments[0]), "space")
    scale = lax.rsqrt(squares / cells_all + 1e-06)
    inverse = fluid / (collision + wall_level(codes) + 6.0)
    source = collision[None] * moments
    fields = moments * fluid[None]
    for sweep in range(SWEEPS):
        fields = sweep_each(fields, source, inverse[None])
    delta = ((fields - moments) * scale).astype(jnp.bfloat16).reshape(NM, width * plane)
    added = jnp.dot(lift, delta, preferred_element_type=jnp.float32)
    corrected = (fluid.reshape(1, width * plane) * (starred_flat + added)).astype(jnp.bfloat16)
    return (corrected.reshape(local_vel, width, plane), fields * scale)


def solution(mesh):
    return jax.shard_map(
        on_device,
        mesh=mesh,
        in_specs=(P("vel", "space", None), P("space", None), P("space", None), P("space", None)),
        out_specs=(P("vel", "space", None), P(None, "space", None)),
        check_vma=False,
    )
```

profile of v0, /device:TPU:126, one launch (start us, length us, event | category | flops | bytes accessed | tf_op | source)
XLA Modules:
  0.0 528.0 jit_solution(5423196602925413805)
XLA Ops:
  0.6 6.4 %fusion.109 = (bf16[2048,4,256]{2,0,1:T(8,128)(2,1)S(1)}, f32[2048,4,256]{2,0,1:T(8,128)}) fusion(bf16[2048,4,256]{2,1,0:T(4,128)(2,1)} %param.4), kind=kLoop, calls=%fused_computation.205 | loop fusion | flops 2097152 | bytes 16777216 | tf_op args[0]
  7.0 2.0 copy-done
  9.0 1.5 fusion.108
  10.5 4.6 collective-permute-start
  15.1 1.9 collective-permute-start.1
  17.3 0.2 multiply_multiply_fusion.1
  17.8 3.0 slice_convert_fusion.1
  20.8 0.2 slice.163
  21.0 1.9 slice.166
  22.9 8.8 %copy.29 = f32[2048,4,256]{0,2,1:T(8,128)} copy(f32[2048,4,256]{2,0,1:T(8,128)} %get-tuple-element.27) | data formatting | bytes 16777216 | tf_op jit(solution)/shard_map/convert_element_type | solution.py:119
  31.7 20.4 %fusion.2 = (f32[2048,4,16,16]{0,3,2,1:T(8,128)}, f32[2048,4,16,16]{0,3,2,1:T(8,128)}) fusion(f32[2048,4,16,16]{0,3,2,1:T(8,128)} %bitcast.43, f32[2048]{0:T(1024)S(1)} %get-tuple-element.51, f32[2048]{0:T(1024)S(1)} %broadcast_maximum_fusion.1, f32[2048]{0:T(1024)S(1)} %get-tuple-element.41, f32[2048]{0:T(1024)S(1)} %get-tuple-element.50), kind=kLoop, calls=%fused_computation.6 | loop fusion | flops 20971520 | bytes 25198592 | tf_op jit(solution)/shard_map/add | solution.py:124
  52.0 8.7 %copy.30 = f32[2048,4,256]{2,0,1:T(8,128)} copy(f32[2048,4,256]{0,2,1:T(8,128)} %bitcast.45) | data formatting | bytes 16777216 | tf_op jit(solution)/shard_map/reshape | solution.py:131
  60.8 8.7 %copy.31 = f32[2048,4,256]{2,0,1:T(8,128)} copy(f32[2048,4,256]{0,2,1:T(8,128)} %bitcast.44) | data formatting | bytes 16777216 | tf_op jit(solution)/shard_map/reshape | solution.py:131
  69.9 0.2 stack.2
  70.1 0.6 fusion.70
  70.9 3.6 copy.26
  74.5 3.2 copy.27
  77.7 8.2 %pad_maximum_fusion = bf16[2048,6,256]{2,1,0:T(8,128)(2,1)} fusion(bf16[2048,1,256]{2,1,0:T(2,128)(2,1)S(1)} %copy.27, bf16[2048,4,256]{2,1,0:T(4,128)(2,1)S(1)} %copy-done.2, bf16[2048,1,256]{2,1,0:T(2,128)(2,1)S(1)} %copy.26), kind=kLoop, calls=%fused_computation.14 | loop fusion | flops 18874368 | bytes 12582912 | tf_op jit(solution)/shard_map/concatenate | solution.py:24
  85.9 7.6 %copy.28 = bf16[2048,6,256]{2,0,1:T(8,128)(2,1)} copy(bf16[2048,6,256]{2,1,0:T(8,128)(2,1)} %pad_maximum_fusion) | data formatting | bytes 12582912 | tf_op jit(solution)/shard_map/concatenate | solution.py:24
  93.4 1.4 slice_convert_fusion.3
  94.8 3.9 fusion.16
  98.7 2.8 pad_maximum_fusion.1
  101.5 8.8 %fusion.15 = bf16[2048,4,256]{2,0,1:T(8,128)(2,1)} fusion(f32[2048,4,256]{2,0,1:T(8,128)} %copy.31, f32[2048,4,256]{2,0,1:T(8,128)} %copy.30, f32[128,16,4,256]{3,1,0,2:T(8,128)S(1)} %pad_maximum_fusion.1, f32[4,256]{1,0:T(4,128)S(1)} %copy-done.3, f32[4,256]{1,0:T(4,128)S(1)} %get-tuple-element.37, bf16[2048,4,256]{2,1,0:T(4,128)(2,1)S(1)} %copy-done.2), kind=kLoop, calls=%fused_computation.22 | loop fusion | flops 18874368 | bytes 33562624 | tf_op jit(solution)/shard_map/convert_element_type | solution.py:134
  110.3 6.3 %copy.32 = bf16[2048,4,256]{0,2,1:T(8,128)(2,1)} copy(bf16[2048,4,256]{2,0,1:T(8,128)(2,1)} %fusion.15) | data formatting | bytes 8388608 | tf_op jit(solution)/shard_map/convert_element_type | solution.py:134
  116.6 4.0 fusion.31
  120.6 3.8 psum.14
  124.5 0.2 reshape.437
  124.7 0.6 fusion.98
  125.3 9.4 %collective-permute-start.2 = (bf16[13,1,256]{2,1,0:T(2,128)(2,1)S(1)}, bf16[13,1,256]{2,1,0:T(2,128)(2,1)S(1)}, u32[]{:S(2)}, u32[]{:S(2)}) collective-permute-start(bf16[13,1,256]{2,1,0:T(2,128)(2,1)S(1)} %get-tuple-element.34), channel_id=1, source_target_pairs={{0,2},{2,4},{4,6},{6,8},{8,10},{10,12},{12,14},{14,16},{16,18},{18... | collective-permute-start | bytes 19976 | tf_op jit(solution)/shard_map/ppermute | solution.py:26
  134.7 1.9 collective-permute-start.3
  136.6 0.3 fusion.20
  136.9 344.8 %psum.15 = f32[]{:T(128)} all-reduce(f32[]{:T(128)} %fusion.98), channel_id=1, replica_groups=mesh['space'=128,'vel'=2] {'space'}, use_global_device_ids=true, to_apply=%region_3.4 | all-reduce | flops 1 | bytes 8 | tf_op jit(solution)/shard_map/psum | solution.py:141
  481.7 0.2 reshape.438
  482.8 7.4 %collective-permute-start.4 = (bf16[13,1,256]{2,1,0:T(2,128)(2,1)S(1)}, bf16[13,1,256]{2,1,0:T(2,128)(2,1)S(1)}, u32[]{:S(2)}, u32[]{:S(2)}) collective-permute-start(bf16[13,1,256]{2,1,0:T(2,128)(2,1)S(1)} %get-tuple-element.32), channel_id=1, source_target_pairs={{0,2},{2,4},{4,6},{6,8},{8,10},{10,12},{12,14},{14,16},{16,18},{18... | collective-permute-start | bytes 19976 | tf_op jit(solution)/shard_map/ppermute | solution.py:26
  490.2 1.9 collective-permute-start.5
  492.1 0.2 reshape.439
  492.3 0.3 fusion.23
  492.6 0.2 reshape.440
  492.8 8.4 %collective-permute-done.5 = bf16[13,1,256]{2,1,0:T(2,128)(2,1)S(1)} collective-permute-done((bf16[13,1,256]{2,1,0:T(2,128)(2,1)S(1)}, bf16[13,1,256]{2,1,0:T(2,128)(2,1)S(1)}, u32[]{:S(2)}, u32[]{:S(2)}) %collective-permute-start.5) | collective-permute-done | bytes 6688 | tf_op jit(solution)/shard_map/ppermute | solution.py:28
  501.3 1.9 collective-permute-start.6
  503.3 3.9 collective-permute-start.7
  507.2 0.2 reshape.441
  507.4 0.3 fusion.26
  507.7 0.2 reshape.442
  507.9 6.4 %collective-permute-done.7 = bf16[13,1,256]{2,1,0:T(2,128)(2,1)S(1)} collective-permute-done((bf16[13,1,256]{2,1,0:T(2,128)(2,1)S(1)}, bf16[13,1,256]{2,1,0:T(2,128)(2,1)S(1)}, u32[]{:S(2)}, u32[]{:S(2)}) %collective-permute-start.7) | collective-permute-done | bytes 6688 | tf_op jit(solution)/shard_map/ppermute | solution.py:28
  514.4 0.7 broadcast_multiply_fusion.1
  515.1 5.5 %multiply_convert_fusion = bf16[2048,1024]{0,1:T(8,128)(2,1)} fusion(bf16[2048,1024]{0,1:T(8,128)(2,1)} %bitcast.42, bf16[13,1024]{1,0:T(8,128)(2,1)S(1)} %bitcast.48, f32[1024]{0:T(1024)S(1)} %bitcast.50, f32[13,2048]{1,0:T(8,128)S(1)} %stack.2, f32[2048]{0:T(1024)S(1)} %exponential_multiply_fusion), kind=kOutput, calls=%fused_computation.23 | convolution fusion | flops 62967808 | bytes 8534016 | tf_op jit(solution)/shard_map/dot_general | solution.py:149
  520.6 7.4 %copy.33 = bf16[2048,4,256]{2,1,0:T(4,128)(2,1)} copy(bf16[2048,4,256]{0,2,1:T(8,128)(2,1)} %bitcast.46) | data formatting | bytes 8388608
  (47 shorter events, 1.5 us)
Async XLA Ops:
  7.0 2.0 copy-start
  10.5 60.4 %collective-permute-start = (bf16[2048,1,256]{2,0,1:T(8,128)(2,1)}, bf16[2048,1,256]{2,0,1:T(8,128)(2,1)}, u32[]{:S(2)}, u32[]{:S(2)}) collective-permute-start(bf16[2048,1,256]{2,0,1:T(8,128)(2,1)} %get-tuple-element.24), channel_id=1, source_target_pairs={{0,2},{2,4},{4,6},{6,8},{8,10},{10,12},{12,14},{14,16},{16,18},{18... | collective-permute-start | bytes 3145736 | tf_op jit(solution)/shard_map/ppermute | solution.py:26
  15.1 59.4 %collective-permute-start.1 = (bf16[2048,1,256]{2,0,1:T(8,128)(2,1)}, bf16[2048,1,256]{2,0,1:T(8,128)(2,1)}, u32[]{:S(2)}, u32[]{:S(2)}) collective-permute-start(bf16[2048,1,256]{2,0,1:T(8,128)(2,1)} %get-tuple-element.25), channel_id=1, source_target_pairs={{2,0},{4,2},{6,4},{8,6},{10,8},{12,10},{14,12},{16,14},{18,16},{20... | collective-permute-start | bytes 3145736 | tf_op jit(solution)/shard_map/ppermute | solution.py:28
  60.8 8.7 %copy-start.4 = (s32[4,256]{1,0:T(4,128)S(1)}, s32[4,256]{1,0:T(4,128)}, u32[]{:S(2)}) copy-start(s32[4,256]{1,0:T(4,128)} %param.6) | copy-start | bytes 12292
  60.8 10.0 %copy-start.3 = (f32[4,256]{1,0:T(4,128)S(1)}, f32[4,256]{1,0:T(4,128)}, u32[]{:S(2)}) copy-start(f32[4,256]{1,0:T(4,128)} %param.5) | copy-start | bytes 12292
  60.8 10.0 %copy-start.5 = (s32[4,256]{1,0:T(4,128)S(1)}, s32[4,256]{1,0:T(4,128)}, u32[]{:S(2)}) copy-start(s32[4,256]{1,0:T(4,128)} %param.7) | copy-start | bytes 12292
  70.1 7.6 %copy-start.2 = (bf16[2048,4,256]{2,1,0:T(4,128)(2,1)S(1)}, bf16[2048,4,256]{2,1,0:T(4,128)(2,1)}, u32[]{:S(2)}) copy-start(bf16[2048,4,256]{2,1,0:T(4,128)(2,1)} %param.4) | copy-start | bytes 12582916
  85.9 8.9 %copy-start.1 = (bf16[2048,4,256]{2,0,1:T(8,128)(2,1)S(1)}, bf16[2048,4,256]{2,0,1:T(8,128)(2,1)}, u32[]{:S(2)}) copy-start(bf16[2048,4,256]{2,0,1:T(8,128)(2,1)} %copy-done) | copy-start | bytes 12582916
  125.3 357.3 %collective-permute-start.2 = (bf16[13,1,256]{2,1,0:T(2,128)(2,1)S(1)}, bf16[13,1,256]{2,1,0:T(2,128)(2,1)S(1)}, u32[]{:S(2)}, u32[]{:S(2)}) collective-permute-start(bf16[13,1,256]{2,1,0:T(2,128)(2,1)S(1)} %get-tuple-element.34), channel_id=1, source_target_pairs={{0,2},{2,4},{4,6},{6,8},{8,10},{10,12},{12,14},{14,16},{16,18},{18... | collective-permute-start | bytes 19976 | tf_op jit(solution)/shard_map/ppermute | solution.py:26
  134.7 348.0 %collective-permute-start.3 = (bf16[13,1,256]{2,1,0:T(2,128)(2,1)S(1)}, bf16[13,1,256]{2,1,0:T(2,128)(2,1)S(1)}, u32[]{:S(2)}, u32[]{:S(2)}) collective-permute-start(bf16[13,1,256]{2,1,0:T(2,128)(2,1)S(1)} %get-tuple-element.35), channel_id=1, source_target_pairs={{2,0},{4,2},{6,4},{8,6},{10,8},{12,10},{14,12},{16,14},{18,16},{20... | collective-permute-start | bytes 19976 | tf_op jit(solution)/shard_map/ppermute | solution.py:28
  482.8 10.0 %collective-permute-start.4 = (bf16[13,1,256]{2,1,0:T(2,128)(2,1)S(1)}, bf16[13,1,256]{2,1,0:T(2,128)(2,1)S(1)}, u32[]{:S(2)}, u32[]{:S(2)}) collective-permute-start(bf16[13,1,256]{2,1,0:T(2,128)(2,1)S(1)} %get-tuple-element.32), channel_id=1, source_target_pairs={{0,2},{2,4},{4,6},{6,8},{8,10},{10,12},{12,14},{14,16},{16,18},{18... | collective-permute-start | bytes 19976 | tf_op jit(solution)/shard_map/ppermute | solution.py:26
  490.2 11.0 %collective-permute-start.5 = (bf16[13,1,256]{2,1,0:T(2,128)(2,1)S(1)}, bf16[13,1,256]{2,1,0:T(2,128)(2,1)S(1)}, u32[]{:S(2)}, u32[]{:S(2)}) collective-permute-start(bf16[13,1,256]{2,1,0:T(2,128)(2,1)S(1)} %get-tuple-element.33), channel_id=1, source_target_pairs={{2,0},{4,2},{6,4},{8,6},{10,8},{12,10},{14,12},{16,14},{18,16},{20... | collective-permute-start | bytes 19976 | tf_op jit(solution)/shard_map/ppermute | solution.py:28
  501.3 6.6 %collective-permute-start.6 = (bf16[13,1,256]{2,1,0:T(2,128)(2,1)S(1)}, bf16[13,1,256]{2,1,0:T(2,128)(2,1)S(1)}, u32[]{:S(2)}, u32[]{:S(2)}) collective-permute-start(bf16[13,1,256]{2,1,0:T(2,128)(2,1)S(1)} %get-tuple-element.30), channel_id=1, source_target_pairs={{0,2},{2,4},{4,6},{6,8},{8,10},{10,12},{12,14},{14,16},{16,18},{18... | collective-permute-start | bytes 19976 | tf_op jit(solution)/shard_map/ppermute | solution.py:26
  503.3 11.0 %collective-permute-start.7 = (bf16[13,1,256]{2,1,0:T(2,128)(2,1)S(1)}, bf16[13,1,256]{2,1,0:T(2,128)(2,1)S(1)}, u32[]{:S(2)}, u32[]{:S(2)}) collective-permute-start(bf16[13,1,256]{2,1,0:T(2,128)(2,1)S(1)} %get-tuple-element.31), channel_id=1, source_target_pairs={{2,0},{4,2},{6,4},{8,6},{10,8},{12,10},{14,12},{16,14},{18,16},{20... | collective-permute-start | bytes 19976 | tf_op jit(solution)/shard_map/ppermute | solution.py:28
where the time goes:
time: 529 us; the launch traced here: 528 us
  blocking collectives  349 us (66%)
  local copies, waits for them, and re-layouts  61.6 us (12%)
  other arithmetic  58.9 us (11%)
  starting transfers between devices  32.9 us (6%)
  waiting for transfers between devices  14.8 us (3%)
  matrix products  9.53 us (2%)
    psum x1, blocking collectives, on_device(): squares = lax.psum(jnp.sum(moments[0] * moments[0]), 'space')  345 us
    ppermute x4, starting transfers between devices, with_halo(): lax.ppermute(tail, axis, [(i, (i + 1) % count) for i in range(ends)])  23.3 us
    add x1, other arithmetic, on_device(): jnp.maximum(shaped_y, 0.0) * (padded[:, :, 2:, 1:-1] - cube)  20.4 us
    ppermute x4, waiting for transfers between devices, with_halo(): lax.ppermute(head, axis, [((i + 1) % count, i) for i in range(ends)])  14.8 us
  transfers between devices with their start and end apart: 8, of which 2 were waited for; matrix products, arithmetic and copies ran while one was open for 11% of the time, Pallas kernels for 0%

commit v1 on v0

--- a/solution.py
+++ b/solution.py
@@ -138,7 +138,9 @@
     partial_value = jnp.dot(weigh, starred_flat, preferred_element_type=jnp.float32)
     moments = lax.psum(partial_value, "vel").reshape(NM, width, plane)
     cells_all = width * lax.axis_size("space") * plane
-    squares = lax.psum(jnp.sum(moments[0] * moments[0]), "space")
+    own = jnp.sum(moments[0] * moments[0])
+    own = jnp.where(lax.axis_index("vel") == 0, own, 0.0)
+    squares = lax.psum(own, ("space", "vel"))
     scale = lax.rsqrt(squares / cells_all + 1e-06)
     inverse = fluid / (collision + wall_level(codes) + 6.0)
     source = collision[None] * moments

time: 529 us -> 260 us (0.49)
  blocking collectives: 349 us -> 79.1 us
    psum x1, blocking collectives: 345 us -> 75.3 us  [on_device(): squares = lax.psum(own, ('space', 'vel'))]
  transfers between devices with their start and end apart: 8 -> 8, of which waited for: 2 -> 2; matrix products, arithmetic and copies ran while one was open for 11% -> 23% of each run, Pallas kernels for 0% -> 0%
where the time goes in v1:
time: 260 us; the launch traced here: 258 us
  blocking collectives  79.1 us (30%)
  local copies, waits for them, and re-layouts  61.6 us (24%)
  other arithmetic  58.9 us (23%)
  starting transfers between devices  32 us (12%)
  waiting for transfers between devices  14.8 us (6%)
  matrix products  9.53 us (4%)
    psum x1, blocking collectives, on_device(): squares = lax.psum(own, ('space', 'vel'))  75.3 us
    ppermute x4, starting transfers between devices, with_halo(): lax.ppermute(tail, axis, [(i, (i + 1) % count) for i in range(ends)])  22.3 us
    add x1, other arithmetic, on_device(): jnp.maximum(shaped_y, 0.0) * (padded[:, :, 2:, 1:-1] - cube)  20.4 us
    ppermute x4, waiting for transfers between devices, with_halo(): lax.ppermute(head, axis, [((i + 1) % count, i) for i in range(ends)])  14.8 us
    ppermute x4, starting transfers between devices, with_halo(): lax.ppermute(head, axis, [((i + 1) % count, i) for i in range(ends)])  9.68 us
    unnamed x16, local copies, waits for them, and re-layouts  9.49 us
    convert_element_type x1, other arithmetic, on_device(): (fluid[None] * (flat + TIME_STEP * (advect - collision[None] * flat))).as...  8.8 us
    convert_element_type x1, local copies, waits for them, and re-layouts, on_device(): flat = adjoint.astype(jnp.float32)  8.79 us
  transfers between devices with their start and end apart: 8, of which 2 were waited for; matrix products, arithmetic and copies ran while one was open for 23% of the time, Pallas kernels for 0%

profile of v1, /device:TPU:126, one launch (start us, length us, event | category | flops | bytes accessed | tf_op | source)
XLA Modules:
  0.0 258.2 jit_solution(12036914608503378547)
XLA Ops:
  0.6 6.4 %fusion.109 = (bf16[2048,4,256]{2,0,1:T(8,128)(2,1)S(1)}, f32[2048,4,256]{2,0,1:T(8,128)}) fusion(bf16[2048,4,256]{2,1,0:T(4,128)(2,1)} %param.4), kind=kLoop, calls=%fused_computation.205 | loop fusion | flops 2097152 | bytes 16777216 | tf_op args[0]
  7.0 2.0 copy-done
  9.0 1.5 fusion.108
  10.5 4.6 %collective-permute-start = (bf16[2048,1,256]{2,0,1:T(8,128)(2,1)}, bf16[2048,1,256]{2,0,1:T(8,128)(2,1)}, u32[]{:S(2)}, u32[]{:S(2)}) collective-permute-start(bf16[2048,1,256]{2,0,1:T(8,128)(2,1)} %get-tuple-element.24), channel_id=1, source_target_pairs={{0,2},{2,4},{4,6},{6,8},{8,10},{10,12},{12,14},{14,16},{16,18},{18... | collective-permute-start | bytes 3145736 | tf_op jit(solution)/shard_map/ppermute | solution.py:26
  15.1 1.9 collective-permute-start.1
  17.3 0.2 multiply_multiply_fusion.1
  17.8 3.0 %slice_convert_fusion.1 = (f32[128,8,4,256]{3,1,0,2:T(8,128)S(1)}, f32[128,8,4,256]{3,1,0,2:T(8,128)S(1)}) fusion(bf16[128,16,4,256]{3,1,0,2:T(8,128)(2,1)} %bitcast.39), kind=kLoop, calls=%fused_computation.29 | loop fusion | flops 2097152 | bytes 12582912 | tf_op jit(solution)/shard_map/convert_element_type | solution.py:110
  20.8 0.2 slice.163
  21.0 1.9 slice.166
  22.9 8.8 %copy.29 = f32[2048,4,256]{0,2,1:T(8,128)} copy(f32[2048,4,256]{2,0,1:T(8,128)} %get-tuple-element.27) | data formatting | bytes 16777216 | tf_op jit(solution)/shard_map/convert_element_type | solution.py:119
  31.7 20.4 %fusion.2 = (f32[2048,4,16,16]{0,3,2,1:T(8,128)}, f32[2048,4,16,16]{0,3,2,1:T(8,128)}) fusion(f32[2048,4,16,16]{0,3,2,1:T(8,128)} %bitcast.43, f32[2048]{0:T(1024)S(1)} %get-tuple-element.51, f32[2048]{0:T(1024)S(1)} %broadcast_maximum_fusion.1, f32[2048]{0:T(1024)S(1)} %get-tuple-element.41, f32[2048]{0:T(1024)S(1)} %get-tuple-element.50), kind=kLoop, calls=%fused_computation.6 | loop fusion | flops 20971520 | bytes 25198592 | tf_op jit(solution)/shard_map/add | solution.py:124
  52.0 8.7 %copy.30 = f32[2048,4,256]{2,0,1:T(8,128)} copy(f32[2048,4,256]{0,2,1:T(8,128)} %bitcast.45) | data formatting | bytes 16777216 | tf_op jit(solution)/shard_map/reshape | solution.py:131
  60.8 8.7 %copy.31 = f32[2048,4,256]{2,0,1:T(8,128)} copy(f32[2048,4,256]{0,2,1:T(8,128)} %bitcast.44) | data formatting | bytes 16777216 | tf_op jit(solution)/shard_map/reshape | solution.py:131
  69.9 0.2 stack.2
  70.1 0.6 fusion.70
  70.9 3.6 %copy.26 = bf16[2048,1,256]{2,1,0:T(2,128)(2,1)S(1)} copy(bf16[2048,1,256]{2,0,1:T(8,128)(2,1)} %collective-permute-done) | data formatting | bytes 2097152 | tf_op jit(solution)/shard_map/ppermute | solution.py:26
  74.5 3.2 %copy.27 = bf16[2048,1,256]{2,1,0:T(2,128)(2,1)S(1)} copy(bf16[2048,1,256]{2,0,1:T(8,128)(2,1)} %collective-permute-done.1) | data formatting | bytes 2097152 | tf_op jit(solution)/shard_map/ppermute | solution.py:28
  77.7 8.2 %pad_maximum_fusion = bf16[2048,6,256]{2,1,0:T(8,128)(2,1)} fusion(bf16[2048,1,256]{2,1,0:T(2,128)(2,1)S(1)} %copy.27, bf16[2048,4,256]{2,1,0:T(4,128)(2,1)S(1)} %copy-done.2, bf16[2048,1,256]{2,1,0:T(2,128)(2,1)S(1)} %copy.26), kind=kLoop, calls=%fused_computation.14 | loop fusion | flops 18874368 | bytes 12582912 | tf_op jit(solution)/shard_map/concatenate | solution.py:24
  85.9 7.6 %copy.28 = bf16[2048,6,256]{2,0,1:T(8,128)(2,1)} copy(bf16[2048,6,256]{2,1,0:T(8,128)(2,1)} %pad_maximum_fusion) | data formatting | bytes 12582912 | tf_op jit(solution)/shard_map/concatenate | solution.py:24
  93.4 1.4 slice_convert_fusion.3
  94.8 3.9 %fusion.16 = (f32[128,8,4,256]{3,1,0,2:T(8,128)S(1)}, f32[128,8,4,256]{3,1,0,2:T(8,128)}) fusion(f32[128,8,3,256]{3,1,0,2:T(8,128)S(1)} %slice.163, f32[128,8,1,256]{3,1,0,2:T(8,128)S(1)} %get-tuple-element.18, f32[128,8]{1,0:T(8,128)S(1)} %get-tuple-element.28, bf16[128,16,4,256]{3,1,0,2:T(8,128)(2,1)S(1)} %bitcast.40, ...), kind=kLoop, calls=%fused_computation.25 | loop fusion | flops 8388608 | bytes 20979712 | tf_op jit(solution)/shard_map/mul | solution.py:116
  98.7 2.8 %pad_maximum_fusion.1 = f32[128,16,4,256]{3,1,0,2:T(8,128)S(1)} fusion(f32[128,8,4,256]{3,1,0,2:T(8,128)} %get-tuple-element.21, f32[128,8,4,256]{3,1,0,2:T(8,128)S(1)} %get-tuple-element.20), kind=kLoop, calls=%fused_computation.15 | loop fusion | flops 2097152 | bytes 16777216 | tf_op jit(solution)/shard_map/concatenate | solution.py:115
  101.5 8.8 %fusion.15 = bf16[2048,4,256]{2,0,1:T(8,128)(2,1)} fusion(f32[2048,4,256]{2,0,1:T(8,128)} %copy.31, f32[2048,4,256]{2,0,1:T(8,128)} %copy.30, f32[128,16,4,256]{3,1,0,2:T(8,128)S(1)} %pad_maximum_fusion.1, f32[4,256]{1,0:T(4,128)S(1)} %copy-done.3, f32[4,256]{1,0:T(4,128)S(1)} %get-tuple-element.37, bf16[2048,4,256]{2,1,0:T(4,128)(2,1)S(1)} %copy-done.2), kind=kLoop, calls=%fused_computation.22 | loop fusion | flops 18874368 | bytes 33562624 | tf_op jit(solution)/shard_map/convert_element_type | solution.py:134
  110.3 6.3 %copy.32 = bf16[2048,4,256]{0,2,1:T(8,128)(2,1)} copy(bf16[2048,4,256]{2,0,1:T(8,128)(2,1)} %fusion.15) | data formatting | bytes 8388608 | tf_op jit(solution)/shard_map/convert_element_type | solution.py:134
  116.6 4.0 %fusion.31 = f32[13,1024]{1,0:T(8,128)S(1)} fusion(bf16[2048,1024]{0,1:T(8,128)(2,1)} %bitcast.41, f32[13,2048]{1,0:T(8,128)S(1)} %stack.2, f32[]{:T(128)} %fusion.70, f32[2048]{0:T(1024)S(1)} %get-tuple-element.40), kind=kOutput, calls=%fused_computation.63 | convolution fusion | flops 54605824 | bytes 4362244 | tf_op jit(solution)/shard_map/dot_general | solution.py:138
  120.6 3.8 %psum.14 = f32[13,1024]{1,0:T(8,128)S(1)} all-reduce(f32[13,1024]{1,0:T(8,128)S(1)} %fusion.31), channel_id=1, replica_groups=mesh['space'=128,'vel'=2] {'vel'}, use_global_device_ids=true, to_apply=%region_1.2 | all-reduce | flops 13312 | bytes 106496 | tf_op jit(solution)/shard_map/psum | solution.py:139
  124.5 0.2 reshape.437
  124.7 0.6 fusion.98
  125.3 9.4 %collective-permute-start.2 = (bf16[13,1,256]{2,1,0:T(2,128)(2,1)S(1)}, bf16[13,1,256]{2,1,0:T(2,128)(2,1)S(1)}, u32[]{:S(2)}, u32[]{:S(2)}) collective-permute-start(bf16[13,1,256]{2,1,0:T(2,128)(2,1)S(1)} %get-tuple-element.34), channel_id=1, source_target_pairs={{0,2},{2,4},{4,6},{6,8},{8,10},{10,12},{12,14},{14,16},{16,18},{18... | collective-permute-start | bytes 19976 | tf_op jit(solution)/shard_map/ppermute | solution.py:26
  134.7 1.9 collective-permute-start.3
  137.3 0.3 fusion.20
  137.6 75.3 %psum.15 = f32[]{:T(128)} all-reduce(f32[]{:T(128)S(6)} %select_n.264), channel_id=1, replica_groups=mesh['space'=128,'vel'=2] {'space','vel'}, use_global_device_ids=true, to_apply=%region_3.4 | all-reduce | flops 1 | bytes 8 | tf_op jit(solution)/shard_map/psum | solution.py:143
  212.9 0.2 reshape.438
  214.0 6.4 %collective-permute-start.4 = (bf16[13,1,256]{2,1,0:T(2,128)(2,1)S(1)}, bf16[13,1,256]{2,1,0:T(2,128)(2,1)S(1)}, u32[]{:S(2)}, u32[]{:S(2)}) collective-permute-start(bf16[13,1,256]{2,1,0:T(2,128)(2,1)S(1)} %get-tuple-element.32), channel_id=1, source_target_pairs={{0,2},{2,4},{4,6},{6,8},{8,10},{10,12},{12,14},{14,16},{16,18},{18... | collective-permute-start | bytes 19976 | tf_op jit(solution)/shard_map/ppermute | solution.py:26
  220.4 1.9 collective-permute-start.5
  222.3 0.2 reshape.439
  222.5 0.3 fusion.23
  222.8 0.2 reshape.440
  223.0 8.4 %collective-permute-done.5 = bf16[13,1,256]{2,1,0:T(2,128)(2,1)S(1)} collective-permute-done((bf16[13,1,256]{2,1,0:T(2,128)(2,1)S(1)}, bf16[13,1,256]{2,1,0:T(2,128)(2,1)S(1)}, u32[]{:S(2)}, u32[]{:S(2)}) %collective-permute-start.5) | collective-permute-done | bytes 6688 | tf_op jit(solution)/shard_map/ppermute | solution.py:28
  231.6 1.9 collective-permute-start.6
  233.5 3.9 %collective-permute-start.7 = (bf16[13,1,256]{2,1,0:T(2,128)(2,1)S(1)}, bf16[13,1,256]{2,1,0:T(2,128)(2,1)S(1)}, u32[]{:S(2)}, u32[]{:S(2)}) collective-permute-start(bf16[13,1,256]{2,1,0:T(2,128)(2,1)S(1)} %get-tuple-element.31), channel_id=1, source_target_pairs={{2,0},{4,2},{6,4},{8,6},{10,8},{12,10},{14,12},{16,14},{18,16},{20... | collective-permute-start | bytes 19976 | tf_op jit(solution)/shard_map/ppermute | solution.py:28
  237.4 0.2 reshape.441
  237.6 0.3 fusion.26
  237.9 0.2 reshape.442
  238.1 6.4 %collective-permute-done.7 = bf16[13,1,256]{2,1,0:T(2,128)(2,1)S(1)} collective-permute-done((bf16[13,1,256]{2,1,0:T(2,128)(2,1)S(1)}, bf16[13,1,256]{2,1,0:T(2,128)(2,1)S(1)}, u32[]{:S(2)}, u32[]{:S(2)}) %collective-permute-start.7) | collective-permute-done | bytes 6688 | tf_op jit(solution)/shard_map/ppermute | solution.py:28
  244.6 0.7 broadcast_multiply_fusion.1
  245.3 5.5 %multiply_convert_fusion = bf16[2048,1024]{0,1:T(8,128)(2,1)} fusion(bf16[2048,1024]{0,1:T(8,128)(2,1)} %bitcast.42, bf16[13,1024]{1,0:T(8,128)(2,1)S(1)} %bitcast.48, f32[1024]{0:T(1024)S(1)} %bitcast.50, f32[13,2048]{1,0:T(8,128)S(1)} %stack.2, f32[2048]{0:T(1024)S(1)} %exponential_multiply_fusion), kind=kOutput, calls=%fused_computation.23 | convolution fusion | flops 62967808 | bytes 8534016 | tf_op jit(solution)/shard_map/dot_general | solution.py:151
  250.8 7.4 %copy.33 = bf16[2048,4,256]{2,1,0:T(4,128)(2,1)} copy(bf16[2048,4,256]{0,2,1:T(8,128)(2,1)} %bitcast.46) | data formatting | bytes 8388608
  (47 shorter events, 1.5 us)
Async XLA Ops:
  7.0 2.0 copy-start
  10.5 60.4 %collective-permute-start = (bf16[2048,1,256]{2,0,1:T(8,128)(2,1)}, bf16[2048,1,256]{2,0,1:T(8,128)(2,1)}, u32[]{:S(2)}, u32[]{:S(2)}) collective-permute-start(bf16[2048,1,256]{2,0,1:T(8,128)(2,1)} %get-tuple-element.24), channel_id=1, source_target_pairs={{0,2},{2,4},{4,6},{6,8},{8,10},{10,12},{12,14},{14,16},{16,18},{18... | collective-permute-start | bytes 3145736 | tf_op jit(solution)/shard_map/ppermute | solution.py:26
  15.1 59.4 %collective-permute-start.1 = (bf16[2048,1,256]{2,0,1:T(8,128)(2,1)}, bf16[2048,1,256]{2,0,1:T(8,128)(2,1)}, u32[]{:S(2)}, u32[]{:S(2)}) collective-permute-start(bf16[2048,1,256]{2,0,1:T(8,128)(2,1)} %get-tuple-element.25), channel_id=1, source_target_pairs={{2,0},{4,2},{6,4},{8,6},{10,8},{12,10},{14,12},{16,14},{18,16},{20... | collective-permute-start | bytes 3145736 | tf_op jit(solution)/shard_map/ppermute | solution.py:28
  60.8 8.7 %copy-start.4 = (s32[4,256]{1,0:T(4,128)S(1)}, s32[4,256]{1,0:T(4,128)}, u32[]{:S(2)}) copy-start(s32[4,256]{1,0:T(4,128)} %param.6) | copy-start | bytes 12292
  60.8 10.0 %copy-start.3 = (f32[4,256]{1,0:T(4,128)S(1)}, f32[4,256]{1,0:T(4,128)}, u32[]{:S(2)}) copy-start(f32[4,256]{1,0:T(4,128)} %param.5) | copy-start | bytes 12292
  60.8 10.0 %copy-start.5 = (s32[4,256]{1,0:T(4,128)S(1)}, s32[4,256]{1,0:T(4,128)}, u32[]{:S(2)}) copy-start(s32[4,256]{1,0:T(4,128)} %param.7) | copy-start | bytes 12292
  70.1 7.6 %copy-start.2 = (bf16[2048,4,256]{2,1,0:T(4,128)(2,1)S(1)}, bf16[2048,4,256]{2,1,0:T(4,128)(2,1)}, u32[]{:S(2)}) copy-start(bf16[2048,4,256]{2,1,0:T(4,128)(2,1)} %param.4) | copy-start | bytes 12582916
  85.9 8.9 %copy-start.1 = (bf16[2048,4,256]{2,0,1:T(8,128)(2,1)S(1)}, bf16[2048,4,256]{2,0,1:T(8,128)(2,1)}, u32[]{:S(2)}) copy-start(bf16[2048,4,256]{2,0,1:T(8,128)(2,1)} %copy-done) | copy-start | bytes 12582916
  125.3 88.5 %collective-permute-start.2 = (bf16[13,1,256]{2,1,0:T(2,128)(2,1)S(1)}, bf16[13,1,256]{2,1,0:T(2,128)(2,1)S(1)}, u32[]{:S(2)}, u32[]{:S(2)}) collective-permute-start(bf16[13,1,256]{2,1,0:T(2,128)(2,1)S(1)} %get-tuple-element.34), channel_id=1, source_target_pairs={{0,2},{2,4},{4,6},{6,8},{8,10},{10,12},{12,14},{14,16},{16,18},{18... | collective-permute-start | bytes 19976 | tf_op jit(solution)/shard_map/ppermute | solution.py:26
  134.7 79.2 %collective-permute-start.3 = (bf16[13,1,256]{2,1,0:T(2,128)(2,1)S(1)}, bf16[13,1,256]{2,1,0:T(2,128)(2,1)S(1)}, u32[]{:S(2)}, u32[]{:S(2)}) collective-permute-start(bf16[13,1,256]{2,1,0:T(2,128)(2,1)S(1)} %get-tuple-element.35), channel_id=1, source_target_pairs={{2,0},{4,2},{6,4},{8,6},{10,8},{12,10},{14,12},{16,14},{18,16},{20... | collective-permute-start | bytes 19976 | tf_op jit(solution)/shard_map/ppermute | solution.py:28
  214.0 9.1 %collective-permute-start.4 = (bf16[13,1,256]{2,1,0:T(2,128)(2,1)S(1)}, bf16[13,1,256]{2,1,0:T(2,128)(2,1)S(1)}, u32[]{:S(2)}, u32[]{:S(2)}) collective-permute-start(bf16[13,1,256]{2,1,0:T(2,128)(2,1)S(1)} %get-tuple-element.32), channel_id=1, source_target_pairs={{0,2},{2,4},{4,6},{6,8},{8,10},{10,12},{12,14},{14,16},{16,18},{18... | collective-permute-start | bytes 19976 | tf_op jit(solution)/shard_map/ppermute | solution.py:26
  220.4 11.0 %collective-permute-start.5 = (bf16[13,1,256]{2,1,0:T(2,128)(2,1)S(1)}, bf16[13,1,256]{2,1,0:T(2,128)(2,1)S(1)}, u32[]{:S(2)}, u32[]{:S(2)}) collective-permute-start(bf16[13,1,256]{2,1,0:T(2,128)(2,1)S(1)} %get-tuple-element.33), channel_id=1, source_target_pairs={{2,0},{4,2},{6,4},{8,6},{10,8},{12,10},{14,12},{16,14},{18,16},{20... | collective-permute-start | bytes 19976 | tf_op jit(solution)/shard_map/ppermute | solution.py:28
  231.6 6.6 %collective-permute-start.6 = (bf16[13,1,256]{2,1,0:T(2,128)(2,1)S(1)}, bf16[13,1,256]{2,1,0:T(2,128)(2,1)S(1)}, u32[]{:S(2)}, u32[]{:S(2)}) collective-permute-start(bf16[13,1,256]{2,1,0:T(2,128)(2,1)S(1)} %get-tuple-element.30), channel_id=1, source_target_pairs={{0,2},{2,4},{4,6},{6,8},{8,10},{10,12},{12,14},{14,16},{16,18},{18... | collective-permute-start | bytes 19976 | tf_op jit(solution)/shard_map/ppermute | solution.py:26
  233.5 11.0 %collective-permute-start.7 = (bf16[13,1,256]{2,1,0:T(2,128)(2,1)S(1)}, bf16[13,1,256]{2,1,0:T(2,128)(2,1)S(1)}, u32[]{:S(2)}, u32[]{:S(2)}) collective-permute-start(bf16[13,1,256]{2,1,0:T(2,128)(2,1)S(1)} %get-tuple-element.31), channel_id=1, source_target_pairs={{2,0},{4,2},{6,4},{8,6},{10,8},{12,10},{14,12},{16,14},{18,16},{20... | collective-permute-start | bytes 19976 | tf_op jit(solution)/shard_map/ppermute | solution.py:28

commit v2 on v0

--- a/solution.py
+++ b/solution.py
@@ -30,6 +30,17 @@
             axis=dim,
         )
     return cells
+
+
+def exchange_sum(value, axis):
+    count = lax.axis_size(axis)
+    if count & (count - 1):
+        return lax.psum(value, axis)
+    step = 1
+    while step < count:
+        value = value + lax.ppermute(value, axis, [(i, i ^ step) for i in range(count)])
+        step *= 2
+    return value
 
 
 def velocity_axes(start, count):
@@ -138,7 +149,7 @@
     partial_value = jnp.dot(weigh, starred_flat, preferred_element_type=jnp.float32)
     moments = lax.psum(partial_value, "vel").reshape(NM, width, plane)
     cells_all = width * lax.axis_size("space") * plane
-    squares = lax.psum(jnp.sum(moments[0] * moments[0]), "space")
+    squares = exchange_sum(jnp.sum(moments[0] * moments[0]), "space")
     scale = lax.rsqrt(squares / cells_all + 1e-06)
     inverse = fluid / (collision + wall_level(codes) + 6.0)
     source = collision[None] * moments

time: 529 us -> 224 us (0.42)
  blocking collectives: 349 us -> 3.81 us
  waiting for transfers between devices: 14.8 us -> 40.5 us
  starting transfers between devices: 32.9 us -> 43.5 us
    psum x1 -> x0, blocking collectives: 345 us -> none  [on_device(): squares = lax.psum(jnp.sum(moments[0] * moments[0]), 'space')]
    ppermute x0 -> x7, waiting for transfers between devices: none -> 25.7 us  [exchange_sum(): lax.ppermute(value, axis, [(i, i ^ step) for i in range(count)])]
    ppermute x0 -> x7, starting transfers between devices: none -> 8.58 us  [exchange_sum(): lax.ppermute(value, axis, [(i, i ^ step) for i in range(count)])]
  transfers between devices with their start and end apart: 8 -> 15, of which waited for: 2 -> 9; matrix products, arithmetic and copies ran while one was open for 11% -> 27% of each run, Pallas kernels for 0% -> 0%
where the time goes in v2:
time: 224 us; the launch traced here: 223 us
  local copies, waits for them, and re-layouts  61.4 us (27%)
  other arithmetic  58.7 us (26%)
  starting transfers between devices  43.5 us (19%)
  waiting for transfers between devices  40.5 us (18%)
  matrix products  9.54 us (4%)
  between operations  5.7 us (3%)
  blocking collectives  3.81 us (2%)
    ppermute x7, waiting for transfers between devices, exchange_sum(): lax.ppermute(value, axis, [(i, i ^ step) for i in range(count)])  25.7 us
    ppermute x4, starting transfers between devices, with_halo(): lax.ppermute(tail, axis, [(i, (i + 1) % count) for i in range(ends)])  25.2 us
    add x1, other arithmetic, on_device(): jnp.maximum(shaped_y, 0.0) * (padded[:, :, 2:, 1:-1] - cube)  20.2 us
    ppermute x4, waiting for transfers between devices, with_halo(): lax.ppermute(head, axis, [((i + 1) % count, i) for i in range(ends)])  14.8 us
    ppermute x4, starting transfers between devices, with_halo(): lax.ppermute(head, axis, [((i + 1) % count, i) for i in range(ends)])  9.68 us
    unnamed x16, local copies, waits for them, and re-layouts  9.49 us
    convert_element_type x1, other arithmetic, on_device(): (fluid[None] * (flat + TIME_STEP * (advect - collision[None] * flat))).as...  8.8 us
    reshape x1, local copies, waits for them, and re-layouts, on_device(): term_y.reshape(local_vel, width, plane)  8.76 us
  transfers between devices with their start and end apart: 15, of which 9 were waited for; matrix products, arithmetic and copies ran while one was open for 27% of the time, Pallas kernels for 0%

profile of v2, /device:TPU:126, one launch (start us, length us, event | category | flops | bytes accessed | tf_op | source)
XLA Modules:
  0.0 223.1 jit_solution(1471590080614519934)
XLA Ops:
  0.6 6.4 %fusion.109 = (bf16[2048,4,256]{2,0,1:T(8,128)(2,1)S(1)}, f32[2048,4,256]{2,0,1:T(8,128)}) fusion(bf16[2048,4,256]{2,1,0:T(4,128)(2,1)} %param.4), kind=kLoop, calls=%fused_computation.205 | loop fusion | flops 2097152 | bytes 16777216 | tf_op args[0]
  7.1 2.0 copy-done
  9.1 1.4 fusion.108
  10.5 4.6 %collective-permute-start = (bf16[2048,1,256]{2,0,1:T(8,128)(2,1)}, bf16[2048,1,256]{2,0,1:T(8,128)(2,1)}, u32[]{:S(2)}, u32[]{:S(2)}) collective-permute-start(bf16[2048,1,256]{2,0,1:T(8,128)(2,1)} %get-tuple-element.24), channel_id=1, source_target_pairs={{0,2},{2,4},{4,6},{6,8},{8,10},{10,12},{12,14},{14,16},{16,18},{18... | collective-permute-start | bytes 3145736 | tf_op jit(solution)/shard_map/ppermute | solution.py:26
  15.1 1.9 collective-permute-start.1
  17.8 3.0 %slice_convert_fusion.1 = (f32[128,8,4,256]{3,1,0,2:T(8,128)S(1)}, f32[128,8,4,256]{3,1,0,2:T(8,128)S(1)}) fusion(bf16[128,16,4,256]{3,1,0,2:T(8,128)(2,1)} %bitcast.39), kind=kLoop, calls=%fused_computation.29 | loop fusion | flops 2097152 | bytes 12582912 | tf_op jit(solution)/shard_map/convert_element_type | solution.py:121
  21.0 1.9 slice.166
  22.8 8.7 %copy.29 = f32[2048,4,256]{0,2,1:T(8,128)} copy(f32[2048,4,256]{2,0,1:T(8,128)} %get-tuple-element.27) | data formatting | bytes 16777216 | tf_op jit(solution)/shard_map/convert_element_type | solution.py:130
  31.5 20.2 %fusion.2 = (f32[2048,4,16,16]{0,3,2,1:T(8,128)}, f32[2048,4,16,16]{0,3,2,1:T(8,128)}) fusion(f32[2048,4,16,16]{0,3,2,1:T(8,128)} %bitcast.43, f32[2048]{0:T(1024)S(1)} %get-tuple-element.51, f32[2048]{0:T(1024)S(1)} %broadcast_maximum_fusion.1, f32[2048]{0:T(1024)S(1)} %get-tuple-element.41, f32[2048]{0:T(1024)S(1)} %get-tuple-element.50), kind=kLoop, calls=%fused_computation.6 | loop fusion | flops 20971520 | bytes 25198592 | tf_op jit(solution)/shard_map/add | solution.py:135
  51.7 8.8 %copy.30 = f32[2048,4,256]{2,0,1:T(8,128)} copy(f32[2048,4,256]{0,2,1:T(8,128)} %bitcast.45) | data formatting | bytes 16777216 | tf_op jit(solution)/shard_map/reshape | solution.py:142
  60.5 8.7 %copy.31 = f32[2048,4,256]{2,0,1:T(8,128)} copy(f32[2048,4,256]{0,2,1:T(8,128)} %bitcast.44) | data formatting | bytes 16777216 | tf_op jit(solution)/shard_map/reshape | solution.py:142
  69.8 0.6 fusion.70
  70.6 3.6 %copy.26 = bf16[2048,1,256]{2,1,0:T(2,128)(2,1)S(1)} copy(bf16[2048,1,256]{2,0,1:T(8,128)(2,1)} %collective-permute-done) | data formatting | bytes 2097152 | tf_op jit(solution)/shard_map/ppermute | solution.py:26
  74.2 3.2 %copy.27 = bf16[2048,1,256]{2,1,0:T(2,128)(2,1)S(1)} copy(bf16[2048,1,256]{2,0,1:T(8,128)(2,1)} %collective-permute-done.1) | data formatting | bytes 2097152 | tf_op jit(solution)/shard_map/ppermute | solution.py:28
  77.4 8.2 %pad_maximum_fusion = bf16[2048,6,256]{2,1,0:T(8,128)(2,1)} fusion(bf16[2048,1,256]{2,1,0:T(2,128)(2,1)S(1)} %copy.27, bf16[2048,4,256]{2,1,0:T(4,128)(2,1)S(1)} %copy-done.2, bf16[2048,1,256]{2,1,0:T(2,128)(2,1)S(1)} %copy.26), kind=kLoop, calls=%fused_computation.14 | loop fusion | flops 18874368 | bytes 12582912 | tf_op jit(solution)/shard_map/concatenate | solution.py:24
  85.6 7.5 %copy.28 = bf16[2048,6,256]{2,0,1:T(8,128)(2,1)} copy(bf16[2048,6,256]{2,1,0:T(8,128)(2,1)} %pad_maximum_fusion) | data formatting | bytes 12582912 | tf_op jit(solution)/shard_map/concatenate | solution.py:24
  93.1 1.4 slice_convert_fusion.3
  94.5 3.9 %fusion.16 = (f32[128,8,4,256]{3,1,0,2:T(8,128)S(1)}, f32[128,8,4,256]{3,1,0,2:T(8,128)}) fusion(f32[128,8,3,256]{3,1,0,2:T(8,128)S(1)} %slice.163, f32[128,8,1,256]{3,1,0,2:T(8,128)S(1)} %get-tuple-element.18, f32[128,8]{1,0:T(8,128)S(1)} %get-tuple-element.28, bf16[128,16,4,256]{3,1,0,2:T(8,128)(2,1)S(1)} %bitcast.40, ...), kind=kLoop, calls=%fused_computation.25 | loop fusion | flops 8388608 | bytes 20979712 | tf_op jit(solution)/shard_map/mul | solution.py:127
  98.4 2.8 %pad_maximum_fusion.1 = f32[128,16,4,256]{3,1,0,2:T(8,128)S(1)} fusion(f32[128,8,4,256]{3,1,0,2:T(8,128)} %get-tuple-element.21, f32[128,8,4,256]{3,1,0,2:T(8,128)S(1)} %get-tuple-element.20), kind=kLoop, calls=%fused_computation.15 | loop fusion | flops 2097152 | bytes 16777216 | tf_op jit(solution)/shard_map/concatenate | solution.py:126
  101.2 8.8 %fusion.15 = bf16[2048,4,256]{2,0,1:T(8,128)(2,1)} fusion(f32[2048,4,256]{2,0,1:T(8,128)} %copy.31, f32[2048,4,256]{2,0,1:T(8,128)} %copy.30, f32[128,16,4,256]{3,1,0,2:T(8,128)S(1)} %pad_maximum_fusion.1, f32[4,256]{1,0:T(4,128)S(1)} %copy-done.3, f32[4,256]{1,0:T(4,128)S(1)} %get-tuple-element.37, bf16[2048,4,256]{2,1,0:T(4,128)(2,1)S(1)} %copy-done.2), kind=kLoop, calls=%fused_computation.22 | loop fusion | flops 18874368 | bytes 33562624 | tf_op jit(solution)/shard_map/convert_element_type | solution.py:145
  110.0 6.3 %copy.32 = bf16[2048,4,256]{0,2,1:T(8,128)(2,1)} copy(bf16[2048,4,256]{2,0,1:T(8,128)(2,1)} %fusion.15) | data formatting | bytes 8388608 | tf_op jit(solution)/shard_map/convert_element_type | solution.py:145
  116.3 4.0 %fusion.31 = f32[13,1024]{1,0:T(8,128)S(1)} fusion(bf16[2048,1024]{0,1:T(8,128)(2,1)} %bitcast.41, f32[13,2048]{1,0:T(8,128)S(1)} %stack.2, f32[]{:T(128)} %fusion.70, f32[2048]{0:T(1024)S(1)} %get-tuple-element.40), kind=kOutput, calls=%fused_computation.63 | convolution fusion | flops 54605824 | bytes 4362244 | tf_op jit(solution)/shard_map/dot_general | solution.py:149
  120.3 3.8 %psum.7 = f32[13,1024]{1,0:T(8,128)S(1)} all-reduce(f32[13,1024]{1,0:T(8,128)S(1)} %fusion.31), channel_id=1, replica_groups=mesh['space'=128,'vel'=2] {'vel'}, use_global_device_ids=true, to_apply=%region_1.2 | all-reduce | flops 13312 | bytes 106496 | tf_op jit(solution)/shard_map/psum | solution.py:150
  124.4 9.4 %collective-permute-start.2 = (bf16[13,1,256]{2,1,0:T(2,128)(2,1)S(1)}, bf16[13,1,256]{2,1,0:T(2,128)(2,1)S(1)}, u32[]{:S(2)}, u32[]{:S(2)}) collective-permute-start(bf16[13,1,256]{2,1,0:T(2,128)(2,1)S(1)} %get-tuple-element.34), channel_id=1, source_target_pairs={{0,2},{2,4},{4,6},{6,8},{8,10},{10,12},{12,14},{14,16},{16,18},{18... | collective-permute-start | bytes 19976 | tf_op jit(solution)/shard_map/ppermute | solution.py:26
  133.7 1.9 collective-permute-start.3
  136.0 0.6 fusion.98
  136.9 3.8 %collective-permute-done.8 = f32[]{:T(128)} collective-permute-done((f32[]{:T(128)}, f32[]{:T(128)}, u32[]{:S(2)}, u32[]{:S(2)}) %collective-permute-start.8) | collective-permute-done | bytes 36 | tf_op jit(solution)/shard_map/ppermute | solution.py:41
  141.9 1.4 collective-permute-start.9
  143.3 3.9 %collective-permute-done.9 = f32[]{:T(128)} collective-permute-done((f32[]{:T(128)}, f32[]{:T(128)}, u32[]{:S(2)}, u32[]{:S(2)}) %collective-permute-start.9) | collective-permute-done | bytes 36 | tf_op jit(solution)/shard_map/ppermute | solution.py:41
  147.8 1.4 collective-permute-start.10
  149.2 2.4 %collective-permute-done.10 = f32[]{:T(128)} collective-permute-done((f32[]{:T(128)}, f32[]{:T(128)}, u32[]{:S(2)}, u32[]{:S(2)}) %collective-permute-start.10) | collective-permute-done | bytes 36 | tf_op jit(solution)/shard_map/ppermute | solution.py:41
  152.1 1.4 collective-permute-start.11
  153.5 3.9 %collective-permute-done.11 = f32[]{:T(128)} collective-permute-done((f32[]{:T(128)}, f32[]{:T(128)}, u32[]{:S(2)}, u32[]{:S(2)}) %collective-permute-start.11) | collective-permute-done | bytes 36 | tf_op jit(solution)/shard_map/ppermute | solution.py:41
  157.9 1.4 collective-permute-start.12
  159.3 2.4 %collective-permute-done.12 = f32[]{:T(128)} collective-permute-done((f32[]{:T(128)}, f32[]{:T(128)}, u32[]{:S(2)}, u32[]{:S(2)}) %collective-permute-start.12) | collective-permute-done | bytes 36 | tf_op jit(solution)/shard_map/ppermute | solution.py:41
  162.3 1.4 collective-permute-start.13
  163.6 3.3 %collective-permute-done.13 = f32[]{:T(128)} collective-permute-done((f32[]{:T(128)}, f32[]{:T(128)}, u32[]{:S(2)}, u32[]{:S(2)}) %collective-permute-start.13) | collective-permute-done | bytes 36 | tf_op jit(solution)/shard_map/ppermute | solution.py:41
  167.5 1.5 collective-permute-start.14
  169.0 6.1 %collective-permute-done.14 = f32[]{:T(128)} collective-permute-done((f32[]{:T(128)}, f32[]{:T(128)}, u32[]{:S(2)}, u32[]{:S(2)}) %collective-permute-start.14) | collective-permute-done | bytes 36 | tf_op jit(solution)/shard_map/ppermute | solution.py:41
  175.9 9.4 %collective-permute-start.4 = (bf16[13,1,256]{2,1,0:T(2,128)(2,1)S(1)}, bf16[13,1,256]{2,1,0:T(2,128)(2,1)S(1)}, u32[]{:S(2)}, u32[]{:S(2)}) collective-permute-start(bf16[13,1,256]{2,1,0:T(2,128)(2,1)S(1)} %get-tuple-element.32), channel_id=1, source_target_pairs={{0,2},{2,4},{4,6},{6,8},{8,10},{10,12},{12,14},{14,16},{16,18},{18... | collective-permute-start | bytes 19976 | tf_op jit(solution)/shard_map/ppermute | solution.py:26
  185.3 1.9 collective-permute-start.5
  187.9 8.4 %collective-permute-done.5 = bf16[13,1,256]{2,1,0:T(2,128)(2,1)S(1)} collective-permute-done((bf16[13,1,256]{2,1,0:T(2,128)(2,1)S(1)}, bf16[13,1,256]{2,1,0:T(2,128)(2,1)S(1)}, u32[]{:S(2)}, u32[]{:S(2)}) %collective-permute-start.5) | collective-permute-done | bytes 6688 | tf_op jit(solution)/shard_map/ppermute | solution.py:28
  196.4 1.9 collective-permute-start.6
  198.4 3.9 %collective-permute-start.7 = (bf16[13,1,256]{2,1,0:T(2,128)(2,1)S(1)}, bf16[13,1,256]{2,1,0:T(2,128)(2,1)S(1)}, u32[]{:S(2)}, u32[]{:S(2)}) collective-permute-start(bf16[13,1,256]{2,1,0:T(2,128)(2,1)S(1)} %get-tuple-element.31), channel_id=1, source_target_pairs={{2,0},{4,2},{6,4},{8,6},{10,8},{12,10},{14,12},{16,14},{18,16},{20... | collective-permute-start | bytes 19976 | tf_op jit(solution)/shard_map/ppermute | solution.py:28
  203.0 6.4 %collective-permute-done.7 = bf16[13,1,256]{2,1,0:T(2,128)(2,1)S(1)} collective-permute-done((bf16[13,1,256]{2,1,0:T(2,128)(2,1)S(1)}, bf16[13,1,256]{2,1,0:T(2,128)(2,1)S(1)}, u32[]{:S(2)}, u32[]{:S(2)}) %collective-permute-start.7) | collective-permute-done | bytes 6688 | tf_op jit(solution)/shard_map/ppermute | solution.py:28
  209.4 0.7 broadcast_multiply_fusion.1
  210.2 5.5 %multiply_convert_fusion = bf16[2048,1024]{0,1:T(8,128)(2,1)} fusion(bf16[2048,1024]{0,1:T(8,128)(2,1)} %bitcast.42, bf16[13,1024]{1,0:T(8,128)(2,1)S(1)} %bitcast.48, f32[1024]{0:T(1024)S(1)} %bitcast.50, f32[13,2048]{1,0:T(8,128)S(1)} %stack.2, f32[2048]{0:T(1024)S(1)} %exponential_multiply_fusion), kind=kOutput, calls=%fused_computation.23 | convolution fusion | flops 62967808 | bytes 8534016 | tf_op jit(solution)/shard_map/dot_general | solution.py:160
  215.7 7.4 %copy.33 = bf16[2048,4,256]{2,1,0:T(4,128)(2,1)} copy(bf16[2048,4,256]{0,2,1:T(8,128)(2,1)} %bitcast.46) | data formatting | bytes 8388608
  (60 shorter events, 4.2 us)
Async XLA Ops:
  7.0 2.0 copy-start
  10.5 60.1 %collective-permute-start = (bf16[2048,1,256]{2,0,1:T(8,128)(2,1)}, bf16[2048,1,256]{2,0,1:T(8,128)(2,1)}, u32[]{:S(2)}, u32[]{:S(2)}) collective-permute-start(bf16[2048,1,256]{2,0,1:T(8,128)(2,1)} %get-tuple-element.24), channel_id=1, source_target_pairs={{0,2},{2,4},{4,6},{6,8},{8,10},{10,12},{12,14},{14,16},{16,18},{18... | collective-permute-start | bytes 3145736 | tf_op jit(solution)/shard_map/ppermute | solution.py:26
  15.1 59.1 %collective-permute-start.1 = (bf16[2048,1,256]{2,0,1:T(8,128)(2,1)}, bf16[2048,1,256]{2,0,1:T(8,128)(2,1)}, u32[]{:S(2)}, u32[]{:S(2)}) collective-permute-start(bf16[2048,1,256]{2,0,1:T(8,128)(2,1)} %get-tuple-element.25), channel_id=1, source_target_pairs={{2,0},{4,2},{6,4},{8,6},{10,8},{12,10},{14,12},{16,14},{18,16},{20... | collective-permute-start | bytes 3145736 | tf_op jit(solution)/shard_map/ppermute | solution.py:28
  60.5 8.7 %copy-start.4 = (s32[4,256]{1,0:T(4,128)S(1)}, s32[4,256]{1,0:T(4,128)}, u32[]{:S(2)}) copy-start(s32[4,256]{1,0:T(4,128)} %param.6) | copy-start | bytes 12292
  60.5 10.0 %copy-start.3 = (f32[4,256]{1,0:T(4,128)S(1)}, f32[4,256]{1,0:T(4,128)}, u32[]{:S(2)}) copy-start(f32[4,256]{1,0:T(4,128)} %param.5) | copy-start | bytes 12292
  60.5 10.0 %copy-start.5 = (s32[4,256]{1,0:T(4,128)S(1)}, s32[4,256]{1,0:T(4,128)}, u32[]{:S(2)}) copy-start(s32[4,256]{1,0:T(4,128)} %param.7) | copy-start | bytes 12292
  69.8 7.6 %copy-start.2 = (bf16[2048,4,256]{2,1,0:T(4,128)(2,1)S(1)}, bf16[2048,4,256]{2,1,0:T(4,128)(2,1)}, u32[]{:S(2)}) copy-start(bf16[2048,4,256]{2,1,0:T(4,128)(2,1)} %param.4) | copy-start | bytes 12582916
  85.6 8.9 %copy-start.1 = (bf16[2048,4,256]{2,0,1:T(8,128)(2,1)S(1)}, bf16[2048,4,256]{2,0,1:T(8,128)(2,1)}, u32[]{:S(2)}) copy-start(bf16[2048,4,256]{2,0,1:T(8,128)(2,1)} %copy-done) | copy-start | bytes 12582916
  124.4 51.4 %collective-permute-start.2 = (bf16[13,1,256]{2,1,0:T(2,128)(2,1)S(1)}, bf16[13,1,256]{2,1,0:T(2,128)(2,1)S(1)}, u32[]{:S(2)}, u32[]{:S(2)}) collective-permute-start(bf16[13,1,256]{2,1,0:T(2,128)(2,1)S(1)} %get-tuple-element.34), channel_id=1, source_target_pairs={{0,2},{2,4},{4,6},{6,8},{8,10},{10,12},{12,14},{14,16},{16,18},{18... | collective-permute-start | bytes 19976 | tf_op jit(solution)/shard_map/ppermute | solution.py:26
  133.7 42.0 %collective-permute-start.3 = (bf16[13,1,256]{2,1,0:T(2,128)(2,1)S(1)}, bf16[13,1,256]{2,1,0:T(2,128)(2,1)S(1)}, u32[]{:S(2)}, u32[]{:S(2)}) collective-permute-start(bf16[13,1,256]{2,1,0:T(2,128)(2,1)S(1)} %get-tuple-element.35), channel_id=1, source_target_pairs={{2,0},{4,2},{6,4},{8,6},{10,8},{12,10},{14,12},{16,14},{18,16},{20... | collective-permute-start | bytes 19976 | tf_op jit(solution)/shard_map/ppermute | solution.py:28
  136.8 3.9 %collective-permute-start.8 = (f32[]{:T(128)}, f32[]{:T(128)}, u32[]{:S(2)}, u32[]{:S(2)}) collective-permute-start(f32[]{:T(128)} %fusion.98), channel_id=1, source_target_pairs={{0,2},{2,0},{4,6},{6,4},{8,10},{10,8},{12,14},{14,12},{16,18},{18,... | collective-permute-start | bytes 20 | tf_op jit(solution)/shard_map/ppermute | solution.py:41
  141.9 5.3 %collective-permute-start.9 = (f32[]{:T(128)}, f32[]{:T(128)}, u32[]{:S(2)}, u32[]{:S(2)}) collective-permute-start(f32[]{:T(128)} %add.749), channel_id=1, source_target_pairs={{0,4},{2,6},{4,0},{6,2},{8,12},{10,14},{12,8},{14,10},{16,20},{18,... | collective-permute-start | bytes 20 | tf_op jit(solution)/shard_map/ppermute | solution.py:41
  147.8 3.8 %collective-permute-start.10 = (f32[]{:T(128)}, f32[]{:T(128)}, u32[]{:S(2)}, u32[]{:S(2)}) collective-permute-start(f32[]{:T(128)} %add.750), channel_id=1, source_target_pairs={{0,8},{2,10},{4,12},{6,14},{8,0},{10,2},{12,4},{14,6},{16,24},{18,... | collective-permute-start | bytes 20 | tf_op jit(solution)/shard_map/ppermute | solution.py:41
  152.1 5.3 %collective-permute-start.11 = (f32[]{:T(128)}, f32[]{:T(128)}, u32[]{:S(2)}, u32[]{:S(2)}) collective-permute-start(f32[]{:T(128)} %add.751), channel_id=1, source_target_pairs={{0,16},{2,18},{4,20},{6,22},{8,24},{10,26},{12,28},{14,30},{16,0},... | collective-permute-start | bytes 20 | tf_op jit(solution)/shard_map/ppermute | solution.py:41
  157.9 3.8 %collective-permute-start.12 = (f32[]{:T(128)}, f32[]{:T(128)}, u32[]{:S(2)}, u32[]{:S(2)}) collective-permute-start(f32[]{:T(128)} %add.752), channel_id=1, source_target_pairs={{0,32},{2,34},{4,36},{6,38},{8,40},{10,42},{12,44},{14,46},{16,48}... | collective-permute-start | bytes 20 | tf_op jit(solution)/shard_map/ppermute | solution.py:41
  162.3 4.7 %collective-permute-start.13 = (f32[]{:T(128)}, f32[]{:T(128)}, u32[]{:S(2)}, u32[]{:S(2)}) collective-permute-start(f32[]{:T(128)} %add.753), channel_id=1, source_target_pairs={{0,64},{2,66},{4,68},{6,70},{8,72},{10,74},{12,76},{14,78},{16,80}... | collective-permute-start | bytes 20 | tf_op jit(solution)/shard_map/ppermute | solution.py:41
  167.5 7.7 %collective-permute-start.14 = (f32[]{:T(128)}, f32[]{:T(128)}, u32[]{:S(2)}, u32[]{:S(2)}) collective-permute-start(f32[]{:T(128)} %add.754), channel_id=1, source_target_pairs={{0,128},{2,130},{4,132},{6,134},{8,136},{10,138},{12,140},{14,142}... | collective-permute-start | bytes 20 | tf_op jit(solution)/shard_map/ppermute | solution.py:41
  175.9 12.0 %collective-permute-start.4 = (bf16[13,1,256]{2,1,0:T(2,128)(2,1)S(1)}, bf16[13,1,256]{2,1,0:T(2,128)(2,1)S(1)}, u32[]{:S(2)}, u32[]{:S(2)}) collective-permute-start(bf16[13,1,256]{2,1,0:T(2,128)(2,1)S(1)} %get-tuple-element.32), channel_id=1, source_target_pairs={{0,2},{2,4},{4,6},{6,8},{8,10},{10,12},{12,14},{14,16},{16,18},{18... | collective-permute-start | bytes 19976 | tf_op jit(solution)/shard_map/ppermute | solution.py:26
  185.3 11.0 %collective-permute-start.5 = (bf16[13,1,256]{2,1,0:T(2,128)(2,1)S(1)}, bf16[13,1,256]{2,1,0:T(2,128)(2,1)S(1)}, u32[]{:S(2)}, u32[]{:S(2)}) collective-permute-start(bf16[13,1,256]{2,1,0:T(2,128)(2,1)S(1)} %get-tuple-element.33), channel_id=1, source_target_pairs={{2,0},{4,2},{6,4},{8,6},{10,8},{12,10},{14,12},{16,14},{18,16},{20... | collective-permute-start | bytes 19976 | tf_op jit(solution)/shard_map/ppermute | solution.py:28
  196.4 6.6 %collective-permute-start.6 = (bf16[13,1,256]{2,1,0:T(2,128)(2,1)S(1)}, bf16[13,1,256]{2,1,0:T(2,128)(2,1)S(1)}, u32[]{:S(2)}, u32[]{:S(2)}) collective-permute-start(bf16[13,1,256]{2,1,0:T(2,128)(2,1)S(1)} %get-tuple-element.30), channel_id=1, source_target_pairs={{0,2},{2,4},{4,6},{6,8},{8,10},{10,12},{12,14},{14,16},{16,18},{18... | collective-permute-start | bytes 19976 | tf_op jit(solution)/shard_map/ppermute | solution.py:26
  198.4 11.0 %collective-permute-start.7 = (bf16[13,1,256]{2,1,0:T(2,128)(2,1)S(1)}, bf16[13,1,256]{2,1,0:T(2,128)(2,1)S(1)}, u32[]{:S(2)}, u32[]{:S(2)}) collective-permute-start(bf16[13,1,256]{2,1,0:T(2,128)(2,1)S(1)} %get-tuple-element.31), channel_id=1, source_target_pairs={{2,0},{4,2},{6,4},{8,6},{10,8},{12,10},{14,12},{16,14},{18,16},{20... | collective-permute-start | bytes 19976 | tf_op jit(solution)/shard_map/ppermute | solution.py:28

commit v3 on v2

--- a/solution.py
+++ b/solution.py
@@ -4,6 +4,8 @@
 import jax.numpy as jnp
 from jax import lax
 from jax.sharding import PartitionSpec as P
+from jax.experimental import pallas as pl
+from jax.experimental.pallas import tpu as pltpu
 
 NV1 = 16
 NM = 13
@@ -13,6 +15,7 @@
 
 
 TIME_STEP = 0.06
+PLANE = NY * NZ
 
 
 def with_halo(cells, sides, width):
@@ -108,45 +111,88 @@
     return inverse * (source + beside_all)
 
 
+def advance_kernel(adj_ref, left_ref, right_ref, cx_ref, cy_ref, cz_ref, coll_ref, fluid_ref, weigh_ref,
+                   star_ref, part_ref):
+    step = pl.program_id(0)
+    g = adj_ref[...].astype(jnp.float32)
+    rows, lanes = g.shape
+    cx = cx_ref[...]
+    cy = cy_ref[...]
+    cz = cz_ref[...]
+    left = left_ref[...].astype(jnp.float32)
+    right = right_ref[...].astype(jnp.float32)
+    after = jnp.concatenate([g[:, PLANE:], right], axis=1)
+    before = jnp.concatenate([left, g[:, : lanes - PLANE]], axis=1)
+    lane = lax.broadcasted_iota(jnp.int32, (1, lanes), 1)
+    zpos = lane % NZ
+    ypos = (lane // NZ) % (PLANE // NZ)
+    y_next = jnp.where(ypos == PLANE // NZ - 1, 0.0, pltpu.roll(g, lanes - NZ, 1))
+    y_prev = jnp.where(ypos == 0, 0.0, pltpu.roll(g, NZ, 1))
+    z_next = jnp.where(zpos == NZ - 1, 0.0, pltpu.roll(g, lanes - 1, 1))
+    z_prev = jnp.where(zpos == 0, 0.0, pltpu.roll(g, 1, 1))
+    term_x = jnp.maximum(cx, 0.0) * (after - g) + jnp.minimum(cx, 0.0) * (g - before)
+    term_y = jnp.maximum(cy, 0.0) * (y_next - g) + jnp.minimum(cy, 0.0) * (g - y_prev)
+    term_z = jnp.maximum(cz, 0.0) * (z_next - g) + jnp.minimum(cz, 0.0) * (g - z_prev)
+    advect = term_x + term_y + term_z
+    starred = (fluid_ref[...] * (g + TIME_STEP * (advect - coll_ref[...] * g))).astype(jnp.bfloat16)
+    star_ref[...] = starred
+    partial = jnp.dot(weigh_ref[...], starred, preferred_element_type=jnp.float32)
+
+    @pl.when(step == 0)
+    def _():
+        part_ref[...] = partial
+
+    @pl.when(step > 0)
+    def _():
+        part_ref[...] += partial
+
+
+def advance(adj, left, right, cx, cy, cz, coll, fluid, weigh, block=256):
+    nv, lanes = adj.shape
+    nm = weigh.shape[0]
+    grid = (nv // block,)
+    row = lambda i: (i, 0)
+    fixed = lambda i: (0, 0)
+    return pl.pallas_call(
+        advance_kernel,
+        grid=grid,
+        in_specs=[
+            pl.BlockSpec((block, lanes), row),
+            pl.BlockSpec((block, PLANE), row),
+            pl.BlockSpec((block, PLANE), row),
+            pl.BlockSpec((block, 1), row),
+            pl.BlockSpec((block, 1), row),
+            pl.BlockSpec((block, 1), row),
+            pl.BlockSpec((1, lanes), fixed),
+            pl.BlockSpec((1, lanes), fixed),
+            pl.BlockSpec((nm, block), lambda i: (0, i)),
+        ],
+        out_specs=[pl.BlockSpec((block, lanes), row), pl.BlockSpec((nm, lanes), fixed)],
+        out_shape=[jax.ShapeDtypeStruct((nv, lanes), jnp.bfloat16), jax.ShapeDtypeStruct((nm, lanes), jnp.float32)],
+        compiler_params=pltpu.CompilerParams(dimension_semantics=("arbitrary",)),
+    )(adj, left, right, cx, cy, cz, coll, fluid, weigh)
+
+
 def on_device(adjoint, collision, solid, codes):
     local_vel, width, plane = adjoint.shape
     start = lax.axis_index("vel") * local_vel
     speed_x, speed_y, speed_z, weigh, lift = tables(start, local_vel)
-    half = NV1 // 2
-    groups = local_vel // NV1
-    grid = adjoint.reshape(groups, NV1, width, plane)
-    widened = with_halo(adjoint, (("space", 1),), 1).reshape(groups, NV1, width + 2, plane)
-    left_rim = widened[:, :half, 0]
-    right_rim = widened[:, half:, width + 1]
-    lower = grid[:, :half].astype(jnp.float32)
-    upper = grid[:, half:].astype(jnp.float32)
-    before = jnp.concatenate([left_rim[:, :, None].astype(jnp.float32), lower[:, :, :-1]], axis=2)
-    after = jnp.concatenate([upper[:, :, 1:], right_rim[:, :, None].astype(jnp.float32)], axis=2)
-    shaped_x = speed_x.reshape(groups, NV1, 1, 1)
-    term_x = jnp.concatenate(
-        [shaped_x[:, :half] * (lower - before), shaped_x[:, half:] * (after - upper)], axis=1
-    )
-    term_x = term_x.reshape(local_vel, width, plane)
-    flat = adjoint.astype(jnp.float32)
-    cube = flat.reshape(local_vel, width, NY, NZ)
-    padded = jnp.pad(cube, ((0, 0), (0, 0), (1, 1), (1, 1)))
-    shaped_y = speed_y[:, None, None, None]
-    shaped_z = speed_z[:, None, None, None]
-    term_y = jnp.maximum(shaped_y, 0.0) * (padded[:, :, 2:, 1:-1] - cube) + jnp.minimum(
-        shaped_y, 0.0
-    ) * (cube - padded[:, :, :-2, 1:-1])
-    term_z = jnp.maximum(shaped_z, 0.0) * (padded[:, :, 1:-1, 2:] - cube) + jnp.minimum(
-        shaped_z, 0.0
-    ) * (cube - padded[:, :, 1:-1, :-2])
-    advect = (
-        term_x + term_y.reshape(local_vel, width, plane) + term_z.reshape(local_vel, width, plane)
-    )
+    count = lax.axis_size("space")
+    ends = count - 1
+    left = lax.ppermute(adjoint[:, width - 1], "space", [(i, i + 1) for i in range(ends)])
+    right = lax.ppermute(adjoint[:, 0], "space", [(i + 1, i) for i in range(ends)])
     fluid = (1 - solid).astype(jnp.float32)
-    starred = (fluid[None] * (flat + TIME_STEP * (advect - collision[None] * flat))).astype(
-        jnp.bfloat16
-    )
-    starred_flat = starred.reshape(local_vel, width * plane)
-    partial_value = jnp.dot(weigh, starred_flat, preferred_element_type=jnp.float32)
+    starred_flat, partial_value = advance(
+        adjoint.reshape(local_vel, width * plane),
+        left,
+        right,
+        speed_x.reshape(local_vel, 1),
+        speed_y.reshape(local_vel, 1),
+        speed_z.reshape(local_vel, 1),
+        collision.reshape(1, width * plane),
+        fluid.reshape(1, width * plane),
+        weigh,
+    )
     moments = lax.psum(partial_value, "vel").reshape(NM, width, plane)
     cells_all = width * lax.axis_size("space") * plane
     squares = exchange_sum(jnp.sum(moments[0] * moments[0]), "space")

time: 224 us -> 155 us (0.69)
  other arithmetic: 58.7 us -> 12.3 us
  local copies, waits for them, and re-layouts: 61.4 us -> 26.3 us
  Pallas kernels: 0 us -> 15.8 us
  waiting for transfers between devices: 40.5 us -> 49.6 us
  matrix products: 9.54 us -> 1.28 us
  starting transfers between devices: 43.5 us -> 38.3 us
    add x1 -> x0, other arithmetic: 20.2 us -> none  [on_device(): jnp.maximum(shaped_y, 0.0) * (padded[:, :, 2:, 1:-1] - cube)]
    ppermute x0 -> x2, waiting for transfers between devices: none -> 16.1 us  [the longest x1 11.1 us: on_device(): lax.ppermute(adjoint[:, 0], 'space', [(i + 1, i) for i in range(ends)])]
    pallas_call x0 -> x1, Pallas kernels: none -> 15.8 us  [advance(): pl.pallas_call(advance_kernel, grid=grid, in_specs=[pl.BlockSpec((block,...]
    convert_element_type x2 -> x0, local copies, waits for them, and re-layouts: 15 us -> none  [the longest x1 8.7 us: on_device(): flat = adjoint.astype(jnp.float32)]
    ppermute x4 -> x3, starting transfers between devices: 25.2 us -> 11.2 us  [with_halo(): lax.ppermute(tail, axis, [(i, (i + 1) % count) for i in range(ends)])]
    concatenate x2 -> x0, other arithmetic: 11 us -> none  [the longest x1 8.21 us: with_halo(): jnp.concatenate([lax.ppermute(tail, axis, [(i, (i + 1) % count) for i in...]
    reshape x2 -> x1, local copies, waits for them, and re-layouts: 17.5 us -> 7.83 us  [on_device(): return (corrected.reshape(local_vel, width, plane), fields * scale)]
    convert_element_type x3 -> x2, other arithmetic: 13.1 us -> 4.84 us  [the longest x1 3.56 us: on_device(): (fluid.reshape(1, width * plane) * (starred_flat + added)).astype(jnp.bfl...]
  transfers between devices with their start and end apart: 15 -> 15, of which waited for: 9 -> 10; matrix products, arithmetic and copies ran while one was open for 27% -> 11% of each run, Pallas kernels for 0% -> 0%
where the time goes in v3:
time: 155 us; the launch traced here: 154 us
  waiting for transfers between devices  49.6 us (32%)
  starting transfers between devices  38.3 us (25%)
  local copies, waits for them, and re-layouts  26.3 us (17%)
  Pallas kernels  15.8 us (10%)
  other arithmetic  12.3 us (8%)
  between operations  6.16 us (4%)
  blocking collectives  4.2 us (3%)
    ppermute x7, waiting for transfers between devices, exchange_sum(): lax.ppermute(value, axis, [(i, i ^ step) for i in range(count)])  18.9 us
    pallas_call x1, Pallas kernels, advance(): pl.pallas_call(advance_kernel, grid=grid, in_specs=[pl.BlockSpec((block,...  15.8 us
    ppermute x3, waiting for transfers between devices, with_halo(): lax.ppermute(head, axis, [((i + 1) % count, i) for i in range(ends)])  14.6 us
    ppermute x3, starting transfers between devices, with_halo(): lax.ppermute(tail, axis, [(i, (i + 1) % count) for i in range(ends)])  11.2 us
    ppermute x1, waiting for transfers between devices, on_device(): lax.ppermute(adjoint[:, 0], 'space', [(i + 1, i) for i in range(ends)])  11.1 us
    ppermute x7, starting transfers between devices, exchange_sum(): lax.ppermute(value, axis, [(i, i ^ step) for i in range(count)])  10.6 us
    ppermute x3, starting transfers between devices, with_halo(): lax.ppermute(head, axis, [((i + 1) % count, i) for i in range(ends)])  9.95 us
    unnamed x16, local copies, waits for them, and re-layouts  8.81 us
  transfers between devices with their start and end apart: 15, of which 10 were waited for; matrix products, arithmetic and copies ran while one was open for 11% of the time, Pallas kernels for 0%

profile of v3, /device:TPU:126, one launch (start us, length us, event | category | flops | bytes accessed | tf_op | source)
XLA Modules:
  0.0 153.9 jit_solution(17806727576031705573)
XLA Ops:
  0.6 6.9 %fusion.94 = (bf16[2048,1,256]{2,1,0:T(2,128)(2,1)S(1)}, bf16[2048,1,256]{2,1,0:T(2,128)(2,1)S(1)}) fusion(bf16[2048,4,256]{2,1,0:T(4,128)(2,1)} %param.4), kind=kLoop, calls=%fused_computation.185 | loop fusion | bytes 4194304 | tf_op jit(solution)/shard_map/slice | solution.py:183
  7.8 4.6 %collective-permute-start = (bf16[2048,256]{1,0:T(8,128)(2,1)S(1)}, bf16[2048,256]{1,0:T(8,128)(2,1)}, u32[]{:S(2)}, u32[]{:S(2)}) collective-permute-start(bf16[2048,256]{1,0:T(8,128)(2,1)S(1)} %bitcast.30), channel_id=1, source_target_pairs={{0,2},{2,4},{4,6},{6,8},{8,10},{10,12},{12,14},{14,16},{16,18},{18... | collective-permute-start | bytes 3145736 | tf_op jit(solution)/shard_map/ppermute | solution.py:182
  12.4 1.2 copy.28
  13.7 1.9 %collective-permute-start.1 = (bf16[2048,256]{1,0:T(8,128)(2,1)}, bf16[2048,256]{1,0:T(8,128)(2,1)}, u32[]{:S(2)}, u32[]{:S(2)}) collective-permute-start(bf16[2048,256]{1,0:T(8,128)(2,1)} %bitcast.26), channel_id=1, source_target_pairs={{2,0},{4,2},{6,4},{8,6},{10,8},{12,10},{14,12},{16,14},{18,16},{20... | collective-permute-start | bytes 3145736 | tf_op jit(solution)/shard_map/ppermute | solution.py:183
  15.6 0.6 fusion.46
  17.3 0.4 copy.12
  17.7 1.0 broadcast_multiply_fusion.2.cx_ref
  18.9 1.3 divide_convert_fusion.weigh_ref
  20.3 0.6 copy.23
  20.9 0.6 copy.24
  21.5 0.4 copy.14
  21.9 0.4 copy.16
  22.3 5.2 %copy.22 = bf16[256,8,4,256]{3,1,2,0:T(8,128)(2,1)} copy(bf16[256,8,4,256]{3,2,1,0:T(4,128)(2,1)} %bitcast.28) | data formatting | bytes 8388608
  27.5 1.1 broadcast_multiply_fusion.1.cy_ref
  28.7 1.1 broadcast_multiply_fusion.cz_ref
  29.8 5.0 %collective-permute-done.left_ref = bf16[2048,256]{1,0:T(8,128)(2,1)} collective-permute-done((bf16[2048,256]{1,0:T(8,128)(2,1)S(1)}, bf16[2048,256]{1,0:T(8,128)(2,1)}, u32[]{:S(2)}, u32[]{:S(2)}) %collective-permute-start) | collective-permute-done | bytes 1048608 | tf_op jit(solution)/shard_map/ppermute | solution.py:182
  34.8 11.1 %collective-permute-done.1.right_ref = bf16[2048,256]{1,0:T(8,128)(2,1)} collective-permute-done((bf16[2048,256]{1,0:T(8,128)(2,1)}, bf16[2048,256]{1,0:T(8,128)(2,1)}, u32[]{:S(2)}, u32[]{:S(2)}) %collective-permute-start.1) | collective-permute-done | bytes 1048608 | tf_op jit(solution)/shard_map/ppermute | solution.py:183
  45.9 15.8 %shard_map.59 = (bf16[2048,1024]{1,0:T(8,128)(2,1)}, f32[13,1024]{1,0:T(8,128)}) custom-call(bf16[2048,1024]{1,0:T(8,128)(2,1)} %bitcast.29, bf16[2048,256]{1,0:T(8,128)(2,1)} %collective-permute-done.left_ref, bf16[2048,256]{1,0:T(8,128)(2,1)} %collective-permute-done.1.right_ref, f32[2048,1]{1,0:T(8,128)} %broadcast_multiply_fusion.2.cx_ref, ...), custom_call_target="tpu_custom_call" | custom-call | tf_op jit(solution)/shard_map/pallas_call | solution.py:156
  61.7 4.2 %psum.7 = f32[13,1024]{1,0:T(8,128)S(1)} all-reduce(f32[13,1024]{1,0:T(8,128)} %get-tuple-element.5), channel_id=1, replica_groups=mesh['space'=128,'vel'=2] {'vel'}, use_global_device_ids=true, to_apply=%region_1.2 | all-reduce | flops 13312 | bytes 106496 | tf_op jit(solution)/shard_map/psum | solution.py:196
  65.9 0.6 fusion.83
  66.9 1.9 %collective-permute-start.2 = (bf16[13,1,256]{2,1,0:T(2,128)(2,1)S(1)}, bf16[13,1,256]{2,1,0:T(2,128)(2,1)S(1)}, u32[]{:S(2)}, u32[]{:S(2)}) collective-permute-start(bf16[13,1,256]{2,1,0:T(2,128)(2,1)S(1)} %get-tuple-element.18), channel_id=1, source_target_pairs={{0,2},{2,4},{4,6},{6,8},{8,10},{10,12},{12,14},{14,16},{16,18},{18... | collective-permute-start | bytes 19976 | tf_op jit(solution)/shard_map/ppermute | solution.py:29
  68.8 3.9 %collective-permute-start.3 = (bf16[13,1,256]{2,1,0:T(2,128)(2,1)S(1)}, bf16[13,1,256]{2,1,0:T(2,128)(2,1)S(1)}, u32[]{:S(2)}, u32[]{:S(2)}) collective-permute-start(bf16[13,1,256]{2,1,0:T(2,128)(2,1)S(1)} %get-tuple-element.19), channel_id=1, source_target_pairs={{2,0},{4,2},{6,4},{8,6},{10,8},{12,10},{14,12},{16,14},{18,16},{20... | collective-permute-start | bytes 19976 | tf_op jit(solution)/shard_map/ppermute | solution.py:31
  72.8 0.3 fusion.2
  74.6 3.4 %collective-permute-start.9 = (f32[]{:T(128)}, f32[]{:T(128)}, u32[]{:S(2)}, u32[]{:S(2)}) collective-permute-start(f32[]{:T(128)} %add.718), channel_id=1, source_target_pairs={{0,4},{2,6},{4,0},{6,2},{8,12},{10,14},{12,8},{14,10},{16,20},{18,... | collective-permute-start | bytes 20 | tf_op jit(solution)/shard_map/ppermute | solution.py:44
  78.0 1.7 %collective-permute-done.9 = f32[]{:T(128)} collective-permute-done((f32[]{:T(128)}, f32[]{:T(128)}, u32[]{:S(2)}, u32[]{:S(2)}) %collective-permute-start.9) | collective-permute-done | bytes 36 | tf_op jit(solution)/shard_map/ppermute | solution.py:44
  80.3 1.4 collective-permute-start.10
  81.7 2.2 %collective-permute-done.10 = f32[]{:T(128)} collective-permute-done((f32[]{:T(128)}, f32[]{:T(128)}, u32[]{:S(2)}, u32[]{:S(2)}) %collective-permute-start.10) | collective-permute-done | bytes 36 | tf_op jit(solution)/shard_map/ppermute | solution.py:44
  84.6 1.4 collective-permute-start.11
  86.0 3.7 %collective-permute-done.11 = f32[]{:T(128)} collective-permute-done((f32[]{:T(128)}, f32[]{:T(128)}, u32[]{:S(2)}, u32[]{:S(2)}) %collective-permute-start.11) | collective-permute-done | bytes 36 | tf_op jit(solution)/shard_map/ppermute | solution.py:44
  90.3 1.4 collective-permute-start.12
  91.7 2.2 %collective-permute-done.12 = f32[]{:T(128)} collective-permute-done((f32[]{:T(128)}, f32[]{:T(128)}, u32[]{:S(2)}, u32[]{:S(2)}) %collective-permute-start.12) | collective-permute-done | bytes 36 | tf_op jit(solution)/shard_map/ppermute | solution.py:44
  94.6 1.4 collective-permute-start.13
  96.0 3.1 %collective-permute-done.13 = f32[]{:T(128)} collective-permute-done((f32[]{:T(128)}, f32[]{:T(128)}, u32[]{:S(2)}, u32[]{:S(2)}) %collective-permute-start.13) | collective-permute-done | bytes 36 | tf_op jit(solution)/shard_map/ppermute | solution.py:44
  99.7 1.5 %collective-permute-start.14 = (f32[]{:T(128)}, f32[]{:T(128)}, u32[]{:S(2)}, u32[]{:S(2)}) collective-permute-start(f32[]{:T(128)} %add.723), channel_id=1, source_target_pairs={{0,128},{2,130},{4,132},{6,134},{8,136},{10,138},{12,140},{14,142}... | collective-permute-start | bytes 20 | tf_op jit(solution)/shard_map/ppermute | solution.py:44
  101.3 6.0 %collective-permute-done.14 = f32[]{:T(128)} collective-permute-done((f32[]{:T(128)}, f32[]{:T(128)}, u32[]{:S(2)}, u32[]{:S(2)}) %collective-permute-start.14) | collective-permute-done | bytes 36 | tf_op jit(solution)/shard_map/ppermute | solution.py:44
  108.1 7.4 %collective-permute-start.4 = (bf16[13,1,256]{2,1,0:T(2,128)(2,1)S(1)}, bf16[13,1,256]{2,1,0:T(2,128)(2,1)S(1)}, u32[]{:S(2)}, u32[]{:S(2)}) collective-permute-start(bf16[13,1,256]{2,1,0:T(2,128)(2,1)S(1)} %get-tuple-element.16), channel_id=1, source_target_pairs={{0,2},{2,4},{4,6},{6,8},{8,10},{10,12},{12,14},{14,16},{16,18},{18... | collective-permute-start | bytes 19976 | tf_op jit(solution)/shard_map/ppermute | solution.py:29
  115.4 2.1 %collective-permute-start.5 = (bf16[13,1,256]{2,1,0:T(2,128)(2,1)S(1)}, bf16[13,1,256]{2,1,0:T(2,128)(2,1)S(1)}, u32[]{:S(2)}, u32[]{:S(2)}) collective-permute-start(bf16[13,1,256]{2,1,0:T(2,128)(2,1)S(1)} %get-tuple-element.17), channel_id=1, source_target_pairs={{2,0},{4,2},{6,4},{8,6},{10,8},{12,10},{14,12},{16,14},{18,16},{20... | collective-permute-start | bytes 19976 | tf_op jit(solution)/shard_map/ppermute | solution.py:31
  117.7 0.3 fusion.5
  118.3 8.2 %collective-permute-done.5 = bf16[13,1,256]{2,1,0:T(2,128)(2,1)S(1)} collective-permute-done((bf16[13,1,256]{2,1,0:T(2,128)(2,1)S(1)}, bf16[13,1,256]{2,1,0:T(2,128)(2,1)S(1)}, u32[]{:S(2)}, u32[]{:S(2)}) %collective-permute-start.5) | collective-permute-done | bytes 6688 | tf_op jit(solution)/shard_map/ppermute | solution.py:31
  126.6 1.9 %collective-permute-start.6 = (bf16[13,1,256]{2,1,0:T(2,128)(2,1)S(1)}, bf16[13,1,256]{2,1,0:T(2,128)(2,1)S(1)}, u32[]{:S(2)}, u32[]{:S(2)}) collective-permute-start(bf16[13,1,256]{2,1,0:T(2,128)(2,1)S(1)} %get-tuple-element.14), channel_id=1, source_target_pairs={{0,2},{2,4},{4,6},{6,8},{8,10},{10,12},{12,14},{14,16},{16,18},{18... | collective-permute-start | bytes 19976 | tf_op jit(solution)/shard_map/ppermute | solution.py:29
  128.5 3.9 %collective-permute-start.7 = (bf16[13,1,256]{2,1,0:T(2,128)(2,1)S(1)}, bf16[13,1,256]{2,1,0:T(2,128)(2,1)S(1)}, u32[]{:S(2)}, u32[]{:S(2)}) collective-permute-start(bf16[13,1,256]{2,1,0:T(2,128)(2,1)S(1)} %get-tuple-element.15), channel_id=1, source_target_pairs={{2,0},{4,2},{6,4},{8,6},{10,8},{12,10},{14,12},{16,14},{18,16},{20... | collective-permute-start | bytes 19976 | tf_op jit(solution)/shard_map/ppermute | solution.py:31
  132.6 0.3 fusion.8
  133.2 6.4 %collective-permute-done.7 = bf16[13,1,256]{2,1,0:T(2,128)(2,1)S(1)} collective-permute-done((bf16[13,1,256]{2,1,0:T(2,128)(2,1)S(1)}, bf16[13,1,256]{2,1,0:T(2,128)(2,1)S(1)}, u32[]{:S(2)}, u32[]{:S(2)}) %collective-permute-start.7) | collective-permute-done | bytes 6688 | tf_op jit(solution)/shard_map/ppermute | solution.py:31
  139.6 0.7 broadcast_multiply_fusion.4
  140.3 1.3 fusion.9
  141.6 0.9 copy-done
  142.5 3.6 %multiply_convert_fusion = bf16[2048,1024]{1,0:T(8,128)(2,1)} fusion(f32[2048,1024]{1,0:T(8,128)S(1)} %fusion.9, bf16[2048,1024]{1,0:T(8,128)(2,1)S(1)} %copy-done, f32[1024]{0:T(1024)S(1)} %bitcast.34), kind=kLoop, calls=%fused_computation | loop fusion | flops 8388608 | bytes 16781312 | tf_op jit(solution)/shard_map/convert_element_type | solution.py:207
  146.1 7.8 %reshape.475 = bf16[2048,4,256]{2,1,0:T(4,128)(2,1)} reshape(bf16[2048,1024]{1,0:T(8,128)(2,1)} %multiply_convert_fusion) | data formatting | bytes 8388608 | tf_op jit(solution)/shard_map/reshape | solution.py:208
  (49 shorter events, 3.3 us)
Async XLA Ops:
  7.6 9.7 %copy-start.2 = (s32[4,256]{1,0:T(4,128)S(1)}, s32[4,256]{1,0:T(4,128)}, u32[]{:S(2)}) copy-start(s32[4,256]{1,0:T(4,128)} %param.6) | copy-start | bytes 12292
  7.6 11.1 %copy-start.1 = (f32[4,256]{1,0:T(4,128)S(1)}, f32[4,256]{1,0:T(4,128)}, u32[]{:S(2)}) copy-start(f32[4,256]{1,0:T(4,128)} %param.5) | copy-start | bytes 12292
  7.6 11.1 %copy-start.3 = (s32[4,256]{1,0:T(4,128)S(1)}, s32[4,256]{1,0:T(4,128)}, u32[]{:S(2)}) copy-start(s32[4,256]{1,0:T(4,128)} %param.7) | copy-start | bytes 12292
  7.8 27.0 %collective-permute-start = (bf16[2048,256]{1,0:T(8,128)(2,1)S(1)}, bf16[2048,256]{1,0:T(8,128)(2,1)}, u32[]{:S(2)}, u32[]{:S(2)}) collective-permute-start(bf16[2048,256]{1,0:T(8,128)(2,1)S(1)} %bitcast.30), channel_id=1, source_target_pairs={{0,2},{2,4},{4,6},{6,8},{8,10},{10,12},{12,14},{14,16},{16,18},{18... | collective-permute-start | bytes 3145736 | tf_op jit(solution)/shard_map/ppermute | solution.py:182
  13.7 32.2 %collective-permute-start.1 = (bf16[2048,256]{1,0:T(8,128)(2,1)}, bf16[2048,256]{1,0:T(8,128)(2,1)}, u32[]{:S(2)}, u32[]{:S(2)}) collective-permute-start(bf16[2048,256]{1,0:T(8,128)(2,1)} %bitcast.26), channel_id=1, source_target_pairs={{2,0},{4,2},{6,4},{8,6},{10,8},{12,10},{14,12},{16,14},{18,16},{20... | collective-permute-start | bytes 3145736 | tf_op jit(solution)/shard_map/ppermute | solution.py:183
  66.7 6.6 %collective-permute-start.8 = (f32[]{:T(128)}, f32[]{:T(128)}, u32[]{:S(2)}, u32[]{:S(2)}) collective-permute-start(f32[]{:T(128)} %fusion.83), channel_id=1, source_target_pairs={{0,2},{2,0},{4,6},{6,4},{8,10},{10,8},{12,14},{14,12},{16,18},{18,... | collective-permute-start | bytes 20 | tf_op jit(solution)/shard_map/ppermute | solution.py:44
  66.9 41.0 %collective-permute-start.2 = (bf16[13,1,256]{2,1,0:T(2,128)(2,1)S(1)}, bf16[13,1,256]{2,1,0:T(2,128)(2,1)S(1)}, u32[]{:S(2)}, u32[]{:S(2)}) collective-permute-start(bf16[13,1,256]{2,1,0:T(2,128)(2,1)S(1)} %get-tuple-element.18), channel_id=1, source_target_pairs={{0,2},{2,4},{4,6},{6,8},{8,10},{10,12},{12,14},{14,16},{16,18},{18... | collective-permute-start | bytes 19976 | tf_op jit(solution)/shard_map/ppermute | solution.py:29
  68.8 39.1 %collective-permute-start.3 = (bf16[13,1,256]{2,1,0:T(2,128)(2,1)S(1)}, bf16[13,1,256]{2,1,0:T(2,128)(2,1)S(1)}, u32[]{:S(2)}, u32[]{:S(2)}) collective-permute-start(bf16[13,1,256]{2,1,0:T(2,128)(2,1)S(1)} %get-tuple-element.19), channel_id=1, source_target_pairs={{2,0},{4,2},{6,4},{8,6},{10,8},{12,10},{14,12},{16,14},{18,16},{20... | collective-permute-start | bytes 19976 | tf_op jit(solution)/shard_map/ppermute | solution.py:31
  74.6 5.1 %collective-permute-start.9 = (f32[]{:T(128)}, f32[]{:T(128)}, u32[]{:S(2)}, u32[]{:S(2)}) collective-permute-start(f32[]{:T(128)} %add.718), channel_id=1, source_target_pairs={{0,4},{2,6},{4,0},{6,2},{8,12},{10,14},{12,8},{14,10},{16,20},{18,... | collective-permute-start | bytes 20 | tf_op jit(solution)/shard_map/ppermute | solution.py:44
  80.3 3.6 %collective-permute-start.10 = (f32[]{:T(128)}, f32[]{:T(128)}, u32[]{:S(2)}, u32[]{:S(2)}) collective-permute-start(f32[]{:T(128)} %add.719), channel_id=1, source_target_pairs={{0,8},{2,10},{4,12},{6,14},{8,0},{10,2},{12,4},{14,6},{16,24},{18,... | collective-permute-start | bytes 20 | tf_op jit(solution)/shard_map/ppermute | solution.py:44
  84.6 5.1 %collective-permute-start.11 = (f32[]{:T(128)}, f32[]{:T(128)}, u32[]{:S(2)}, u32[]{:S(2)}) collective-permute-start(f32[]{:T(128)} %add.720), channel_id=1, source_target_pairs={{0,16},{2,18},{4,20},{6,22},{8,24},{10,26},{12,28},{14,30},{16,0},... | collective-permute-start | bytes 20 | tf_op jit(solution)/shard_map/ppermute | solution.py:44
  90.3 3.6 %collective-permute-start.12 = (f32[]{:T(128)}, f32[]{:T(128)}, u32[]{:S(2)}, u32[]{:S(2)}) collective-permute-start(f32[]{:T(128)} %add.721), channel_id=1, source_target_pairs={{0,32},{2,34},{4,36},{6,38},{8,40},{10,42},{12,44},{14,46},{16,48}... | collective-permute-start | bytes 20 | tf_op jit(solution)/shard_map/ppermute | solution.py:44
  94.6 4.5 %collective-permute-start.13 = (f32[]{:T(128)}, f32[]{:T(128)}, u32[]{:S(2)}, u32[]{:S(2)}) collective-permute-start(f32[]{:T(128)} %add.722), channel_id=1, source_target_pairs={{0,64},{2,66},{4,68},{6,70},{8,72},{10,74},{12,76},{14,78},{16,80}... | collective-permute-start | bytes 20 | tf_op jit(solution)/shard_map/ppermute | solution.py:44
  99.7 7.5 %collective-permute-start.14 = (f32[]{:T(128)}, f32[]{:T(128)}, u32[]{:S(2)}, u32[]{:S(2)}) collective-permute-start(f32[]{:T(128)} %add.723), channel_id=1, source_target_pairs={{0,128},{2,130},{4,132},{6,134},{8,136},{10,138},{12,140},{14,142}... | collective-permute-start | bytes 20 | tf_op jit(solution)/shard_map/ppermute | solution.py:44
  108.1 10.2 %collective-permute-start.4 = (bf16[13,1,256]{2,1,0:T(2,128)(2,1)S(1)}, bf16[13,1,256]{2,1,0:T(2,128)(2,1)S(1)}, u32[]{:S(2)}, u32[]{:S(2)}) collective-permute-start(bf16[13,1,256]{2,1,0:T(2,128)(2,1)S(1)} %get-tuple-element.16), channel_id=1, source_target_pairs={{0,2},{2,4},{4,6},{6,8},{8,10},{10,12},{12,14},{14,16},{16,18},{18... | collective-permute-start | bytes 19976 | tf_op jit(solution)/shard_map/ppermute | solution.py:29
  115.4 11.0 %collective-permute-start.5 = (bf16[13,1,256]{2,1,0:T(2,128)(2,1)S(1)}, bf16[13,1,256]{2,1,0:T(2,128)(2,1)S(1)}, u32[]{:S(2)}, u32[]{:S(2)}) collective-permute-start(bf16[13,1,256]{2,1,0:T(2,128)(2,1)S(1)} %get-tuple-element.17), channel_id=1, source_target_pairs={{2,0},{4,2},{6,4},{8,6},{10,8},{12,10},{14,12},{16,14},{18,16},{20... | collective-permute-start | bytes 19976 | tf_op jit(solution)/shard_map/ppermute | solution.py:31
  126.6 6.6 %collective-permute-start.6 = (bf16[13,1,256]{2,1,0:T(2,128)(2,1)S(1)}, bf16[13,1,256]{2,1,0:T(2,128)(2,1)S(1)}, u32[]{:S(2)}, u32[]{:S(2)}) collective-permute-start(bf16[13,1,256]{2,1,0:T(2,128)(2,1)S(1)} %get-tuple-element.14), channel_id=1, source_target_pairs={{0,2},{2,4},{4,6},{6,8},{8,10},{10,12},{12,14},{14,16},{16,18},{18... | collective-permute-start | bytes 19976 | tf_op jit(solution)/shard_map/ppermute | solution.py:29
  128.5 11.0 %collective-permute-start.7 = (bf16[13,1,256]{2,1,0:T(2,128)(2,1)S(1)}, bf16[13,1,256]{2,1,0:T(2,128)(2,1)S(1)}, u32[]{:S(2)}, u32[]{:S(2)}) collective-permute-start(bf16[13,1,256]{2,1,0:T(2,128)(2,1)S(1)} %get-tuple-element.15), channel_id=1, source_target_pairs={{2,0},{4,2},{6,4},{8,6},{10,8},{12,10},{14,12},{16,14},{18,16},{20... | collective-permute-start | bytes 19976 | tf_op jit(solution)/shard_map/ppermute | solution.py:31
  140.3 2.2 %copy-start = (bf16[2048,1024]{1,0:T(8,128)(2,1)S(1)}, bf16[2048,1024]{1,0:T(8,128)(2,1)}, u32[]{:S(2)}) copy-start(bf16[2048,1024]{1,0:T(8,128)(2,1)} %get-tuple-element.4) | copy-start | bytes 12582916

commit v4 on v3

--- a/solution.py
+++ b/solution.py
@@ -119,8 +119,12 @@
     cx = cx_ref[...]
     cy = cy_ref[...]
     cz = cz_ref[...]
-    left = left_ref[...].astype(jnp.float32)
-    right = right_ref[...].astype(jnp.float32)
+    half = NV1 // 2
+    blank = jnp.zeros((rows // NV1, half, PLANE), jnp.float32)
+    left = left_ref[...].astype(jnp.float32).reshape(rows // NV1, half, PLANE)
+    right = right_ref[...].astype(jnp.float32).reshape(rows // NV1, half, PLANE)
+    left = jnp.concatenate([left, blank], axis=1).reshape(rows, PLANE)
+    right = jnp.concatenate([blank, right], axis=1).reshape(rows, PLANE)
     after = jnp.concatenate([g[:, PLANE:], right], axis=1)
     before = jnp.concatenate([left, g[:, : lanes - PLANE]], axis=1)
     lane = lax.broadcasted_iota(jnp.int32, (1, lanes), 1)
@@ -158,8 +162,8 @@
         grid=grid,
         in_specs=[
             pl.BlockSpec((block, lanes), row),
-            pl.BlockSpec((block, PLANE), row),
-            pl.BlockSpec((block, PLANE), row),
+            pl.BlockSpec((block // 2, PLANE), row),
+            pl.BlockSpec((block // 2, PLANE), row),
             pl.BlockSpec((block, 1), row),
             pl.BlockSpec((block, 1), row),
             pl.BlockSpec((block, 1), row),
@@ -179,11 +183,16 @@
     speed_x, speed_y, speed_z, weigh, lift = tables(start, local_vel)
     count = lax.axis_size("space")
     ends = count - 1
-    left = lax.ppermute(adjoint[:, width - 1], "space", [(i, i + 1) for i in range(ends)])
-    right = lax.ppermute(adjoint[:, 0], "space", [(i + 1, i) for i in range(ends)])
+    flat = adjoint.reshape(local_vel, width * plane)
+    grouped = flat.reshape(local_vel // NV1, NV1, width * plane)
+    half = NV1 // 2
+    tail = grouped[:, :half, (width - 1) * plane :].reshape(local_vel // 2, plane)
+    head = grouped[:, half:, :plane].reshape(local_vel // 2, plane)
+    left = lax.ppermute(tail, "space", [(i, i + 1) for i in range(ends)])
+    right = lax.ppermute(head, "space", [(i + 1, i) for i in range(ends)])
     fluid = (1 - solid).astype(jnp.float32)
     starred_flat, partial_value = advance(
-        adjoint.reshape(local_vel, width * plane),
+        flat,
         left,
         right,
         speed_x.reshape(local_vel, 1),

time: 155 us -> 151 us (0.974)
  waiting for transfers between devices: 49.6 us -> 34.7 us
  starting transfers between devices: 38.3 us -> 46.3 us
  local copies, waits for them, and re-layouts: 26.3 us -> 28.8 us
    ppermute x2, waiting for transfers between devices: 16.1 us -> 0.01 us  [the longest x1 0.01 us: on_device(): right = lax.ppermute(head, 'space', [(i + 1, i) for i in range(ends)])]
    another operation x0 -> x1, local copies, waits for them, and re-layouts: none -> 7.7 us  [on_device(): grouped = flat.reshape(local_vel // NV1, NV1, width * plane)]
    slice x1 -> x0, local copies, waits for them, and re-layouts: 6.95 us -> none  [on_device(): adjoint[:, 0]]
    ppermute x3, starting transfers between devices: 11.2 us -> 17.6 us  [with_halo(): lax.ppermute(tail, axis, [(i, (i + 1) % count) for i in range(ends)])]
    ppermute x2, starting transfers between devices: 6.52 us -> 11.3 us  [the longest x1 8.54 us: on_device(): left = lax.ppermute(tail, 'space', [(i, i + 1) for i in range(ends)])]
    reshape x0 -> x1, local copies, waits for them, and re-layouts: none -> 2.12 us  [on_device(): head = grouped[:, half:, :plane].reshape(local_vel // 2, plane)]
    ppermute x3, starting transfers between devices: 9.95 us -> 7.94 us  [with_halo(): lax.ppermute(head, axis, [((i + 1) % count, i) for i in range(ends)])]
    unnamed x16 -> x18, local copies, waits for them, and re-layouts: 8.81 us -> 8.45 us
  transfers between devices with their start and end apart: 15 -> 15, of which waited for: 10 -> 8; matrix products, arithmetic and copies ran while one was open for 11% -> 11% of each run, Pallas kernels for 0% -> 0%
where the time goes in v4:
time: 151 us; the launch traced here: 150 us
  starting transfers between devices  46.3 us (31%)
  waiting for transfers between devices  34.7 us (23%)
  local copies, waits for them, and re-layouts  28.8 us (19%)
  Pallas kernels  15.8 us (10%)
  other arithmetic  12.2 us (8%)
  between operations  6.46 us (4%)
  blocking collectives  4.2 us (3%)
    ppermute x7, waiting for transfers between devices, exchange_sum(): lax.ppermute(value, axis, [(i, i ^ step) for i in range(count)])  20.1 us
    ppermute x3, starting transfers between devices, with_halo(): lax.ppermute(tail, axis, [(i, (i + 1) % count) for i in range(ends)])  17.6 us
    pallas_call x1, Pallas kernels, advance(): pl.pallas_call(advance_kernel, grid=grid, in_specs=[pl.BlockSpec((block,...  15.8 us
    ppermute x3, waiting for transfers between devices, with_halo(): lax.ppermute(head, axis, [((i + 1) % count, i) for i in range(ends)])  14.6 us
    ppermute x7, starting transfers between devices, exchange_sum(): lax.ppermute(value, axis, [(i, i ^ step) for i in range(count)])  9.48 us
    ppermute x1, starting transfers between devices, on_device(): left = lax.ppermute(tail, 'space', [(i, i + 1) for i in range(ends)])  8.54 us
    unnamed x18, local copies, waits for them, and re-layouts  8.45 us
    ppermute x3, starting transfers between devices, with_halo(): lax.ppermute(head, axis, [((i + 1) % count, i) for i in range(ends)])  7.94 us
  transfers between devices with their start and end apart: 15, of which 8 were waited for; matrix products, arithmetic and copies ran while one was open for 11% of the time, Pallas kernels for 0%

profile of v4, /device:TPU:126, one launch (start us, length us, event | category | flops | bytes accessed | tf_op | source)
XLA Modules:
  0.0 149.6 jit_solution(840264181959466025)
XLA Ops:
  0.6 7.7 %reshape_reshape.3 = bf16[128,16,1024]{2,1,0:T(8,128)(2,1)} reshape(bf16[2048,4,256]{2,1,0:T(4,128)(2,1)} %param.4) | data formatting | bytes 8388608 | tf_op jit(solution)/shard_map/reshape;reshape | solution.py:187
  8.3 2.1 %slice_bitcast_fusion = (bf16[1024,256]{1,0:T(8,128)(2,1)}, bf16[1024,256]{1,0:T(8,128)(2,1)S(1)}) fusion(bf16[128,16,1024]{2,1,0:T(8,128)(2,1)} %reshape_reshape.3), kind=kLoop, calls=%fused_computation.13 | loop fusion | bytes 2097152 | tf_op jit(solution)/shard_map/reshape | solution.py:190
  10.5 2.7 %collective-permute-start.1 = (bf16[1024,256]{1,0:T(8,128)(2,1)}, bf16[1024,256]{1,0:T(8,128)(2,1)S(1)}, u32[]{:S(2)}, u32[]{:S(2)}) collective-permute-start(bf16[1024,256]{1,0:T(8,128)(2,1)} %get-tuple-element.12), channel_id=1, source_target_pairs={{2,0},{4,2},{6,4},{8,6},{10,8},{12,10},{14,12},{16,14},{18,16},{20... | collective-permute-start | bytes 1572872 | tf_op jit(solution)/shard_map/ppermute | solution.py:192
  13.2 8.5 %collective-permute-start = (bf16[1024,256]{1,0:T(8,128)(2,1)S(1)}, bf16[1024,256]{1,0:T(8,128)(2,1)S(1)}, u32[]{:S(2)}, u32[]{:S(2)}) collective-permute-start(bf16[1024,256]{1,0:T(8,128)(2,1)S(1)} %get-tuple-element.13), channel_id=1, source_target_pairs={{0,2},{2,4},{4,6},{6,8},{8,10},{10,12},{12,14},{14,16},{16,18},{18... | collective-permute-start | bytes 1572872 | tf_op jit(solution)/shard_map/ppermute | solution.py:191
  21.7 0.6 fusion.46
  23.5 0.4 copy.8
  23.9 1.1 broadcast_multiply_fusion.2.cx_ref
  24.9 0.4 copy.10
  25.3 1.1 broadcast_multiply_fusion.1.cy_ref
  26.6 1.3 divide_convert_fusion.weigh_ref
  27.9 0.6 copy.17
  28.5 0.6 copy.18
  29.2 0.4 copy.12
  29.5 5.2 %copy.16 = bf16[256,8,4,256]{3,1,2,0:T(8,128)(2,1)} copy(bf16[256,8,4,256]{3,2,1,0:T(4,128)(2,1)} %bitcast.27) | data formatting | bytes 8388608
  34.8 1.0 broadcast_multiply_fusion.cz_ref
  35.8 0.8 copy-done.1
  36.9 15.8 %shard_map.59 = (bf16[2048,1024]{1,0:T(8,128)(2,1)}, f32[13,1024]{1,0:T(8,128)}) custom-call(bf16[2048,1024]{1,0:T(8,128)(2,1)} %bitcast.26, bf16[1024,256]{1,0:T(8,128)(2,1)} %copy-done.2, bf16[1024,256]{1,0:T(8,128)(2,1)} %copy-done.1, f32[2048,1]{1,0:T(8,128)} %broadcast_multiply_fusion.2.cx_ref, f32[2048,1]{1,0:T(8,128)} %broadcast_multiply_fusion.1.cy_ref, ...), custom_call_target="tpu_custom_call" | custom-call | tf_op jit(solution)/shard_map/pallas_call | solution.py:160
  52.7 4.2 %psum.7 = f32[13,1024]{1,0:T(8,128)S(1)} all-reduce(f32[13,1024]{1,0:T(8,128)} %get-tuple-element.5), channel_id=1, replica_groups=mesh['space'=128,'vel'=2] {'vel'}, use_global_device_ids=true, to_apply=%region_1.2 | all-reduce | flops 13312 | bytes 106496 | tf_op jit(solution)/shard_map/psum | solution.py:205
  56.9 0.6 fusion.83
  57.8 6.3 %collective-permute-start.2 = (bf16[13,1,256]{2,1,0:T(2,128)(2,1)S(1)}, bf16[13,1,256]{2,1,0:T(2,128)(2,1)S(1)}, u32[]{:S(2)}, u32[]{:S(2)}) collective-permute-start(bf16[13,1,256]{2,1,0:T(2,128)(2,1)S(1)} %get-tuple-element.18), channel_id=1, source_target_pairs={{0,2},{2,4},{4,6},{6,8},{8,10},{10,12},{12,14},{14,16},{16,18},{18... | collective-permute-start | bytes 19976 | tf_op jit(solution)/shard_map/ppermute | solution.py:29
  64.2 1.9 %collective-permute-start.3 = (bf16[13,1,256]{2,1,0:T(2,128)(2,1)S(1)}, bf16[13,1,256]{2,1,0:T(2,128)(2,1)S(1)}, u32[]{:S(2)}, u32[]{:S(2)}) collective-permute-start(bf16[13,1,256]{2,1,0:T(2,128)(2,1)S(1)} %get-tuple-element.19), channel_id=1, source_target_pairs={{2,0},{4,2},{6,4},{8,6},{10,8},{12,10},{14,12},{16,14},{18,16},{20... | collective-permute-start | bytes 19976 | tf_op jit(solution)/shard_map/ppermute | solution.py:31
  66.2 0.3 fusion.2
  66.5 0.2 reshape.477
  68.0 1.4 collective-permute-start.9
  69.4 3.7 %collective-permute-done.9 = f32[]{:T(128)} collective-permute-done((f32[]{:T(128)}, f32[]{:T(128)}, u32[]{:S(2)}, u32[]{:S(2)}) %collective-permute-start.9) | collective-permute-done | bytes 36 | tf_op jit(solution)/shard_map/ppermute | solution.py:44
  73.8 1.4 collective-permute-start.10
  75.2 2.2 %collective-permute-done.10 = f32[]{:T(128)} collective-permute-done((f32[]{:T(128)}, f32[]{:T(128)}, u32[]{:S(2)}, u32[]{:S(2)}) %collective-permute-start.10) | collective-permute-done | bytes 36 | tf_op jit(solution)/shard_map/ppermute | solution.py:44
  78.1 1.4 collective-permute-start.11
  79.5 3.7 %collective-permute-done.11 = f32[]{:T(128)} collective-permute-done((f32[]{:T(128)}, f32[]{:T(128)}, u32[]{:S(2)}, u32[]{:S(2)}) %collective-permute-start.11) | collective-permute-done | bytes 36 | tf_op jit(solution)/shard_map/ppermute | solution.py:44
  83.9 1.4 collective-permute-start.12
  85.3 2.2 %collective-permute-done.12 = f32[]{:T(128)} collective-permute-done((f32[]{:T(128)}, f32[]{:T(128)}, u32[]{:S(2)}, u32[]{:S(2)}) %collective-permute-start.12) | collective-permute-done | bytes 36 | tf_op jit(solution)/shard_map/ppermute | solution.py:44
  88.2 1.4 collective-permute-start.13
  89.6 3.1 %collective-permute-done.13 = f32[]{:T(128)} collective-permute-done((f32[]{:T(128)}, f32[]{:T(128)}, u32[]{:S(2)}, u32[]{:S(2)}) %collective-permute-start.13) | collective-permute-done | bytes 36 | tf_op jit(solution)/shard_map/ppermute | solution.py:44
  93.4 2.4 %collective-permute-start.14 = (f32[]{:T(128)}, f32[]{:T(128)}, u32[]{:S(2)}, u32[]{:S(2)}) collective-permute-start(f32[]{:T(128)} %add.723), channel_id=1, source_target_pairs={{0,128},{2,130},{4,132},{6,134},{8,136},{10,138},{12,140},{14,142}... | collective-permute-start | bytes 20 | tf_op jit(solution)/shard_map/ppermute | solution.py:44
  95.8 5.1 %collective-permute-done.14 = f32[]{:T(128)} collective-permute-done((f32[]{:T(128)}, f32[]{:T(128)}, u32[]{:S(2)}, u32[]{:S(2)}) %collective-permute-start.14) | collective-permute-done | bytes 36 | tf_op jit(solution)/shard_map/ppermute | solution.py:44
  101.8 9.4 %collective-permute-start.4 = (bf16[13,1,256]{2,1,0:T(2,128)(2,1)S(1)}, bf16[13,1,256]{2,1,0:T(2,128)(2,1)S(1)}, u32[]{:S(2)}, u32[]{:S(2)}) collective-permute-start(bf16[13,1,256]{2,1,0:T(2,128)(2,1)S(1)} %get-tuple-element.16), channel_id=1, source_target_pairs={{0,2},{2,4},{4,6},{6,8},{8,10},{10,12},{12,14},{14,16},{16,18},{18... | collective-permute-start | bytes 19976 | tf_op jit(solution)/shard_map/ppermute | solution.py:29
  111.2 1.9 %collective-permute-start.5 = (bf16[13,1,256]{2,1,0:T(2,128)(2,1)S(1)}, bf16[13,1,256]{2,1,0:T(2,128)(2,1)S(1)}, u32[]{:S(2)}, u32[]{:S(2)}) collective-permute-start(bf16[13,1,256]{2,1,0:T(2,128)(2,1)S(1)} %get-tuple-element.17), channel_id=1, source_target_pairs={{2,0},{4,2},{6,4},{8,6},{10,8},{12,10},{14,12},{16,14},{18,16},{20... | collective-permute-start | bytes 19976 | tf_op jit(solution)/shard_map/ppermute | solution.py:31
  113.3 0.3 fusion.5
  113.8 8.4 %collective-permute-done.5 = bf16[13,1,256]{2,1,0:T(2,128)(2,1)S(1)} collective-permute-done((bf16[13,1,256]{2,1,0:T(2,128)(2,1)S(1)}, bf16[13,1,256]{2,1,0:T(2,128)(2,1)S(1)}, u32[]{:S(2)}, u32[]{:S(2)}) %collective-permute-start.5) | collective-permute-done | bytes 6688 | tf_op jit(solution)/shard_map/ppermute | solution.py:31
  122.3 1.9 %collective-permute-start.6 = (bf16[13,1,256]{2,1,0:T(2,128)(2,1)S(1)}, bf16[13,1,256]{2,1,0:T(2,128)(2,1)S(1)}, u32[]{:S(2)}, u32[]{:S(2)}) collective-permute-start(bf16[13,1,256]{2,1,0:T(2,128)(2,1)S(1)} %get-tuple-element.14), channel_id=1, source_target_pairs={{0,2},{2,4},{4,6},{6,8},{8,10},{10,12},{12,14},{14,16},{16,18},{18... | collective-permute-start | bytes 19976 | tf_op jit(solution)/shard_map/ppermute | solution.py:29
  124.2 4.1 %collective-permute-start.7 = (bf16[13,1,256]{2,1,0:T(2,128)(2,1)S(1)}, bf16[13,1,256]{2,1,0:T(2,128)(2,1)S(1)}, u32[]{:S(2)}, u32[]{:S(2)}) collective-permute-start(bf16[13,1,256]{2,1,0:T(2,128)(2,1)S(1)} %get-tuple-element.15), channel_id=1, source_target_pairs={{2,0},{4,2},{6,4},{8,6},{10,8},{12,10},{14,12},{16,14},{18,16},{20... | collective-permute-start | bytes 19976 | tf_op jit(solution)/shard_map/ppermute | solution.py:31
  128.5 0.3 fusion.8
  129.1 6.2 %collective-permute-done.7 = bf16[13,1,256]{2,1,0:T(2,128)(2,1)S(1)} collective-permute-done((bf16[13,1,256]{2,1,0:T(2,128)(2,1)S(1)}, bf16[13,1,256]{2,1,0:T(2,128)(2,1)S(1)}, u32[]{:S(2)}, u32[]{:S(2)}) %collective-permute-start.7) | collective-permute-done | bytes 6688 | tf_op jit(solution)/shard_map/ppermute | solution.py:31
  135.3 0.7 broadcast_multiply_fusion.4
  136.0 1.3 fusion.9
  137.3 0.9 copy-done
  138.2 3.6 %multiply_convert_fusion = bf16[2048,1024]{1,0:T(8,128)(2,1)} fusion(f32[2048,1024]{1,0:T(8,128)S(1)} %fusion.9, bf16[2048,1024]{1,0:T(8,128)(2,1)S(1)} %copy-done, f32[1024]{0:T(1024)S(1)} %bitcast.33), kind=kLoop, calls=%fused_computation | loop fusion | flops 8388608 | bytes 16781312 | tf_op jit(solution)/shard_map/convert_element_type | solution.py:216
  141.8 7.8 %reshape.483 = bf16[2048,4,256]{2,1,0:T(4,128)(2,1)} reshape(bf16[2048,1024]{1,0:T(8,128)(2,1)} %multiply_convert_fusion) | data formatting | bytes 8388608 | tf_op jit(solution)/shard_map/reshape | solution.py:217
  (52 shorter events, 3.1 us)
Async XLA Ops:
  8.3 18.0 %copy-start.3 = (f32[4,256]{1,0:T(4,128)S(1)}, f32[4,256]{1,0:T(4,128)}, u32[]{:S(2)}) copy-start(f32[4,256]{1,0:T(4,128)} %param.5) | copy-start | bytes 12292
  8.3 18.0 %copy-start.4 = (s32[4,256]{1,0:T(4,128)S(1)}, s32[4,256]{1,0:T(4,128)}, u32[]{:S(2)}) copy-start(s32[4,256]{1,0:T(4,128)} %param.6) | copy-start | bytes 12292
  8.3 18.0 %copy-start.5 = (s32[4,256]{1,0:T(4,128)S(1)}, s32[4,256]{1,0:T(4,128)}, u32[]{:S(2)}) copy-start(s32[4,256]{1,0:T(4,128)} %param.7) | copy-start | bytes 12292
  10.5 25.4 %collective-permute-start.1 = (bf16[1024,256]{1,0:T(8,128)(2,1)}, bf16[1024,256]{1,0:T(8,128)(2,1)S(1)}, u32[]{:S(2)}, u32[]{:S(2)}) collective-permute-start(bf16[1024,256]{1,0:T(8,128)(2,1)} %get-tuple-element.12), channel_id=1, source_target_pairs={{2,0},{4,2},{6,4},{8,6},{10,8},{12,10},{14,12},{16,14},{18,16},{20... | collective-permute-start | bytes 1572872 | tf_op jit(solution)/shard_map/ppermute | solution.py:192
  13.2 22.6 %collective-permute-start = (bf16[1024,256]{1,0:T(8,128)(2,1)S(1)}, bf16[1024,256]{1,0:T(8,128)(2,1)S(1)}, u32[]{:S(2)}, u32[]{:S(2)}) collective-permute-start(bf16[1024,256]{1,0:T(8,128)(2,1)S(1)} %get-tuple-element.13), channel_id=1, source_target_pairs={{0,2},{2,4},{4,6},{6,8},{8,10},{10,12},{12,14},{14,16},{16,18},{18... | collective-permute-start | bytes 1572872 | tf_op jit(solution)/shard_map/ppermute | solution.py:191
  35.8 0.9 copy-start.1
  35.8 1.1 copy-start.2
  57.7 9.0 %collective-permute-start.8 = (f32[]{:T(128)}, f32[]{:T(128)}, u32[]{:S(2)}, u32[]{:S(2)}) collective-permute-start(f32[]{:T(128)} %fusion.83), channel_id=1, source_target_pairs={{0,2},{2,0},{4,6},{6,4},{8,10},{10,8},{12,14},{14,12},{16,18},{18,... | collective-permute-start | bytes 20 | tf_op jit(solution)/shard_map/ppermute | solution.py:44
  57.8 43.8 %collective-permute-start.2 = (bf16[13,1,256]{2,1,0:T(2,128)(2,1)S(1)}, bf16[13,1,256]{2,1,0:T(2,128)(2,1)S(1)}, u32[]{:S(2)}, u32[]{:S(2)}) collective-permute-start(bf16[13,1,256]{2,1,0:T(2,128)(2,1)S(1)} %get-tuple-element.18), channel_id=1, source_target_pairs={{0,2},{2,4},{4,6},{6,8},{8,10},{10,12},{12,14},{14,16},{16,18},{18... | collective-permute-start | bytes 19976 | tf_op jit(solution)/shard_map/ppermute | solution.py:29
  64.2 37.5 %collective-permute-start.3 = (bf16[13,1,256]{2,1,0:T(2,128)(2,1)S(1)}, bf16[13,1,256]{2,1,0:T(2,128)(2,1)S(1)}, u32[]{:S(2)}, u32[]{:S(2)}) collective-permute-start(bf16[13,1,256]{2,1,0:T(2,128)(2,1)S(1)} %get-tuple-element.19), channel_id=1, source_target_pairs={{2,0},{4,2},{6,4},{8,6},{10,8},{12,10},{14,12},{16,14},{18,16},{20... | collective-permute-start | bytes 19976 | tf_op jit(solution)/shard_map/ppermute | solution.py:31
  68.0 5.1 %collective-permute-start.9 = (f32[]{:T(128)}, f32[]{:T(128)}, u32[]{:S(2)}, u32[]{:S(2)}) collective-permute-start(f32[]{:T(128)} %add.718), channel_id=1, source_target_pairs={{0,4},{2,6},{4,0},{6,2},{8,12},{10,14},{12,8},{14,10},{16,20},{18,... | collective-permute-start | bytes 20 | tf_op jit(solution)/shard_map/ppermute | solution.py:44
  73.8 3.6 %collective-permute-start.10 = (f32[]{:T(128)}, f32[]{:T(128)}, u32[]{:S(2)}, u32[]{:S(2)}) collective-permute-start(f32[]{:T(128)} %add.719), channel_id=1, source_target_pairs={{0,8},{2,10},{4,12},{6,14},{8,0},{10,2},{12,4},{14,6},{16,24},{18,... | collective-permute-start | bytes 20 | tf_op jit(solution)/shard_map/ppermute | solution.py:44
  78.1 5.1 %collective-permute-start.11 = (f32[]{:T(128)}, f32[]{:T(128)}, u32[]{:S(2)}, u32[]{:S(2)}) collective-permute-start(f32[]{:T(128)} %add.720), channel_id=1, source_target_pairs={{0,16},{2,18},{4,20},{6,22},{8,24},{10,26},{12,28},{14,30},{16,0},... | collective-permute-start | bytes 20 | tf_op jit(solution)/shard_map/ppermute | solution.py:44
  83.9 3.6 %collective-permute-start.12 = (f32[]{:T(128)}, f32[]{:T(128)}, u32[]{:S(2)}, u32[]{:S(2)}) collective-permute-start(f32[]{:T(128)} %add.721), channel_id=1, source_target_pairs={{0,32},{2,34},{4,36},{6,38},{8,40},{10,42},{12,44},{14,46},{16,48}... | collective-permute-start | bytes 20 | tf_op jit(solution)/shard_map/ppermute | solution.py:44
  88.2 4.5 %collective-permute-start.13 = (f32[]{:T(128)}, f32[]{:T(128)}, u32[]{:S(2)}, u32[]{:S(2)}) collective-permute-start(f32[]{:T(128)} %add.722), channel_id=1, source_target_pairs={{0,64},{2,66},{4,68},{6,70},{8,72},{10,74},{12,76},{14,78},{16,80}... | collective-permute-start | bytes 20 | tf_op jit(solution)/shard_map/ppermute | solution.py:44
  93.4 7.5 %collective-permute-start.14 = (f32[]{:T(128)}, f32[]{:T(128)}, u32[]{:S(2)}, u32[]{:S(2)}) collective-permute-start(f32[]{:T(128)} %add.723), channel_id=1, source_target_pairs={{0,128},{2,130},{4,132},{6,134},{8,136},{10,138},{12,140},{14,142}... | collective-permute-start | bytes 20 | tf_op jit(solution)/shard_map/ppermute | solution.py:44
  101.8 12.0 %collective-permute-start.4 = (bf16[13,1,256]{2,1,0:T(2,128)(2,1)S(1)}, bf16[13,1,256]{2,1,0:T(2,128)(2,1)S(1)}, u32[]{:S(2)}, u32[]{:S(2)}) collective-permute-start(bf16[13,1,256]{2,1,0:T(2,128)(2,1)S(1)} %get-tuple-element.16), channel_id=1, source_target_pairs={{0,2},{2,4},{4,6},{6,8},{8,10},{10,12},{12,14},{14,16},{16,18},{18... | collective-permute-start | bytes 19976 | tf_op jit(solution)/shard_map/ppermute | solution.py:29
  111.2 11.0 %collective-permute-start.5 = (bf16[13,1,256]{2,1,0:T(2,128)(2,1)S(1)}, bf16[13,1,256]{2,1,0:T(2,128)(2,1)S(1)}, u32[]{:S(2)}, u32[]{:S(2)}) collective-permute-start(bf16[13,1,256]{2,1,0:T(2,128)(2,1)S(1)} %get-tuple-element.17), channel_id=1, source_target_pairs={{2,0},{4,2},{6,4},{8,6},{10,8},{12,10},{14,12},{16,14},{18,16},{20... | collective-permute-start | bytes 19976 | tf_op jit(solution)/shard_map/ppermute | solution.py:31
  122.3 6.8 %collective-permute-start.6 = (bf16[13,1,256]{2,1,0:T(2,128)(2,1)S(1)}, bf16[13,1,256]{2,1,0:T(2,128)(2,1)S(1)}, u32[]{:S(2)}, u32[]{:S(2)}) collective-permute-start(bf16[13,1,256]{2,1,0:T(2,128)(2,1)S(1)} %get-tuple-element.14), channel_id=1, source_target_pairs={{0,2},{2,4},{4,6},{6,8},{8,10},{10,12},{12,14},{14,16},{16,18},{18... | collective-permute-start | bytes 19976 | tf_op jit(solution)/shard_map/ppermute | solution.py:29
  124.2 11.0 %collective-permute-start.7 = (bf16[13,1,256]{2,1,0:T(2,128)(2,1)S(1)}, bf16[13,1,256]{2,1,0:T(2,128)(2,1)S(1)}, u32[]{:S(2)}, u32[]{:S(2)}) collective-permute-start(bf16[13,1,256]{2,1,0:T(2,128)(2,1)S(1)} %get-tuple-element.15), channel_id=1, source_target_pairs={{2,0},{4,2},{6,4},{8,6},{10,8},{12,10},{14,12},{16,14},{18,16},{20... | collective-permute-start | bytes 19976 | tf_op jit(solution)/shard_map/ppermute | solution.py:31
  136.0 2.2 %copy-start = (bf16[2048,1024]{1,0:T(8,128)(2,1)S(1)}, bf16[2048,1024]{1,0:T(8,128)(2,1)}, u32[]{:S(2)}) copy-start(bf16[2048,1024]{1,0:T(8,128)(2,1)} %get-tuple-element.4) | copy-start | bytes 12582916

commit v5 on v4

--- a/solution.py
+++ b/solution.py
@@ -105,10 +105,25 @@
     return summed.reshape(count, rows, plane)
 
 
-def sweep_each(fields, source, inverse):
-    widened = with_halo(fields.astype(jnp.bfloat16), (("space", 1),), 1).astype(fields.dtype)
-    beside_all = widened[:, 2:] + widened[:, :-2] + plane_around(fields)
-    return inverse * (source + beside_all)
+def sweep_all(moments, fluid, collision, kappa):
+    count = lax.axis_size("space")
+    ends = count - 1
+    width = moments.shape[1]
+    depth = SWEEPS
+    pack = jnp.concatenate([moments, jnp.stack([fluid, collision, kappa])], axis=0)
+    before = lax.ppermute(pack[:, width - depth :], "space", [(i, i + 1) for i in range(ends)])
+    after = lax.ppermute(pack[:, :depth], "space", [(i + 1, i) for i in range(ends)])
+    wide = jnp.concatenate([before, pack, after], axis=1)
+    total = wide.shape[1]
+    grown = wide[:NM]
+    inverse = wide[NM] / (wide[NM + 1] + wide[NM + 2] + 6.0)
+    source = wide[NM + 1][None] * grown
+    fields = grown * wide[NM][None]
+    for sweep in range(SWEEPS):
+        lo, hi = sweep + 1, total - 1 - sweep
+        beside_all = fields[:, 2:] + fields[:, :-2] + plane_around(fields[:, 1:-1])
+        fields = inverse[None, lo:hi] * (source[:, lo:hi] + beside_all)
+    return fields
 
 
 def advance_kernel(adj_ref, left_ref, right_ref, cx_ref, cy_ref, cz_ref, coll_ref, fluid_ref, weigh_ref,
@@ -183,7 +198,7 @@
     speed_x, speed_y, speed_z, weigh, lift = tables(start, local_vel)
     count = lax.axis_size("space")
     ends = count - 1
-    flat = adjoint.reshape(local_vel, width * plane)
+    flat = lax.optimization_barrier(adjoint.reshape(local_vel, width * plane))
     grouped = flat.reshape(local_vel // NV1, NV1, width * plane)
     half = NV1 // 2
     tail = grouped[:, :half, (width - 1) * plane :].reshape(local_vel // 2, plane)
@@ -206,11 +221,7 @@
     cells_all = width * lax.axis_size("space") * plane
     squares = exchange_sum(jnp.sum(moments[0] * moments[0]), "space")
     scale = lax.rsqrt(squares / cells_all + 1e-06)
-    inverse = fluid / (collision + wall_level(codes) + 6.0)
-    source = collision[None] * moments
-    fields = moments * fluid[None]
-    for sweep in range(SWEEPS):
-        fields = sweep_each(fields, source, inverse[None])
+    fields = sweep_all(moments, fluid, collision, wall_level(codes))
     delta = ((fields - moments) * scale).astype(jnp.bfloat16).reshape(NM, width * plane)
     added = jnp.dot(lift, delta, preferred_element_type=jnp.float32)
     corrected = (fluid.reshape(1, width * plane) * (starred_flat + added)).astype(jnp.bfloat16)

time: 151 us -> 123 us (0.81)
  the two profiles are of different devices: /device:TPU:126 before, /device:TPU:10 now
where the time goes in v5:
time: 123 us; the launch traced here: 121 us
  starting transfers between devices  49.9 us (41%)
  local copies, waits for them, and re-layouts  19 us (15%)
  Pallas kernels  15.8 us (13%)
  other arithmetic  12.5 us (10%)
  waiting for transfers between devices  11.4 us (9%)
  between operations  6.43 us (5%)
  blocking collectives  4.2 us (3%)
  matrix products  1.27 us (1%)
    ppermute x7, starting transfers between devices, exchange_sum(): lax.ppermute(value, axis, [(i, i ^ step) for i in range(count)])  36.4 us
    pallas_call x1, Pallas kernels, advance(): pl.pallas_call(advance_kernel, grid=grid, in_specs=[pl.BlockSpec((block,...  15.8 us
    unnamed x20, local copies, waits for them, and re-layouts  8.16 us
    reshape x1, local copies, waits for them, and re-layouts, on_device(): return (corrected.reshape(local_vel, width, plane), fields * scale)  7.83 us
    ppermute x7, waiting for transfers between devices, exchange_sum(): lax.ppermute(value, axis, [(i, i ^ step) for i in range(count)])  7.42 us
    ppermute x1, starting transfers between devices, sweep_all(): lax.ppermute(pack[:, :depth], 'space', [(i + 1, i) for i in range(ends)])  5.18 us
    psum x1, blocking collectives, on_device(): moments = lax.psum(partial_value, 'vel').reshape(NM, width, plane)  4.2 us
    convert_element_type x1, other arithmetic, on_device(): (fluid.reshape(1, width * plane) * (starred_flat + added)).astype(jnp.bfl...  3.55 us
  transfers between devices with their start and end apart: 11, of which 9 were waited for; matrix products, arithmetic and copies ran while one was open for 8% of the time, Pallas kernels for 0%

profile of v5, /device:TPU:10, one launch (start us, length us, event | category | flops | bytes accessed | tf_op | source)
XLA Modules:
  0.0 120.5 jit_solution(14739747848678059724)
XLA Ops:
  0.6 3.2 %copy.28 = bf16[256,8,4,256]{3,1,2,0:T(8,128)(2,1)S(1)} copy(bf16[256,8,4,256]{3,2,1,0:T(4,128)(2,1)} %bitcast.54) | data formatting | bytes 8388608
  3.9 2.0 %copy-done = bf16[256,8,4,256]{3,1,2,0:T(8,128)(2,1)} copy-done((bf16[256,8,4,256]{3,1,2,0:T(8,128)(2,1)}, bf16[256,8,4,256]{3,1,2,0:T(8,128)(2,1)S(1)}, u32[]{:S(2)}) %copy-start) | copy-done | bytes 4194328
  6.0 2.4 %collective-permute-start.1 = (bf16[1024,256]{1,0:T(8,128)(2,1)S(1)}, bf16[1024,256]{1,0:T(8,128)(2,1)S(1)}, u32[]{:S(2)}, u32[]{:S(2)}) collective-permute-start(bf16[1024,256]{1,0:T(8,128)(2,1)S(1)} %get-tuple-element.10), channel_id=1, source_target_pairs={{2,0},{4,2},{6,4},{8,6},{10,8},{12,10},{14,12},{16,14},{18,16},{20... | collective-permute-start | bytes 1572872 | tf_op jit(solution)/shard_map/ppermute | solution.py:207
  8.4 3.4 %collective-permute-start = (bf16[1024,256]{1,0:T(8,128)(2,1)S(1)}, bf16[1024,256]{1,0:T(8,128)(2,1)S(1)}, u32[]{:S(2)}, u32[]{:S(2)}) collective-permute-start(bf16[1024,256]{1,0:T(8,128)(2,1)S(1)} %get-tuple-element.11), channel_id=1, source_target_pairs={{0,2},{2,4},{4,6},{6,8},{8,10},{10,12},{12,14},{14,16},{16,18},{18... | collective-permute-start | bytes 1572872 | tf_op jit(solution)/shard_map/ppermute | solution.py:206
  11.8 0.6 fusion.49
  13.6 0.4 copy.18
  14.0 1.1 broadcast_multiply_fusion.2.cx_ref
  15.1 0.4 copy.20
  15.4 1.1 broadcast_multiply_fusion.1.cy_ref
  16.7 1.3 %divide_convert_fusion.weigh_ref = bf16[13,2048]{1,0:T(8,128)(2,1)} fusion(f32[13,2048]{1,0:T(8,128)S(1)} %stack.8, f32[]{:T(128)} %fusion.49, f32[2048]{0:T(1024)S(1)} %get-tuple-element.26), kind=kLoop, calls=%fused_computation.33 | loop fusion | flops 79872 | bytes 167940 | tf_op jit(solution)/shard_map/convert_element_type | solution.py:82
  18.0 0.6 copy.29
  18.6 0.6 copy.30
  19.2 0.4 copy.22
  19.6 1.0 broadcast_multiply_fusion.cz_ref
  20.6 0.9 collective-permute-done.1.right_ref
  21.5 3.1 %collective-permute-done.left_ref = bf16[1024,256]{1,0:T(8,128)(2,1)S(1)} collective-permute-done((bf16[1024,256]{1,0:T(8,128)(2,1)S(1)}, bf16[1024,256]{1,0:T(8,128)(2,1)S(1)}, u32[]{:S(2)}, u32[]{:S(2)}) %collective-permute-start) | collective-permute-done | bytes 524320 | tf_op jit(solution)/shard_map/ppermute | solution.py:206
  24.6 0.8 copy-done.3
  25.4 15.8 %shard_map.59 = (bf16[2048,1024]{1,0:T(8,128)(2,1)}, f32[13,1024]{1,0:T(8,128)}) custom-call(bf16[2048,1024]{1,0:T(8,128)(2,1)} %bitcast.53, bf16[1024,256]{1,0:T(8,128)(2,1)} %copy-done.3, bf16[1024,256]{1,0:T(8,128)(2,1)} %copy-done.2, f32[2048,1]{1,0:T(8,128)} %broadcast_multiply_fusion.2.cx_ref, f32[2048,1]{1,0:T(8,128)} %broadcast_multiply_fusion.1.cy_ref, ...), custom_call_target="tpu_custom_call" | custom-call | tf_op jit(solution)/shard_map/pallas_call | solution.py:175
  41.2 4.2 %psum.7 = f32[13,1024]{1,0:T(8,128)S(1)} all-reduce(f32[13,1024]{1,0:T(8,128)} %get-tuple-element.5), channel_id=1, replica_groups=mesh['space'=128,'vel'=2] {'vel'}, use_global_device_ids=true, to_apply=%region_1.2 | all-reduce | flops 13312 | bytes 106496 | tf_op jit(solution)/shard_map/psum | solution.py:220
  45.5 2.5 %collective-permute-start.2 = (f32[16,3,256]{2,1,0:T(4,128)S(1)}, f32[16,3,256]{2,1,0:T(4,128)S(1)}, u32[]{:S(2)}, u32[]{:S(2)}) collective-permute-start(f32[16,3,256]{2,1,0:T(4,128)S(1)} %get-tuple-element.16), channel_id=1, source_target_pairs={{0,2},{2,4},{4,6},{6,8},{8,10},{10,12},{12,14},{14,16},{16,18},{18... | collective-permute-start | bytes 147464 | tf_op jit(solution)/shard_map/ppermute | solution.py:114
  48.0 5.2 %collective-permute-start.3 = (f32[16,3,256]{2,1,0:T(4,128)S(1)}, f32[16,3,256]{2,1,0:T(4,128)S(1)}, u32[]{:S(2)}, u32[]{:S(2)}) collective-permute-start(f32[16,3,256]{2,1,0:T(4,128)S(1)} %get-tuple-element.17), channel_id=1, source_target_pairs={{2,0},{4,2},{6,4},{8,6},{10,8},{12,10},{14,12},{16,14},{18,16},{20... | collective-permute-start | bytes 147464 | tf_op jit(solution)/shard_map/ppermute | solution.py:115
  53.2 0.6 fusion.86
  53.8 4.1 %collective-permute-start.4 = (f32[]{:T(128)}, f32[]{:T(128)}, u32[]{:S(2)}, u32[]{:S(2)}) collective-permute-start(f32[]{:T(128)} %fusion.86), channel_id=1, source_target_pairs={{0,2},{2,0},{4,6},{6,4},{8,10},{10,8},{12,14},{14,12},{16,18},{18,... | collective-permute-start | bytes 20 | tf_op jit(solution)/shard_map/ppermute | solution.py:44
  57.9 1.6 %collective-permute-done.4 = f32[]{:T(128)} collective-permute-done((f32[]{:T(128)}, f32[]{:T(128)}, u32[]{:S(2)}, u32[]{:S(2)}) %collective-permute-start.4) | collective-permute-done | bytes 36 | tf_op jit(solution)/shard_map/ppermute | solution.py:44
  60.8 2.4 %collective-permute-start.5 = (f32[]{:T(128)}, f32[]{:T(128)}, u32[]{:S(2)}, u32[]{:S(2)}) collective-permute-start(f32[]{:T(128)} %add.718), channel_id=1, source_target_pairs={{0,4},{2,6},{4,0},{6,2},{8,12},{10,14},{12,8},{14,10},{16,20},{18,... | collective-permute-start | bytes 20 | tf_op jit(solution)/shard_map/ppermute | solution.py:44
  63.2 2.7 %collective-permute-done.5 = f32[]{:T(128)} collective-permute-done((f32[]{:T(128)}, f32[]{:T(128)}, u32[]{:S(2)}, u32[]{:S(2)}) %collective-permute-start.5) | collective-permute-done | bytes 36 | tf_op jit(solution)/shard_map/ppermute | solution.py:44
  66.6 1.4 %collective-permute-start.6 = (f32[]{:T(128)}, f32[]{:T(128)}, u32[]{:S(2)}, u32[]{:S(2)}) collective-permute-start(f32[]{:T(128)} %add.719), channel_id=1, source_target_pairs={{0,8},{2,10},{4,12},{6,14},{8,0},{10,2},{12,4},{14,6},{16,24},{18,... | collective-permute-start | bytes 20 | tf_op jit(solution)/shard_map/ppermute | solution.py:44
  68.0 2.2 %collective-permute-done.6 = f32[]{:T(128)} collective-permute-done((f32[]{:T(128)}, f32[]{:T(128)}, u32[]{:S(2)}, u32[]{:S(2)}) %collective-permute-start.6) | collective-permute-done | bytes 36 | tf_op jit(solution)/shard_map/ppermute | solution.py:44
  70.9 5.4 %collective-permute-start.7 = (f32[]{:T(128)}, f32[]{:T(128)}, u32[]{:S(2)}, u32[]{:S(2)}) collective-permute-start(f32[]{:T(128)} %add.720), channel_id=1, source_target_pairs={{0,16},{2,18},{4,20},{6,22},{8,24},{10,26},{12,28},{14,30},{16,0},... | collective-permute-start | bytes 20 | tf_op jit(solution)/shard_map/ppermute | solution.py:44
  76.3 0.2 collective-permute-done.7
  77.2 7.6 %collective-permute-start.8 = (f32[]{:T(128)}, f32[]{:T(128)}, u32[]{:S(2)}, u32[]{:S(2)}) collective-permute-start(f32[]{:T(128)} %add.721), channel_id=1, source_target_pairs={{0,32},{2,34},{4,36},{6,38},{8,40},{10,42},{12,44},{14,46},{16,48}... | collective-permute-start | bytes 20 | tf_op jit(solution)/shard_map/ppermute | solution.py:44
  84.8 0.2 collective-permute-done.8
  85.7 4.8 %collective-permute-start.9 = (f32[]{:T(128)}, f32[]{:T(128)}, u32[]{:S(2)}, u32[]{:S(2)}) collective-permute-start(f32[]{:T(128)} %add.722), channel_id=1, source_target_pairs={{0,64},{2,66},{4,68},{6,70},{8,72},{10,74},{12,76},{14,78},{16,80}... | collective-permute-start | bytes 20 | tf_op jit(solution)/shard_map/ppermute | solution.py:44
  90.4 0.2 collective-permute-done.9
  91.3 10.8 %collective-permute-start.10 = (f32[]{:T(128)}, f32[]{:T(128)}, u32[]{:S(2)}, u32[]{:S(2)}) collective-permute-start(f32[]{:T(128)} %add.723), channel_id=1, source_target_pairs={{0,128},{2,130},{4,132},{6,134},{8,136},{10,138},{12,140},{14,142}... | collective-permute-start | bytes 20 | tf_op jit(solution)/shard_map/ppermute | solution.py:44
  103.3 0.3 reshape.478
  103.5 0.5 fusion.2
  104.0 0.4 reshape.479
  104.5 0.2 reshape.480
  104.7 0.4 fusion.5
  105.1 0.3 reshape.481
  105.7 0.3 fusion.8
  106.0 0.2 reshape.483
  106.2 0.7 broadcast_multiply_fusion.5
  107.0 1.3 %fusion.15 = f32[2048,1024]{1,0:T(8,128)S(1)} fusion(bf16[13,1024]{1,0:T(8,128)(2,1)S(1)} %bitcast.55, f32[13,2048]{1,0:T(8,128)S(1)} %stack.8, f32[2048]{0:T(1024)S(1)} %get-tuple-element.25), kind=kOutput, calls=%fused_computation.44 | convolution fusion | flops 54579200 | bytes 8529920 | tf_op jit(solution)/shard_map/dot_general | solution.py:226
  108.3 0.9 copy-done.1
  109.2 3.6 %multiply_convert_fusion = bf16[2048,1024]{1,0:T(8,128)(2,1)} fusion(f32[2048,1024]{1,0:T(8,128)S(1)} %fusion.15, bf16[2048,1024]{1,0:T(8,128)(2,1)S(1)} %copy-done.1, f32[1024]{0:T(1024)S(1)} %bitcast.64), kind=kLoop, calls=%fused_computation | loop fusion | flops 8388608 | bytes 16781312 | tf_op jit(solution)/shard_map/convert_element_type | solution.py:227
  112.7 7.8 %reshape.485 = bf16[2048,4,256]{2,1,0:T(4,128)(2,1)} reshape(bf16[2048,1024]{1,0:T(8,128)(2,1)} %multiply_convert_fusion) | data formatting | bytes 8388608 | tf_op jit(solution)/shard_map/reshape | solution.py:228
  (48 shorter events, 2.2 us)
Async XLA Ops:
  0.6 13.0 %copy-start.6 = (s32[4,256]{1,0:T(4,128)S(1)}, s32[4,256]{1,0:T(4,128)}, u32[]{:S(2)}) copy-start(s32[4,256]{1,0:T(4,128)} %param.6) | copy-start | bytes 12292
  3.9 2.0 %copy-start = (bf16[256,8,4,256]{3,1,2,0:T(8,128)(2,1)}, bf16[256,8,4,256]{3,1,2,0:T(8,128)(2,1)S(1)}, u32[]{:S(2)}) copy-start(bf16[256,8,4,256]{3,1,2,0:T(8,128)(2,1)S(1)} %copy.28) | copy-start | bytes 12582916
  5.9 12.1 %copy-start.5 = (s32[4,256]{1,0:T(4,128)S(1)}, s32[4,256]{1,0:T(4,128)}, u32[]{:S(2)}) copy-start(s32[4,256]{1,0:T(4,128)} %param.7) | copy-start | bytes 12292
  5.9 12.1 %copy-start.4 = (f32[4,256]{1,0:T(4,128)S(1)}, f32[4,256]{1,0:T(4,128)}, u32[]{:S(2)}) copy-start(f32[4,256]{1,0:T(4,128)} %param.5) | copy-start | bytes 12292
  6.0 15.6 %collective-permute-start.1 = (bf16[1024,256]{1,0:T(8,128)(2,1)S(1)}, bf16[1024,256]{1,0:T(8,128)(2,1)S(1)}, u32[]{:S(2)}, u32[]{:S(2)}) collective-permute-start(bf16[1024,256]{1,0:T(8,128)(2,1)S(1)} %get-tuple-element.10), channel_id=1, source_target_pairs={{2,0},{4,2},{6,4},{8,6},{10,8},{12,10},{14,12},{16,14},{18,16},{20... | collective-permute-start | bytes 1572872 | tf_op jit(solution)/shard_map/ppermute | solution.py:207
  8.4 16.2 %collective-permute-start = (bf16[1024,256]{1,0:T(8,128)(2,1)S(1)}, bf16[1024,256]{1,0:T(8,128)(2,1)S(1)}, u32[]{:S(2)}, u32[]{:S(2)}) collective-permute-start(bf16[1024,256]{1,0:T(8,128)(2,1)S(1)} %get-tuple-element.11), channel_id=1, source_target_pairs={{0,2},{2,4},{4,6},{6,8},{8,10},{10,12},{12,14},{14,16},{16,18},{18... | collective-permute-start | bytes 1572872 | tf_op jit(solution)/shard_map/ppermute | solution.py:206
  21.5 3.1 %copy-start.2 = (bf16[1024,256]{1,0:T(8,128)(2,1)}, bf16[1024,256]{1,0:T(8,128)(2,1)S(1)}, u32[]{:S(2)}) copy-start(bf16[1024,256]{1,0:T(8,128)(2,1)S(1)} %collective-permute-done.1.right_ref) | copy-start | bytes 1572868
  24.6 0.8 copy-start.3
  45.5 57.6 %collective-permute-start.2 = (f32[16,3,256]{2,1,0:T(4,128)S(1)}, f32[16,3,256]{2,1,0:T(4,128)S(1)}, u32[]{:S(2)}, u32[]{:S(2)}) collective-permute-start(f32[16,3,256]{2,1,0:T(4,128)S(1)} %get-tuple-element.16), channel_id=1, source_target_pairs={{0,2},{2,4},{4,6},{6,8},{8,10},{10,12},{12,14},{14,16},{16,18},{18... | collective-permute-start | bytes 147464 | tf_op jit(solution)/shard_map/ppermute | solution.py:114
  48.0 55.1 %collective-permute-start.3 = (f32[16,3,256]{2,1,0:T(4,128)S(1)}, f32[16,3,256]{2,1,0:T(4,128)S(1)}, u32[]{:S(2)}, u32[]{:S(2)}) collective-permute-start(f32[16,3,256]{2,1,0:T(4,128)S(1)} %get-tuple-element.17), channel_id=1, source_target_pairs={{2,0},{4,2},{6,4},{8,6},{10,8},{12,10},{14,12},{16,14},{18,16},{20... | collective-permute-start | bytes 147464 | tf_op jit(solution)/shard_map/ppermute | solution.py:115
  53.8 5.8 %collective-permute-start.4 = (f32[]{:T(128)}, f32[]{:T(128)}, u32[]{:S(2)}, u32[]{:S(2)}) collective-permute-start(f32[]{:T(128)} %fusion.86), channel_id=1, source_target_pairs={{0,2},{2,0},{4,6},{6,4},{8,10},{10,8},{12,14},{14,12},{16,18},{18,... | collective-permute-start | bytes 20 | tf_op jit(solution)/shard_map/ppermute | solution.py:44
  60.8 5.1 %collective-permute-start.5 = (f32[]{:T(128)}, f32[]{:T(128)}, u32[]{:S(2)}, u32[]{:S(2)}) collective-permute-start(f32[]{:T(128)} %add.718), channel_id=1, source_target_pairs={{0,4},{2,6},{4,0},{6,2},{8,12},{10,14},{12,8},{14,10},{16,20},{18,... | collective-permute-start | bytes 20 | tf_op jit(solution)/shard_map/ppermute | solution.py:44
  66.6 3.6 %collective-permute-start.6 = (f32[]{:T(128)}, f32[]{:T(128)}, u32[]{:S(2)}, u32[]{:S(2)}) collective-permute-start(f32[]{:T(128)} %add.719), channel_id=1, source_target_pairs={{0,8},{2,10},{4,12},{6,14},{8,0},{10,2},{12,4},{14,6},{16,24},{18,... | collective-permute-start | bytes 20 | tf_op jit(solution)/shard_map/ppermute | solution.py:44
  70.9 5.6 %collective-permute-start.7 = (f32[]{:T(128)}, f32[]{:T(128)}, u32[]{:S(2)}, u32[]{:S(2)}) collective-permute-start(f32[]{:T(128)} %add.720), channel_id=1, source_target_pairs={{0,16},{2,18},{4,20},{6,22},{8,24},{10,26},{12,28},{14,30},{16,0},... | collective-permute-start | bytes 20 | tf_op jit(solution)/shard_map/ppermute | solution.py:44
  77.2 7.8 %collective-permute-start.8 = (f32[]{:T(128)}, f32[]{:T(128)}, u32[]{:S(2)}, u32[]{:S(2)}) collective-permute-start(f32[]{:T(128)} %add.721), channel_id=1, source_target_pairs={{0,32},{2,34},{4,36},{6,38},{8,40},{10,42},{12,44},{14,46},{16,48}... | collective-permute-start | bytes 20 | tf_op jit(solution)/shard_map/ppermute | solution.py:44
  85.7 5.0 %collective-permute-start.9 = (f32[]{:T(128)}, f32[]{:T(128)}, u32[]{:S(2)}, u32[]{:S(2)}) collective-permute-start(f32[]{:T(128)} %add.722), channel_id=1, source_target_pairs={{0,64},{2,66},{4,68},{6,70},{8,72},{10,74},{12,76},{14,78},{16,80}... | collective-permute-start | bytes 20 | tf_op jit(solution)/shard_map/ppermute | solution.py:44
  91.3 11.0 %collective-permute-start.10 = (f32[]{:T(128)}, f32[]{:T(128)}, u32[]{:S(2)}, u32[]{:S(2)}) collective-permute-start(f32[]{:T(128)} %add.723), channel_id=1, source_target_pairs={{0,128},{2,130},{4,132},{6,134},{8,136},{10,138},{12,140},{14,142}... | collective-permute-start | bytes 20 | tf_op jit(solution)/shard_map/ppermute | solution.py:44
  107.0 2.2 %copy-start.1 = (bf16[2048,1024]{1,0:T(8,128)(2,1)S(1)}, bf16[2048,1024]{1,0:T(8,128)(2,1)}, u32[]{:S(2)}) copy-start(bf16[2048,1024]{1,0:T(8,128)(2,1)} %get-tuple-element.4) | copy-start | bytes 12582916

commit v6 on v5

--- a/solution.py
+++ b/solution.py
@@ -219,7 +219,8 @@
     )
     moments = lax.psum(partial_value, "vel").reshape(NM, width, plane)
     cells_all = width * lax.axis_size("space") * plane
-    squares = exchange_sum(jnp.sum(moments[0] * moments[0]), "space")
+    own = jnp.where(lax.axis_index("vel") == 0, jnp.sum(moments[0] * moments[0]), 0.0)
+    squares = lax.psum(jnp.zeros((16384,), jnp.float32).at[0].set(own), ("space", "vel"))[0]
     scale = lax.rsqrt(squares / cells_all + 1e-06)
     fields = sweep_all(moments, fluid, collision, wall_level(codes))
     delta = ((fields - moments) * scale).astype(jnp.bfloat16).reshape(NM, width * plane)

time: 123 us -> 342 us (2.78)
  waiting for transfers between devices: 11.4 us -> 254 us
  starting transfers between devices: 49.9 us -> 13.7 us
  between operations: 6.43 us -> 15.7 us
    psum x0 -> x1, waiting for transfers between devices: none -> 250 us  [on_device(): lax.psum(jnp.zeros((16384,), jnp.float32).at[0].set(own), ('space', 'vel'))]
    ppermute x7 -> x0, starting transfers between devices: 36.4 us -> none  [exchange_sum(): lax.ppermute(value, axis, [(i, i ^ step) for i in range(count)])]
    ppermute x7 -> x0, waiting for transfers between devices: 7.42 us -> none  [exchange_sum(): lax.ppermute(value, axis, [(i, i ^ step) for i in range(count)])]
  transfers between devices with their start and end apart: 11 -> 5, of which waited for: 9 -> 3; matrix products, arithmetic and copies ran while one was open for 8% -> 3% of each run, Pallas kernels for 0% -> 0%
where the time goes in v6:
time: 342 us; the launch traced here: 339 us
  waiting for transfers between devices  254 us (74%)
  local copies, waits for them, and re-layouts  20.9 us (6%)
  Pallas kernels  15.8 us (5%)
  between operations  15.7 us (5%)
  starting transfers between devices  13.7 us (4%)
  other arithmetic  12.5 us (4%)
  blocking collectives  4.2 us (1%)
    psum x1, waiting for transfers between devices, on_device(): lax.psum(jnp.zeros((16384,), jnp.float32).at[0].set(own), ('space', 'vel'))  250 us
    pallas_call x1, Pallas kernels, advance(): pl.pallas_call(advance_kernel, grid=grid, in_specs=[pl.BlockSpec((block,...  15.8 us
    unnamed x20, local copies, waits for them, and re-layouts  8.16 us
    reshape x1, local copies, waits for them, and re-layouts, on_device(): return (corrected.reshape(local_vel, width, plane), fields * scale)  7.83 us
  transfers between devices with their start and end apart: 5, of which 3 were waited for; matrix products, arithmetic and copies ran while one was open for 3% of the time, Pallas kernels for 0%

profile of v6, /device:TPU:10, one launch (start us, length us, event | category | flops | bytes accessed | tf_op | source)
XLA Modules:
  0.0 338.5 jit_solution(9195851580057151682)
XLA Ops:
  7.2 3.2 copy.28
  10.5 2.0 copy-done
  12.6 2.4 collective-permute-start.1
  15.0 3.4 %collective-permute-start = (bf16[1024,256]{1,0:T(8,128)(2,1)S(1)}, bf16[1024,256]{1,0:T(8,128)(2,1)S(1)}, u32[]{:S(2)}, u32[]{:S(2)}) collective-permute-start(bf16[1024,256]{1,0:T(8,128)(2,1)S(1)} %get-tuple-element.23), channel_id=1, source_target_pairs={{0,2},{2,4},{4,6},{6,8},{8,10},{10,12},{12,14},{14,16},{16,18},{18... | collective-permute-start | bytes 1572872 | tf_op jit(solution)/shard_map/ppermute | solution.py:206
  18.4 0.6 fusion.49
  19.1 0.2 add_multiply_fusion
  19.3 0.2 subtract_multiply_fusion
  19.4 0.1 fusion.88
  19.6 0.1 broadcast_multiply_fusion.6
  19.7 0.2 multiply_multiply_fusion.1
  19.9 0.2 fusion.72
  20.1 0.1 fusion.67
  20.2 0.4 copy.18
  20.6 1.1 broadcast_multiply_fusion.2.cx_ref
  21.6 0.4 copy.20
  22.0 1.1 broadcast_multiply_fusion.1.cy_ref
  23.1 0.2 stack.8
  23.3 1.3 divide_convert_fusion.weigh_ref
  24.6 0.6 copy.29
  25.2 0.6 copy.30
  25.8 0.4 copy.22
  26.1 1.1 broadcast_multiply_fusion.cz_ref
  27.2 0.9 collective-permute-done.1.right_ref
  28.1 3.1 collective-permute-done.left_ref
  31.2 0.8 copy-done.3
  32.0 15.8 %shard_map.59 = (bf16[2048,1024]{1,0:T(8,128)(2,1)}, f32[13,1024]{1,0:T(8,128)}) custom-call(bf16[2048,1024]{1,0:T(8,128)(2,1)} %bitcast.55, bf16[1024,256]{1,0:T(8,128)(2,1)} %copy-done.3, bf16[1024,256]{1,0:T(8,128)(2,1)} %copy-done.2, f32[2048,1]{1,0:T(8,128)} %broadcast_multiply_fusion.2.cx_ref, f32[2048,1]{1,0:T(8,128)} %broadcast_multiply_fusion.1.cy_ref, ...), custom_call_target="tpu_custom_call" | custom-call | tf_op jit(solution)/shard_map/pallas_call | solution.py:175
  47.8 4.2 %psum.14 = f32[13,1024]{1,0:T(8,128)S(1)} all-reduce(f32[13,1024]{1,0:T(8,128)} %get-tuple-element.17), channel_id=1, replica_groups=mesh['space'=128,'vel'=2] {'vel'}, use_global_device_ids=true, to_apply=%region_1.2 | all-reduce | flops 13312 | bytes 106496 | tf_op jit(solution)/shard_map/psum | solution.py:220
  52.1 2.5 collective-permute-start.2
  54.6 5.4 %collective-permute-start.3 = (f32[16,3,256]{2,1,0:T(4,128)S(1)}, f32[16,3,256]{2,1,0:T(4,128)S(1)}, u32[]{:S(2)}, u32[]{:S(2)}) collective-permute-start(f32[16,3,256]{2,1,0:T(4,128)S(1)} %get-tuple-element.29), channel_id=1, source_target_pairs={{2,0},{4,2},{6,4},{8,6},{10,8},{12,10},{14,12},{16,14},{18,16},{20... | collective-permute-start | bytes 147464 | tf_op jit(solution)/shard_map/ppermute | solution.py:115
  60.0 0.6 fusion.86
  61.2 0.6 scatter.4
  61.9 250.4 %all-reduce.6.cloned.1.call-done = f32[16384]{0:T(1024)} async-done(((f32[16384]{0:T(1024)}), f32[16384]{0:T(1024)}) %all-reduce.6.cloned.1.call-update) | async-done | bytes 65552 | tf_op jit(solution)/shard_map/psum | solution.py:223
  312.3 1.2 slice.181
  314.4 0.3 reshape.509
  314.7 0.5 fusion.2
  315.2 0.4 reshape.510
  315.6 0.2 reshape.511
  315.9 0.4 fusion.5
  316.3 0.3 reshape.512
  316.6 0.1 fusion.11
  316.7 0.2 reshape.513
  316.9 0.3 fusion.8
  317.1 0.2 reshape.514
  317.4 0.7 broadcast_multiply_fusion.5
  318.1 1.3 fusion.15
  319.4 0.9 copy-done.1
  320.3 3.6 %multiply_convert_fusion = bf16[2048,1024]{1,0:T(8,128)(2,1)} fusion(f32[2048,1024]{1,0:T(8,128)S(1)} %fusion.15, bf16[2048,1024]{1,0:T(8,128)(2,1)S(1)} %copy-done.1, f32[1024]{0:T(1024)S(1)} %bitcast.66), kind=kLoop, calls=%fused_computation | loop fusion | flops 8388608 | bytes 16781312 | tf_op jit(solution)/shard_map/convert_element_type | solution.py:228
  323.9 7.8 %reshape.517 = bf16[2048,4,256]{2,1,0:T(4,128)(2,1)} reshape(bf16[2048,1024]{1,0:T(8,128)(2,1)} %multiply_convert_fusion) | data formatting | bytes 8388608 | tf_op jit(solution)/shard_map/reshape | solution.py:229
  (39 shorter events, 0.6 us)
Async XLA Ops:
  7.2 305.1 %all-reduce.6.cloned.1.call-start = ((), (), s32[]{:S(2)}) async-start(), calls=%async_computation | async-start | bytes 131072 | tf_op jit(solution)/shard_map/psum | solution.py:223
  7.2 13.0 %copy-start.6 = (s32[4,256]{1,0:T(4,128)S(1)}, s32[4,256]{1,0:T(4,128)}, u32[]{:S(2)}) copy-start(s32[4,256]{1,0:T(4,128)} %param.8) | copy-start | bytes 12292
  10.5 2.0 copy-start
  12.5 12.1 %copy-start.5 = (s32[4,256]{1,0:T(4,128)S(1)}, s32[4,256]{1,0:T(4,128)}, u32[]{:S(2)}) copy-start(s32[4,256]{1,0:T(4,128)} %param.9) | copy-start | bytes 12292
  12.5 12.1 %copy-start.4 = (f32[4,256]{1,0:T(4,128)S(1)}, f32[4,256]{1,0:T(4,128)}, u32[]{:S(2)}) copy-start(f32[4,256]{1,0:T(4,128)} %param.7) | copy-start | bytes 12292
  12.6 15.6 %collective-permute-start.1 = (bf16[1024,256]{1,0:T(8,128)(2,1)S(1)}, bf16[1024,256]{1,0:T(8,128)(2,1)S(1)}, u32[]{:S(2)}, u32[]{:S(2)}) collective-permute-start(bf16[1024,256]{1,0:T(8,128)(2,1)S(1)} %get-tuple-element.22), channel_id=1, source_target_pairs={{2,0},{4,2},{6,4},{8,6},{10,8},{12,10},{14,12},{16,14},{18,16},{20... | collective-permute-start | bytes 1572872 | tf_op jit(solution)/shard_map/ppermute | solution.py:207
  15.0 16.2 %collective-permute-start = (bf16[1024,256]{1,0:T(8,128)(2,1)S(1)}, bf16[1024,256]{1,0:T(8,128)(2,1)S(1)}, u32[]{:S(2)}, u32[]{:S(2)}) collective-permute-start(bf16[1024,256]{1,0:T(8,128)(2,1)S(1)} %get-tuple-element.23), channel_id=1, source_target_pairs={{0,2},{2,4},{4,6},{6,8},{8,10},{10,12},{12,14},{14,16},{16,18},{18... | collective-permute-start | bytes 1572872 | tf_op jit(solution)/shard_map/ppermute | solution.py:206
  28.1 3.1 copy-start.2
  31.2 0.8 copy-start.3
  52.1 262.1 %collective-permute-start.2 = (f32[16,3,256]{2,1,0:T(4,128)S(1)}, f32[16,3,256]{2,1,0:T(4,128)S(1)}, u32[]{:S(2)}, u32[]{:S(2)}) collective-permute-start(f32[16,3,256]{2,1,0:T(4,128)S(1)} %get-tuple-element.28), channel_id=1, source_target_pairs={{0,2},{2,4},{4,6},{6,8},{8,10},{10,12},{12,14},{14,16},{16,18},{18... | collective-permute-start | bytes 147464 | tf_op jit(solution)/shard_map/ppermute | solution.py:114
  54.6 259.6 %collective-permute-start.3 = (f32[16,3,256]{2,1,0:T(4,128)S(1)}, f32[16,3,256]{2,1,0:T(4,128)S(1)}, u32[]{:S(2)}, u32[]{:S(2)}) collective-permute-start(f32[16,3,256]{2,1,0:T(4,128)S(1)} %get-tuple-element.29), channel_id=1, source_target_pairs={{2,0},{4,2},{6,4},{8,6},{10,8},{12,10},{14,12},{16,14},{18,16},{20... | collective-permute-start | bytes 147464 | tf_op jit(solution)/shard_map/ppermute | solution.py:115
  318.1 2.2 copy-start.1
Sparse Core Ops, SparseCore 0:
  62.0 250.2 all-reduce.5

commit v7 on v5

--- a/solution.py
+++ b/solution.py
@@ -223,9 +223,14 @@
     scale = lax.rsqrt(squares / cells_all + 1e-06)
     fields = sweep_all(moments, fluid, collision, wall_level(codes))
     delta = ((fields - moments) * scale).astype(jnp.bfloat16).reshape(NM, width * plane)
-    added = jnp.dot(lift, delta, preferred_element_type=jnp.float32)
-    corrected = (fluid.reshape(1, width * plane) * (starred_flat + added)).astype(jnp.bfloat16)
-    return (corrected.reshape(local_vel, width, plane), fields * scale)
+    lifted = lift.astype(jnp.float32).reshape(local_vel, NM, 1, 1)
+    spread = delta.astype(jnp.float32).reshape(NM, width, plane)
+    added = lifted[:, 0] * spread[0]
+    for m in range(1, NM):
+        added = added + lifted[:, m] * spread[m]
+    starred_cells = starred_flat.reshape(local_vel, width, plane)
+    corrected = (fluid[None] * (starred_cells + added)).astype(jnp.bfloat16)
+    return (corrected, fields * scale)
 
 
 def solution(mesh):

time: 123 us -> 148 us (1.20)
  other arithmetic: 12.5 us -> 40.7 us
  starting transfers between devices: 49.9 us -> 48 us
    convert_element_type x3, other arithmetic: 4.86 us -> 31.7 us  [the longest x1 31.7 us: on_device(): corrected = (fluid[None] * (starred_cells + added)).astype(jnp.bfloat16)]
    convert_element_type x0 -> x1, local copies, waits for them, and re-layouts: none -> 8.97 us  [on_device(): corrected = (fluid[None] * (starred_cells + added)).astype(jnp.bfloat16)]
    reshape x1 -> x0, local copies, waits for them, and re-layouts: 7.83 us -> none  [on_device(): return (corrected.reshape(local_vel, width, plane), fields * scale)]
    ppermute x7, starting transfers between devices: 36.4 us -> 34.5 us  [exchange_sum(): lax.ppermute(value, axis, [(i, i ^ step) for i in range(count)])]
    unnamed x20 -> x15, local copies, waits for them, and re-layouts: 8.16 us -> 7.25 us
  transfers between devices with their start and end apart: 11 -> 11, of which waited for: 9 -> 8; matrix products, arithmetic and copies ran while one was open for 8% -> 13% of each run, Pallas kernels for 0% -> 0%
where the time goes in v7:
time: 148 us; the launch traced here: 146 us
  starting transfers between devices  48 us (32%)
  other arithmetic  40.7 us (28%)
  local copies, waits for them, and re-layouts  19.3 us (13%)
  Pallas kernels  15.8 us (11%)
  waiting for transfers between devices  11.6 us (8%)
  between operations  6.51 us (4%)
  blocking collectives  4.2 us (3%)
    ppermute x7, starting transfers between devices, exchange_sum(): lax.ppermute(value, axis, [(i, i ^ step) for i in range(count)])  34.5 us
    convert_element_type x1, other arithmetic, on_device(): corrected = (fluid[None] * (starred_cells + added)).astype(jnp.bfloat16)  31.7 us
    pallas_call x1, Pallas kernels, advance(): pl.pallas_call(advance_kernel, grid=grid, in_specs=[pl.BlockSpec((block,...  15.8 us
    convert_element_type x1, local copies, waits for them, and re-layouts, on_device(): corrected = (fluid[None] * (starred_cells + added)).astype(jnp.bfloat16)  8.97 us
    ppermute x7, waiting for transfers between devices, exchange_sum(): lax.ppermute(value, axis, [(i, i ^ step) for i in range(count)])  7.7 us
    unnamed x15, local copies, waits for them, and re-layouts  7.25 us
    ppermute x1, starting transfers between devices, sweep_all(): lax.ppermute(pack[:, :depth], 'space', [(i + 1, i) for i in range(ends)])  5.18 us
    psum x1, blocking collectives, on_device(): moments = lax.psum(partial_value, 'vel').reshape(NM, width, plane)  4.2 us
  transfers between devices with their start and end apart: 11, of which 8 were waited for; matrix products, arithmetic and copies ran while one was open for 13% of the time, Pallas kernels for 0%

profile of v7, /device:TPU:10, one launch (start us, length us, event | category | flops | bytes accessed | tf_op | source)
XLA Modules:
  0.0 146.1 jit_solution(5393200072486656162)
XLA Ops:
  0.7 3.2 %copy.22 = bf16[256,8,4,256]{3,1,2,0:T(8,128)(2,1)S(1)} copy(bf16[256,8,4,256]{3,2,1,0:T(4,128)(2,1)} %bitcast.90) | data formatting | bytes 8388608
  3.9 2.0 %copy-done = bf16[256,8,4,256]{3,1,2,0:T(8,128)(2,1)} copy-done((bf16[256,8,4,256]{3,1,2,0:T(8,128)(2,1)}, bf16[256,8,4,256]{3,1,2,0:T(8,128)(2,1)S(1)}, u32[]{:S(2)}) %copy-start) | copy-done | bytes 4194328
  6.0 2.4 %collective-permute-start.1 = (bf16[1024,256]{1,0:T(8,128)(2,1)S(1)}, bf16[1024,256]{1,0:T(8,128)(2,1)S(1)}, u32[]{:S(2)}, u32[]{:S(2)}) collective-permute-start(bf16[1024,256]{1,0:T(8,128)(2,1)S(1)} %get-tuple-element.10), channel_id=1, source_target_pairs={{2,0},{4,2},{6,4},{8,6},{10,8},{12,10},{14,12},{16,14},{18,16},{20... | collective-permute-start | bytes 1572872 | tf_op jit(solution)/shard_map/ppermute | solution.py:207
  8.5 3.4 %collective-permute-start = (bf16[1024,256]{1,0:T(8,128)(2,1)S(1)}, bf16[1024,256]{1,0:T(8,128)(2,1)S(1)}, u32[]{:S(2)}, u32[]{:S(2)}) collective-permute-start(bf16[1024,256]{1,0:T(8,128)(2,1)S(1)} %get-tuple-element.11), channel_id=1, source_target_pairs={{0,2},{2,4},{4,6},{6,8},{8,10},{10,12},{12,14},{14,16},{16,18},{18... | collective-permute-start | bytes 1572872 | tf_op jit(solution)/shard_map/ppermute | solution.py:206
  11.9 0.6 fusion.48
  13.7 0.2 stack.6
  13.8 1.3 convert_bitcast_fusion
  15.2 0.4 copy.15
  15.6 1.1 broadcast_multiply_fusion.2.cx_ref
  16.7 0.4 copy.17
  17.1 1.0 broadcast_multiply_fusion.1.cy_ref
  18.1 0.6 copy.23
  18.7 0.6 copy.24
  19.3 0.4 copy.19
  19.7 1.1 broadcast_multiply_fusion.cz_ref
  20.7 0.8 collective-permute-done.1.right_ref
  21.6 3.1 %collective-permute-done.left_ref = bf16[1024,256]{1,0:T(8,128)(2,1)S(1)} collective-permute-done((bf16[1024,256]{1,0:T(8,128)(2,1)S(1)}, bf16[1024,256]{1,0:T(8,128)(2,1)S(1)}, u32[]{:S(2)}, u32[]{:S(2)}) %collective-permute-start) | collective-permute-done | bytes 524320 | tf_op jit(solution)/shard_map/ppermute | solution.py:206
  24.6 0.8 copy-done.2
  25.4 15.8 %shard_map.59 = (bf16[2048,1024]{1,0:T(8,128)(2,1)}, f32[13,1024]{1,0:T(8,128)}) custom-call(bf16[2048,1024]{1,0:T(8,128)(2,1)} %bitcast.89, bf16[1024,256]{1,0:T(8,128)(2,1)} %copy-done.2, bf16[1024,256]{1,0:T(8,128)(2,1)} %copy-done.1, f32[2048,1]{1,0:T(8,128)} %broadcast_multiply_fusion.2.cx_ref, f32[2048,1]{1,0:T(8,128)} %broadcast_multiply_fusion.1.cy_ref, ...), custom_call_target="tpu_custom_call" | custom-call | tf_op jit(solution)/shard_map/pallas_call | solution.py:175
  41.2 4.2 %psum.7 = f32[13,1024]{1,0:T(8,128)S(1)} all-reduce(f32[13,1024]{1,0:T(8,128)} %get-tuple-element.5), channel_id=1, replica_groups=mesh['space'=128,'vel'=2] {'vel'}, use_global_device_ids=true, to_apply=%region_1.2 | all-reduce | flops 13312 | bytes 106496 | tf_op jit(solution)/shard_map/psum | solution.py:220
  45.5 2.5 %collective-permute-start.2 = (f32[16,3,256]{2,1,0:T(4,128)S(1)}, f32[16,3,256]{2,1,0:T(4,128)S(1)}, u32[]{:S(2)}, u32[]{:S(2)}) collective-permute-start(f32[16,3,256]{2,1,0:T(4,128)S(1)} %get-tuple-element.31), channel_id=1, source_target_pairs={{0,2},{2,4},{4,6},{6,8},{8,10},{10,12},{12,14},{14,16},{16,18},{18... | collective-permute-start | bytes 147464 | tf_op jit(solution)/shard_map/ppermute | solution.py:114
  48.0 5.2 %collective-permute-start.3 = (f32[16,3,256]{2,1,0:T(4,128)S(1)}, f32[16,3,256]{2,1,0:T(4,128)S(1)}, u32[]{:S(2)}, u32[]{:S(2)}) collective-permute-start(f32[16,3,256]{2,1,0:T(4,128)S(1)} %get-tuple-element.32), channel_id=1, source_target_pairs={{2,0},{4,2},{6,4},{8,6},{10,8},{12,10},{14,12},{16,14},{18,16},{20... | collective-permute-start | bytes 147464 | tf_op jit(solution)/shard_map/ppermute | solution.py:115
  53.2 0.6 fusion.85
  53.8 4.1 %collective-permute-start.4 = (f32[]{:T(128)}, f32[]{:T(128)}, u32[]{:S(2)}, u32[]{:S(2)}) collective-permute-start(f32[]{:T(128)} %fusion.85), channel_id=1, source_target_pairs={{0,2},{2,0},{4,6},{6,4},{8,10},{10,8},{12,14},{14,12},{16,18},{18,... | collective-permute-start | bytes 20 | tf_op jit(solution)/shard_map/ppermute | solution.py:44
  58.0 9.0 %reshape.556 = f32[2048,4,256]{2,1,0:T(4,128)} reshape(bf16[2048,1024]{1,0:T(8,128)(2,1)} %get-tuple-element.4) | data formatting | bytes 12582912 | tf_op jit(solution)/shard_map/convert_element_type | solution.py:232
  68.2 1.4 collective-permute-start.5
  69.6 3.7 %collective-permute-done.5 = f32[]{:T(128)} collective-permute-done((f32[]{:T(128)}, f32[]{:T(128)}, u32[]{:S(2)}, u32[]{:S(2)}) %collective-permute-start.5) | collective-permute-done | bytes 36 | tf_op jit(solution)/shard_map/ppermute | solution.py:44
  74.0 1.4 collective-permute-start.6
  75.4 2.2 %collective-permute-done.6 = f32[]{:T(128)} collective-permute-done((f32[]{:T(128)}, f32[]{:T(128)}, u32[]{:S(2)}, u32[]{:S(2)}) %collective-permute-start.6) | collective-permute-done | bytes 36 | tf_op jit(solution)/shard_map/ppermute | solution.py:44
  78.3 4.0 %collective-permute-start.7 = (f32[]{:T(128)}, f32[]{:T(128)}, u32[]{:S(2)}, u32[]{:S(2)}) collective-permute-start(f32[]{:T(128)} %add.756), channel_id=1, source_target_pairs={{0,16},{2,18},{4,20},{6,22},{8,24},{10,26},{12,28},{14,30},{16,0},... | collective-permute-start | bytes 20 | tf_op jit(solution)/shard_map/ppermute | solution.py:44
  82.3 1.1 collective-permute-done.7
  84.1 8.1 %collective-permute-start.8 = (f32[]{:T(128)}, f32[]{:T(128)}, u32[]{:S(2)}, u32[]{:S(2)}) collective-permute-start(f32[]{:T(128)} %add.757), channel_id=1, source_target_pairs={{0,32},{2,34},{4,36},{6,38},{8,40},{10,42},{12,44},{14,46},{16,48}... | collective-permute-start | bytes 20 | tf_op jit(solution)/shard_map/ppermute | solution.py:44
  92.2 0.2 collective-permute-done.8
  93.1 4.8 %collective-permute-start.9 = (f32[]{:T(128)}, f32[]{:T(128)}, u32[]{:S(2)}, u32[]{:S(2)}) collective-permute-start(f32[]{:T(128)} %add.758), channel_id=1, source_target_pairs={{0,64},{2,66},{4,68},{6,70},{8,72},{10,74},{12,76},{14,78},{16,80}... | collective-permute-start | bytes 20 | tf_op jit(solution)/shard_map/ppermute | solution.py:44
  97.9 0.2 collective-permute-done.9
  98.8 10.8 %collective-permute-start.10 = (f32[]{:T(128)}, f32[]{:T(128)}, u32[]{:S(2)}, u32[]{:S(2)}) collective-permute-start(f32[]{:T(128)} %add.759), channel_id=1, source_target_pairs={{0,128},{2,130},{4,132},{6,134},{8,136},{10,138},{12,140},{14,142}... | collective-permute-start | bytes 20 | tf_op jit(solution)/shard_map/ppermute | solution.py:44
  109.6 0.2 collective-permute-done.10
  110.8 0.3 reshape.550
  111.0 0.5 fusion.2
  111.5 0.4 reshape.551
  112.0 0.2 reshape.552
  112.2 0.4 fusion.5
  112.6 0.3 reshape.553
  113.0 0.2 reshape.554
  113.2 0.3 fusion.8
  113.5 0.2 reshape.555
  113.8 0.7 broadcast_multiply_fusion.5
  114.4 31.7 %multiply_convert_fusion = bf16[2048,4,256]{2,1,0:T(4,128)(2,1)} fusion(f32[2048,4,256]{2,1,0:T(4,128)} %reshape.556, f32[4,256]{1,0:T(4,128)S(1)} %get-tuple-element.34, f32[2048]{0:T(1024)S(1)} %bitcast.97, f32[4,256]{1,0:T(4,128)S(1)} %get-tuple-element.35, f32[2048]{0:T(1024)S(1)} %bitcast.98, f32[4,256]{1,0:T(4,128)S(1)} %get-tuple-element.36, ...), kind=kLoop, calls=%fused_computation | loop fusion | flops 58720256 | bytes 12746752 | tf_op jit(solution)/shard_map/convert_element_type | solution.py:232
  (44 shorter events, 1.7 us)
Async XLA Ops:
  0.6 13.0 %copy-start.4 = (s32[4,256]{1,0:T(4,128)S(1)}, s32[4,256]{1,0:T(4,128)}, u32[]{:S(2)}) copy-start(s32[4,256]{1,0:T(4,128)} %param.7) | copy-start | bytes 12292
  0.6 17.5 %copy-start.5 = (s32[4,256]{1,0:T(4,128)S(1)}, s32[4,256]{1,0:T(4,128)}, u32[]{:S(2)}) copy-start(s32[4,256]{1,0:T(4,128)} %param.6) | copy-start | bytes 12292
  0.7 17.5 %copy-start.3 = (f32[4,256]{1,0:T(4,128)S(1)}, f32[4,256]{1,0:T(4,128)}, u32[]{:S(2)}) copy-start(f32[4,256]{1,0:T(4,128)} %param.5) | copy-start | bytes 12292
  3.9 2.0 %copy-start = (bf16[256,8,4,256]{3,1,2,0:T(8,128)(2,1)}, bf16[256,8,4,256]{3,1,2,0:T(8,128)(2,1)S(1)}, u32[]{:S(2)}) copy-start(bf16[256,8,4,256]{3,1,2,0:T(8,128)(2,1)S(1)} %copy.22) | copy-start | bytes 12582916
  6.0 15.6 %collective-permute-start.1 = (bf16[1024,256]{1,0:T(8,128)(2,1)S(1)}, bf16[1024,256]{1,0:T(8,128)(2,1)S(1)}, u32[]{:S(2)}, u32[]{:S(2)}) collective-permute-start(bf16[1024,256]{1,0:T(8,128)(2,1)S(1)} %get-tuple-element.10), channel_id=1, source_target_pairs={{2,0},{4,2},{6,4},{8,6},{10,8},{12,10},{14,12},{16,14},{18,16},{20... | collective-permute-start | bytes 1572872 | tf_op jit(solution)/shard_map/ppermute | solution.py:207
  8.5 16.2 %collective-permute-start = (bf16[1024,256]{1,0:T(8,128)(2,1)S(1)}, bf16[1024,256]{1,0:T(8,128)(2,1)S(1)}, u32[]{:S(2)}, u32[]{:S(2)}) collective-permute-start(bf16[1024,256]{1,0:T(8,128)(2,1)S(1)} %get-tuple-element.11), channel_id=1, source_target_pairs={{0,2},{2,4},{4,6},{6,8},{8,10},{10,12},{12,14},{14,16},{16,18},{18... | collective-permute-start | bytes 1572872 | tf_op jit(solution)/shard_map/ppermute | solution.py:206
  21.6 3.1 %copy-start.1 = (bf16[1024,256]{1,0:T(8,128)(2,1)}, bf16[1024,256]{1,0:T(8,128)(2,1)S(1)}, u32[]{:S(2)}) copy-start(bf16[1024,256]{1,0:T(8,128)(2,1)S(1)} %collective-permute-done.1.right_ref) | copy-start | bytes 1572868
  24.6 0.8 copy-start.2
  45.5 65.0 %collective-permute-start.2 = (f32[16,3,256]{2,1,0:T(4,128)S(1)}, f32[16,3,256]{2,1,0:T(4,128)S(1)}, u32[]{:S(2)}, u32[]{:S(2)}) collective-permute-start(f32[16,3,256]{2,1,0:T(4,128)S(1)} %get-tuple-element.31), channel_id=1, source_target_pairs={{0,2},{2,4},{4,6},{6,8},{8,10},{10,12},{12,14},{14,16},{16,18},{18... | collective-permute-start | bytes 147464 | tf_op jit(solution)/shard_map/ppermute | solution.py:114
  48.0 62.5 %collective-permute-start.3 = (f32[16,3,256]{2,1,0:T(4,128)S(1)}, f32[16,3,256]{2,1,0:T(4,128)S(1)}, u32[]{:S(2)}, u32[]{:S(2)}) collective-permute-start(f32[16,3,256]{2,1,0:T(4,128)S(1)} %get-tuple-element.32), channel_id=1, source_target_pairs={{2,0},{4,2},{6,4},{8,6},{10,8},{12,10},{14,12},{16,14},{18,16},{20... | collective-permute-start | bytes 147464 | tf_op jit(solution)/shard_map/ppermute | solution.py:115
  53.8 13.1 %collective-permute-start.4 = (f32[]{:T(128)}, f32[]{:T(128)}, u32[]{:S(2)}, u32[]{:S(2)}) collective-permute-start(f32[]{:T(128)} %fusion.85), channel_id=1, source_target_pairs={{0,2},{2,0},{4,6},{6,4},{8,10},{10,8},{12,14},{14,12},{16,18},{18,... | collective-permute-start | bytes 20 | tf_op jit(solution)/shard_map/ppermute | solution.py:44
  68.2 5.1 %collective-permute-start.5 = (f32[]{:T(128)}, f32[]{:T(128)}, u32[]{:S(2)}, u32[]{:S(2)}) collective-permute-start(f32[]{:T(128)} %add.754), channel_id=1, source_target_pairs={{0,4},{2,6},{4,0},{6,2},{8,12},{10,14},{12,8},{14,10},{16,20},{18,... | collective-permute-start | bytes 20 | tf_op jit(solution)/shard_map/ppermute | solution.py:44
  74.0 3.6 %collective-permute-start.6 = (f32[]{:T(128)}, f32[]{:T(128)}, u32[]{:S(2)}, u32[]{:S(2)}) collective-permute-start(f32[]{:T(128)} %add.755), channel_id=1, source_target_pairs={{0,8},{2,10},{4,12},{6,14},{8,0},{10,2},{12,4},{14,6},{16,24},{18,... | collective-permute-start | bytes 20 | tf_op jit(solution)/shard_map/ppermute | solution.py:44
  78.3 5.1 %collective-permute-start.7 = (f32[]{:T(128)}, f32[]{:T(128)}, u32[]{:S(2)}, u32[]{:S(2)}) collective-permute-start(f32[]{:T(128)} %add.756), channel_id=1, source_target_pairs={{0,16},{2,18},{4,20},{6,22},{8,24},{10,26},{12,28},{14,30},{16,0},... | collective-permute-start | bytes 20 | tf_op jit(solution)/shard_map/ppermute | solution.py:44
  84.1 8.3 %collective-permute-start.8 = (f32[]{:T(128)}, f32[]{:T(128)}, u32[]{:S(2)}, u32[]{:S(2)}) collective-permute-start(f32[]{:T(128)} %add.757), channel_id=1, source_target_pairs={{0,32},{2,34},{4,36},{6,38},{8,40},{10,42},{12,44},{14,46},{16,48}... | collective-permute-start | bytes 20 | tf_op jit(solution)/shard_map/ppermute | solution.py:44
  93.1 5.0 %collective-permute-start.9 = (f32[]{:T(128)}, f32[]{:T(128)}, u32[]{:S(2)}, u32[]{:S(2)}) collective-permute-start(f32[]{:T(128)} %add.758), channel_id=1, source_target_pairs={{0,64},{2,66},{4,68},{6,70},{8,72},{10,74},{12,76},{14,78},{16,80}... | collective-permute-start | bytes 20 | tf_op jit(solution)/shard_map/ppermute | solution.py:44
  98.8 11.0 %collective-permute-start.10 = (f32[]{:T(128)}, f32[]{:T(128)}, u32[]{:S(2)}, u32[]{:S(2)}) collective-permute-start(f32[]{:T(128)} %add.759), channel_id=1, source_target_pairs={{0,128},{2,130},{4,132},{6,134},{8,136},{10,138},{12,140},{14,142}... | collective-permute-start | bytes 20 | tf_op jit(solution)/shard_map/ppermute | solution.py:44

commit v8 on v5

--- a/solution.py
+++ b/solution.py
@@ -12,6 +12,8 @@
 NY = 16
 NZ = 16
 SWEEPS = 3
+SPACE_AXES = ("sz", "sy", "sx")
+SPACE_SIZES = (8, 4, 4)
 
 
 TIME_STEP = 0.06
@@ -106,13 +108,13 @@
 
 
 def sweep_all(moments, fluid, collision, kappa):
-    count = lax.axis_size("space")
+    count = axis_count(SPACE_AXES)
     ends = count - 1
     width = moments.shape[1]
     depth = SWEEPS
     pack = jnp.concatenate([moments, jnp.stack([fluid, collision, kappa])], axis=0)
-    before = lax.ppermute(pack[:, width - depth :], "space", [(i, i + 1) for i in range(ends)])
-    after = lax.ppermute(pack[:, :depth], "space", [(i + 1, i) for i in range(ends)])
+    before = lax.ppermute(pack[:, width - depth :], SPACE_AXES, [(i, i + 1) for i in range(ends)])
+    after = lax.ppermute(pack[:, :depth], SPACE_AXES, [(i + 1, i) for i in range(ends)])
     wide = jnp.concatenate([before, pack, after], axis=1)
     total = wide.shape[1]
     grown = wide[:NM]
@@ -196,15 +198,15 @@
     local_vel, width, plane = adjoint.shape
     start = lax.axis_index("vel") * local_vel
     speed_x, speed_y, speed_z, weigh, lift = tables(start, local_vel)
-    count = lax.axis_size("space")
+    count = axis_count(SPACE_AXES)
     ends = count - 1
     flat = lax.optimization_barrier(adjoint.reshape(local_vel, width * plane))
     grouped = flat.reshape(local_vel // NV1, NV1, width * plane)
     half = NV1 // 2
     tail = grouped[:, :half, (width - 1) * plane :].reshape(local_vel // 2, plane)
     head = grouped[:, half:, :plane].reshape(local_vel // 2, plane)
-    left = lax.ppermute(tail, "space", [(i, i + 1) for i in range(ends)])
-    right = lax.ppermute(head, "space", [(i + 1, i) for i in range(ends)])
+    left = lax.ppermute(tail, SPACE_AXES, [(i, i + 1) for i in range(ends)])
+    right = lax.ppermute(head, SPACE_AXES, [(i + 1, i) for i in range(ends)])
     fluid = (1 - solid).astype(jnp.float32)
     starred_flat, partial_value = advance(
         flat,
@@ -218,8 +220,10 @@
         weigh,
     )
     moments = lax.psum(partial_value, "vel").reshape(NM, width, plane)
-    cells_all = width * lax.axis_size("space") * plane
-    squares = exchange_sum(jnp.sum(moments[0] * moments[0]), "space")
+    cells_all = width * axis_count(SPACE_AXES) * plane
+    squares = jnp.sum(moments[0] * moments[0])
+    for axis in SPACE_AXES[::-1]:
+        squares = lax.psum(squares, axis)
     scale = lax.rsqrt(squares / cells_all + 1e-06)
     fields = sweep_all(moments, fluid, collision, wall_level(codes))
     delta = ((fields - moments) * scale).astype(jnp.bfloat16).reshape(NM, width * plane)
@@ -228,11 +232,21 @@
     return (corrected.reshape(local_vel, width, plane), fields * scale)
 
 
+def axis_count(axes):
+    count = 1
+    for axis in axes:
+        count *= lax.axis_size(axis)
+    return count
+
+
 def solution(mesh):
+    sizes = SPACE_SIZES if mesh.devices.shape[0] == math.prod(SPACE_SIZES) else (mesh.devices.shape[0],)
+    names = SPACE_AXES if len(sizes) == len(SPACE_AXES) else ("space",)
+    fine = jax.sharding.Mesh(mesh.devices.reshape(sizes + (mesh.devices.shape[1],)), names + ("vel",))
     return jax.shard_map(
         on_device,
-        mesh=mesh,
-        in_specs=(P("vel", "space", None), P("space", None), P("space", None), P("space", None)),
-        out_specs=(P("vel", "space", None), P(None, "space", None)),
+        mesh=fine,
+        in_specs=(P("vel", names, None), P(names, None), P(names, None), P(names, None)),
+        out_specs=(P("vel", names, None), P(None, names, None)),
         check_vma=False,
     )

time: 123 us -> 122 us (level); the launches traced: 121 us -> 121 us
  blocking collectives: 4.2 us -> 53.5 us
  starting transfers between devices: 49.9 us -> 13.5 us
  waiting for transfers between devices: 11.4 us -> 4.02 us
  between operations: 6.43 us -> 1.68 us
    psum x0 -> x3, blocking collectives: none -> 49.3 us  [on_device(): squares = lax.psum(squares, axis)]
    ppermute x11 -> x4, starting transfers between devices: 49.9 us -> 13.5 us  [the longest x1 5.18 us: sweep_all(): lax.ppermute(pack[:, :depth], SPACE_AXES, [(i + 1, i) for i in range(ends)])]
    ppermute x11 -> x4, waiting for transfers between devices: 11.4 us -> 4.02 us  [the longest x1 3.08 us: on_device(): left = lax.ppermute(tail, SPACE_AXES, [(i, i + 1) for i in range(ends)])]
  transfers between devices with their start and end apart: 11 -> 4, of which waited for: 9 -> 2; matrix products, arithmetic and copies ran while one was open for 8% -> 8% of each run, Pallas kernels for 0% -> 0%
where the time goes in v8:
time: 122 us; the launch traced here: 121 us
  blocking collectives  53.5 us (44%)
  local copies, waits for them, and re-layouts  19 us (16%)
  Pallas kernels  15.8 us (13%)
  starting transfers between devices  13.5 us (11%)
  other arithmetic  12.5 us (10%)
  waiting for transfers between devices  4.02 us (3%)
  between operations  1.68 us (1%)
  matrix products  1.28 us (1%)
    psum x3, blocking collectives, on_device(): squares = lax.psum(squares, axis)  49.3 us
    pallas_call x1, Pallas kernels, advance(): pl.pallas_call(advance_kernel, grid=grid, in_specs=[pl.BlockSpec((block,...  15.8 us
    unnamed x20, local copies, waits for them, and re-layouts  8.15 us
    reshape x1, local copies, waits for them, and re-layouts, on_device(): return (corrected.reshape(local_vel, width, plane), fields * scale)  7.83 us
    ppermute x1, starting transfers between devices, sweep_all(): lax.ppermute(pack[:, :depth], SPACE_AXES, [(i + 1, i) for i in range(ends)])  5.18 us
    psum x1, blocking collectives, on_device(): moments = lax.psum(partial_value, 'vel').reshape(NM, width, plane)  4.2 us
    convert_element_type x1, other arithmetic, on_device(): (fluid.reshape(1, width * plane) * (starred_flat + added)).astype(jnp.bfl...  3.54 us
    ppermute x1, starting transfers between devices, on_device(): left = lax.ppermute(tail, SPACE_AXES, [(i, i + 1) for i in range(ends)])  3.4 us
  transfers between devices with their start and end apart: 4, of which 2 were waited for; matrix products, arithmetic and copies ran while one was open for 8% of the time, Pallas kernels for 0%

profile of v8, /device:TPU:10, one launch (start us, length us, event | category | flops | bytes accessed | tf_op | source)
XLA Modules:
  0.0 121.2 jit_solution(14694112874523739044)
XLA Ops:
  0.6 3.2 %copy.28 = bf16[256,8,4,256]{3,1,2,0:T(8,128)(2,1)S(1)} copy(bf16[256,8,4,256]{3,2,1,0:T(4,128)(2,1)} %bitcast.54) | data formatting | bytes 8388608
  3.9 2.0 %copy-done = bf16[256,8,4,256]{3,1,2,0:T(8,128)(2,1)} copy-done((bf16[256,8,4,256]{3,1,2,0:T(8,128)(2,1)}, bf16[256,8,4,256]{3,1,2,0:T(8,128)(2,1)S(1)}, u32[]{:S(2)}) %copy-start) | copy-done | bytes 4194328
  6.0 2.4 %collective-permute-start.1 = (bf16[1024,256]{1,0:T(8,128)(2,1)S(1)}, bf16[1024,256]{1,0:T(8,128)(2,1)S(1)}, u32[]{:S(2)}, u32[]{:S(2)}) collective-permute-start(bf16[1024,256]{1,0:T(8,128)(2,1)S(1)} %get-tuple-element.10), channel_id=1, source_target_pairs={{2,0},{4,2},{6,4},{8,6},{10,8},{12,10},{14,12},{16,14},{18,16},{20... | collective-permute-start | bytes 1572872 | tf_op jit(solution)/shard_map/ppermute | solution.py:209
  8.4 3.4 %collective-permute-start = (bf16[1024,256]{1,0:T(8,128)(2,1)S(1)}, bf16[1024,256]{1,0:T(8,128)(2,1)S(1)}, u32[]{:S(2)}, u32[]{:S(2)}) collective-permute-start(bf16[1024,256]{1,0:T(8,128)(2,1)S(1)} %get-tuple-element.11), channel_id=1, source_target_pairs={{0,2},{2,4},{4,6},{6,8},{8,10},{10,12},{12,14},{14,16},{16,18},{18... | collective-permute-start | bytes 1572872 | tf_op jit(solution)/shard_map/ppermute | solution.py:208
  11.8 0.6 fusion.49
  12.5 0.2 add_multiply_fusion
  12.7 0.2 subtract_multiply_fusion
  12.8 0.1 fusion.88
  13.0 0.1 broadcast_multiply_fusion.6
  13.2 0.2 multiply_multiply_fusion.1
  13.3 0.2 fusion.72
  13.5 0.1 fusion.67
  13.6 0.4 copy.18
  14.0 1.0 broadcast_multiply_fusion.2.cx_ref
  15.0 0.4 copy.20
  15.4 1.1 broadcast_multiply_fusion.1.cy_ref
  16.5 0.2 stack.8
  16.7 1.3 %divide_convert_fusion.weigh_ref = bf16[13,2048]{1,0:T(8,128)(2,1)} fusion(f32[13,2048]{1,0:T(8,128)S(1)} %stack.8, f32[]{:T(128)} %fusion.49, f32[2048]{0:T(1024)S(1)} %get-tuple-element.26), kind=kLoop, calls=%fused_computation.33 | loop fusion | flops 79872 | bytes 167940 | tf_op jit(solution)/shard_map/convert_element_type | solution.py:84
  18.0 0.6 copy.29
  18.6 0.6 copy.30
  19.2 0.4 copy.22
  19.5 1.1 broadcast_multiply_fusion.cz_ref
  20.6 0.9 collective-permute-done.1.right_ref
  21.5 3.1 %collective-permute-done.left_ref = bf16[1024,256]{1,0:T(8,128)(2,1)S(1)} collective-permute-done((bf16[1024,256]{1,0:T(8,128)(2,1)S(1)}, bf16[1024,256]{1,0:T(8,128)(2,1)S(1)}, u32[]{:S(2)}, u32[]{:S(2)}) %collective-permute-start) | collective-permute-done | bytes 524320 | tf_op jit(solution)/shard_map/ppermute | solution.py:208
  24.6 0.8 copy-done.3
  25.4 15.8 %shard_map.59 = (bf16[2048,1024]{1,0:T(8,128)(2,1)}, f32[13,1024]{1,0:T(8,128)}) custom-call(bf16[2048,1024]{1,0:T(8,128)(2,1)} %bitcast.53, bf16[1024,256]{1,0:T(8,128)(2,1)} %copy-done.3, bf16[1024,256]{1,0:T(8,128)(2,1)} %copy-done.2, f32[2048,1]{1,0:T(8,128)} %broadcast_multiply_fusion.2.cx_ref, f32[2048,1]{1,0:T(8,128)} %broadcast_multiply_fusion.1.cy_ref, ...), custom_call_target="tpu_custom_call" | custom-call | tf_op jit(solution)/shard_map/pallas_call | solution.py:177
  41.2 4.2 %psum.28 = f32[13,1024]{1,0:T(8,128)S(1)} all-reduce(f32[13,1024]{1,0:T(8,128)} %get-tuple-element.5), channel_id=1, replica_groups=mesh['sz'=8,'sy'=4,'sx'=4,'vel'=2] {'vel'}, use_global_device_ids=true, to_apply=%region_1.2 | all-reduce | flops 13312 | bytes 106496 | tf_op jit(solution)/shard_map/psum | solution.py:222
  45.5 2.5 %collective-permute-start.2 = (f32[16,3,256]{2,1,0:T(4,128)S(1)}, f32[16,3,256]{2,1,0:T(4,128)S(1)}, u32[]{:S(2)}, u32[]{:S(2)}) collective-permute-start(f32[16,3,256]{2,1,0:T(4,128)S(1)} %get-tuple-element.16), channel_id=1, source_target_pairs={{0,2},{2,4},{4,6},{6,8},{8,10},{10,12},{12,14},{14,16},{16,18},{18... | collective-permute-start | bytes 147464 | tf_op jit(solution)/shard_map/ppermute | solution.py:116
  48.0 5.2 %collective-permute-start.3 = (f32[16,3,256]{2,1,0:T(4,128)S(1)}, f32[16,3,256]{2,1,0:T(4,128)S(1)}, u32[]{:S(2)}, u32[]{:S(2)}) collective-permute-start(f32[16,3,256]{2,1,0:T(4,128)S(1)} %get-tuple-element.17), channel_id=1, source_target_pairs={{2,0},{4,2},{6,4},{8,6},{10,8},{12,10},{14,12},{16,14},{18,16},{20... | collective-permute-start | bytes 147464 | tf_op jit(solution)/shard_map/ppermute | solution.py:117
  53.2 0.6 fusion.86
  53.8 12.5 %psum.29 = f32[]{:T(128)} all-reduce(f32[]{:T(128)} %fusion.86), channel_id=1, replica_groups=mesh['sz'=8,'sy'=4,'sx'=4,'vel'=2] {'sx'}, use_global_device_ids=true, to_apply=%region_3.4 | all-reduce | flops 1 | bytes 8 | tf_op jit(solution)/shard_map/psum | solution.py:226
  66.2 9.7 %psum.30 = f32[]{:T(128)} all-reduce(f32[]{:T(128)} %psum.29), channel_id=1, replica_groups=mesh['sz'=8,'sy'=4,'sx'=4,'vel'=2] {'sy'}, use_global_device_ids=true, to_apply=%region_4.5 | all-reduce | flops 1 | bytes 8 | tf_op jit(solution)/shard_map/psum | solution.py:226
  75.9 27.1 %psum.31 = f32[]{:T(128)} all-reduce(f32[]{:T(128)} %psum.30), channel_id=1, replica_groups=mesh['sz'=8,'sy'=4,'sx'=4,'vel'=2] {'sz'}, use_global_device_ids=true, to_apply=%region_5.6 | all-reduce | flops 1 | bytes 8 | tf_op jit(solution)/shard_map/psum | solution.py:226
  103.9 0.3 reshape.478
  104.2 0.5 fusion.2
  104.7 0.4 reshape.479
  105.2 0.2 reshape.480
  105.4 0.4 fusion.5
  105.8 0.3 reshape.481
  106.1 0.1 fusion.11
  106.2 0.2 reshape.482
  106.4 0.3 fusion.8
  106.7 0.2 reshape.483
  106.9 0.7 broadcast_multiply_fusion.5
  107.7 1.3 %fusion.15 = f32[2048,1024]{1,0:T(8,128)S(1)} fusion(bf16[13,1024]{1,0:T(8,128)(2,1)S(1)} %bitcast.55, f32[13,2048]{1,0:T(8,128)S(1)} %stack.8, f32[2048]{0:T(1024)S(1)} %get-tuple-element.25), kind=kOutput, calls=%fused_computation.44 | convolution fusion | flops 54579200 | bytes 8529920 | tf_op jit(solution)/shard_map/dot_general | solution.py:230
  108.9 0.9 copy-done.1
  109.8 3.5 %multiply_convert_fusion = bf16[2048,1024]{1,0:T(8,128)(2,1)} fusion(f32[2048,1024]{1,0:T(8,128)S(1)} %fusion.15, bf16[2048,1024]{1,0:T(8,128)(2,1)S(1)} %copy-done.1, f32[1024]{0:T(1024)S(1)} %bitcast.64), kind=kLoop, calls=%fused_computation | loop fusion | flops 8388608 | bytes 16781312 | tf_op jit(solution)/shard_map/convert_element_type | solution.py:231
  113.4 7.8 %reshape.485 = bf16[2048,4,256]{2,1,0:T(4,128)(2,1)} reshape(bf16[2048,1024]{1,0:T(8,128)(2,1)} %multiply_convert_fusion) | data formatting | bytes 8388608 | tf_op jit(solution)/shard_map/reshape | solution.py:232
  (37 shorter events, 0.6 us)
Async XLA Ops:
  0.6 13.0 %copy-start.6 = (s32[4,256]{1,0:T(4,128)S(1)}, s32[4,256]{1,0:T(4,128)}, u32[]{:S(2)}) copy-start(s32[4,256]{1,0:T(4,128)} %param.6) | copy-start | bytes 12292
  3.9 2.0 %copy-start = (bf16[256,8,4,256]{3,1,2,0:T(8,128)(2,1)}, bf16[256,8,4,256]{3,1,2,0:T(8,128)(2,1)S(1)}, u32[]{:S(2)}) copy-start(bf16[256,8,4,256]{3,1,2,0:T(8,128)(2,1)S(1)} %copy.28) | copy-start | bytes 12582916
  5.9 12.1 %copy-start.5 = (s32[4,256]{1,0:T(4,128)S(1)}, s32[4,256]{1,0:T(4,128)}, u32[]{:S(2)}) copy-start(s32[4,256]{1,0:T(4,128)} %param.7) | copy-start | bytes 12292
  5.9 12.1 %copy-start.4 = (f32[4,256]{1,0:T(4,128)S(1)}, f32[4,256]{1,0:T(4,128)}, u32[]{:S(2)}) copy-start(f32[4,256]{1,0:T(4,128)} %param.5) | copy-start | bytes 12292
  6.0 15.6 %collective-permute-start.1 = (bf16[1024,256]{1,0:T(8,128)(2,1)S(1)}, bf16[1024,256]{1,0:T(8,128)(2,1)S(1)}, u32[]{:S(2)}, u32[]{:S(2)}) collective-permute-start(bf16[1024,256]{1,0:T(8,128)(2,1)S(1)} %get-tuple-element.10), channel_id=1, source_target_pairs={{2,0},{4,2},{6,4},{8,6},{10,8},{12,10},{14,12},{16,14},{18,16},{20... | collective-permute-start | bytes 1572872 | tf_op jit(solution)/shard_map/ppermute | solution.py:209
  8.4 16.2 %collective-permute-start = (bf16[1024,256]{1,0:T(8,128)(2,1)S(1)}, bf16[1024,256]{1,0:T(8,128)(2,1)S(1)}, u32[]{:S(2)}, u32[]{:S(2)}) collective-permute-start(bf16[1024,256]{1,0:T(8,128)(2,1)S(1)} %get-tuple-element.11), channel_id=1, source_target_pairs={{0,2},{2,4},{4,6},{6,8},{8,10},{10,12},{12,14},{14,16},{16,18},{18... | collective-permute-start | bytes 1572872 | tf_op jit(solution)/shard_map/ppermute | solution.py:208
  21.5 3.1 %copy-start.2 = (bf16[1024,256]{1,0:T(8,128)(2,1)}, bf16[1024,256]{1,0:T(8,128)(2,1)S(1)}, u32[]{:S(2)}) copy-start(bf16[1024,256]{1,0:T(8,128)(2,1)S(1)} %collective-permute-done.1.right_ref) | copy-start | bytes 1572868
  24.6 0.8 copy-start.3
  45.5 58.3 %collective-permute-start.2 = (f32[16,3,256]{2,1,0:T(4,128)S(1)}, f32[16,3,256]{2,1,0:T(4,128)S(1)}, u32[]{:S(2)}, u32[]{:S(2)}) collective-permute-start(f32[16,3,256]{2,1,0:T(4,128)S(1)} %get-tuple-element.16), channel_id=1, source_target_pairs={{0,2},{2,4},{4,6},{6,8},{8,10},{10,12},{12,14},{14,16},{16,18},{18... | collective-permute-start | bytes 147464 | tf_op jit(solution)/shard_map/ppermute | solution.py:116
  48.0 55.8 %collective-permute-start.3 = (f32[16,3,256]{2,1,0:T(4,128)S(1)}, f32[16,3,256]{2,1,0:T(4,128)S(1)}, u32[]{:S(2)}, u32[]{:S(2)}) collective-permute-start(f32[16,3,256]{2,1,0:T(4,128)S(1)} %get-tuple-element.17), channel_id=1, source_target_pairs={{2,0},{4,2},{6,4},{8,6},{10,8},{12,10},{14,12},{16,14},{18,16},{20... | collective-permute-start | bytes 147464 | tf_op jit(solution)/shard_map/ppermute | solution.py:117
  107.7 2.2 %copy-start.1 = (bf16[2048,1024]{1,0:T(8,128)(2,1)S(1)}, bf16[2048,1024]{1,0:T(8,128)(2,1)}, u32[]{:S(2)}) copy-start(bf16[2048,1024]{1,0:T(8,128)(2,1)} %get-tuple-element.4) | copy-start | bytes 12582916

commit v9 on v8

--- a/solution.py
+++ b/solution.py
@@ -128,14 +128,17 @@
     return fields
 
 
-def advance_kernel(adj_ref, left_ref, right_ref, cx_ref, cy_ref, cz_ref, coll_ref, fluid_ref, weigh_ref,
+def advance_kernel(adj_ref, left_ref, right_ref, cy_ref, coll_ref, fluid_ref, weigh_ref,
                    star_ref, part_ref):
     step = pl.program_id(0)
     g = adj_ref[...].astype(jnp.float32)
     rows, lanes = g.shape
-    cx = cx_ref[...]
+    spacing = 9.0 / NV1
+    centre = (NV1 - 1) / 2.0
+    row = step * rows + lax.broadcasted_iota(jnp.int32, (rows, 1), 0)
+    cx = ((row % NV1).astype(jnp.float32) - centre) * spacing
+    cz = ((row // NV1 % NV1).astype(jnp.float32) - centre) * spacing
     cy = cy_ref[...]
-    cz = cz_ref[...]
     half = NV1 // 2
     blank = jnp.zeros((rows // NV1, half, PLANE), jnp.float32)
     left = left_ref[...].astype(jnp.float32).reshape(rows // NV1, half, PLANE)
@@ -151,9 +154,9 @@
     y_prev = jnp.where(ypos == 0, 0.0, pltpu.roll(g, NZ, 1))
     z_next = jnp.where(zpos == NZ - 1, 0.0, pltpu.roll(g, lanes - 1, 1))
     z_prev = jnp.where(zpos == 0, 0.0, pltpu.roll(g, 1, 1))
-    term_x = jnp.maximum(cx, 0.0) * (after - g) + jnp.minimum(cx, 0.0) * (g - before)
-    term_y = jnp.maximum(cy, 0.0) * (y_next - g) + jnp.minimum(cy, 0.0) * (g - y_prev)
-    term_z = jnp.maximum(cz, 0.0) * (z_next - g) + jnp.minimum(cz, 0.0) * (g - z_prev)
+    term_x = jnp.abs(cx) * (jnp.where(cx > 0.0, after, before) - g)
+    term_y = jnp.abs(cy) * (jnp.where(cy > 0.0, y_next, y_prev) - g)
+    term_z = jnp.abs(cz) * (jnp.where(cz > 0.0, z_next, z_prev) - g)
     advect = term_x + term_y + term_z
     starred = (fluid_ref[...] * (g + TIME_STEP * (advect - coll_ref[...] * g))).astype(jnp.bfloat16)
     star_ref[...] = starred
@@ -168,7 +171,7 @@
         part_ref[...] += partial
 
 
-def advance(adj, left, right, cx, cy, cz, coll, fluid, weigh, block=256):
+def advance(adj, left, right, cy, coll, fluid, weigh, block=256):
     nv, lanes = adj.shape
     nm = weigh.shape[0]
     grid = (nv // block,)
@@ -182,8 +185,6 @@
             pl.BlockSpec((block // 2, PLANE), row),
             pl.BlockSpec((block // 2, PLANE), row),
             pl.BlockSpec((block, 1), row),
-            pl.BlockSpec((block, 1), row),
-            pl.BlockSpec((block, 1), row),
             pl.BlockSpec((1, lanes), fixed),
             pl.BlockSpec((1, lanes), fixed),
             pl.BlockSpec((nm, block), lambda i: (0, i)),
@@ -191,7 +192,7 @@
         out_specs=[pl.BlockSpec((block, lanes), row), pl.BlockSpec((nm, lanes), fixed)],
         out_shape=[jax.ShapeDtypeStruct((nv, lanes), jnp.bfloat16), jax.ShapeDtypeStruct((nm, lanes), jnp.float32)],
         compiler_params=pltpu.CompilerParams(dimension_semantics=("arbitrary",)),
-    )(adj, left, right, cx, cy, cz, coll, fluid, weigh)
+    )(adj, left, right, cy, coll, fluid, weigh)
 
 
 def on_device(adjoint, collision, solid, codes):
@@ -212,9 +213,7 @@
         flat,
         left,
         right,
-        speed_x.reshape(local_vel, 1),
         speed_y.reshape(local_vel, 1),
-        speed_z.reshape(local_vel, 1),
         collision.reshape(1, width * plane),
         fluid.reshape(1, width * plane),
         weigh,

time: 122 us -> 122 us (level)
  waiting for transfers between devices: 4.02 us -> 7.01 us
  other arithmetic: 12.5 us -> 10.2 us
    ppermute x1, waiting for transfers between devices: 0.93 us -> 3.92 us  [on_device(): right = lax.ppermute(head, SPACE_AXES, [(i + 1, i) for i in range(ends)])]
  transfers between devices with their start and end apart: 4 -> 4, of which waited for: 2 -> 2; matrix products, arithmetic and copies ran while one was open for 8% -> 5% of each run, Pallas kernels for 0% -> 0%
where the time goes in v9:
time: 122 us; the launch traced here: 121 us
  blocking collectives  53.3 us (44%)
  local copies, waits for them, and re-layouts  18.3 us (15%)
  Pallas kernels  16.1 us (13%)
  starting transfers between devices  13.5 us (11%)
  other arithmetic  10.2 us (8%)
  waiting for transfers between devices  7.01 us (6%)
  between operations  1.68 us (1%)
  matrix products  1.28 us (1%)
    psum x3, blocking collectives, on_device(): squares = lax.psum(squares, axis)  49.1 us
    pallas_call x1, Pallas kernels, advance(): pl.pallas_call(advance_kernel, grid=grid, in_specs=[pl.BlockSpec((block,...  16.1 us
    unnamed x20, local copies, waits for them, and re-layouts  8.2 us
    reshape x1, local copies, waits for them, and re-layouts, on_device(): return (corrected.reshape(local_vel, width, plane), fields * scale)  7.83 us
    ppermute x1, starting transfers between devices, sweep_all(): lax.ppermute(pack[:, :depth], SPACE_AXES, [(i + 1, i) for i in range(ends)])  5.18 us
    psum x1, blocking collectives, on_device(): moments = lax.psum(partial_value, 'vel').reshape(NM, width, plane)  4.19 us
    ppermute x1, waiting for transfers between devices, on_device(): right = lax.ppermute(head, SPACE_AXES, [(i + 1, i) for i in range(ends)])  3.92 us
    convert_element_type x1, other arithmetic, on_device(): (fluid.reshape(1, width * plane) * (starred_flat + added)).astype(jnp.bfl...  3.55 us
  transfers between devices with their start and end apart: 4, of which 2 were waited for; matrix products, arithmetic and copies ran while one was open for 5% of the time, Pallas kernels for 0%

profile of v9, /device:TPU:10, one launch (start us, length us, event | category | flops | bytes accessed | tf_op | source)
XLA Modules:
  0.0 121.4 jit_solution(9053759312663683999)
XLA Ops:
  0.7 3.2 %copy.24 = bf16[256,8,4,256]{3,1,2,0:T(8,128)(2,1)S(1)} copy(bf16[256,8,4,256]{3,2,1,0:T(4,128)(2,1)} %bitcast.54) | data formatting | bytes 8388608
  3.9 0.0 copy-start
  3.9 2.0 %copy-done = bf16[256,8,4,256]{3,1,2,0:T(8,128)(2,1)} copy-done((bf16[256,8,4,256]{3,1,2,0:T(8,128)(2,1)}, bf16[256,8,4,256]{3,1,2,0:T(8,128)(2,1)S(1)}, u32[]{:S(2)}) %copy-start) | copy-done | bytes 4194328
  5.9 0.1 slice_bitcast_fusion
  6.0 2.4 %collective-permute-start.1 = (bf16[1024,256]{1,0:T(8,128)(2,1)S(1)}, bf16[1024,256]{1,0:T(8,128)(2,1)S(1)}, u32[]{:S(2)}, u32[]{:S(2)}) collective-permute-start(bf16[1024,256]{1,0:T(8,128)(2,1)S(1)} %get-tuple-element.10), channel_id=1, source_target_pairs={{2,0},{4,2},{6,4},{8,6},{10,8},{12,10},{14,12},{16,14},{18,16},{20... | collective-permute-start | bytes 1572872 | tf_op jit(solution)/shard_map/ppermute | solution.py:210
  8.5 3.4 %collective-permute-start = (bf16[1024,256]{1,0:T(8,128)(2,1)S(1)}, bf16[1024,256]{1,0:T(8,128)(2,1)S(1)}, u32[]{:S(2)}, u32[]{:S(2)}) collective-permute-start(bf16[1024,256]{1,0:T(8,128)(2,1)S(1)} %get-tuple-element.11), channel_id=1, source_target_pairs={{0,2},{2,4},{4,6},{6,8},{8,10},{10,12},{12,14},{14,16},{16,18},{18... | collective-permute-start | bytes 1572872 | tf_op jit(solution)/shard_map/ppermute | solution.py:209
  11.9 0.6 fusion.49
  12.5 0.1 convert_add_fusion
  12.5 0.2 multiply_multiply_fusion.1
  12.7 0.2 subtract_multiply_fusion
  12.9 0.2 add_multiply_fusion
  13.0 0.1 broadcast_multiply_fusion.4
  13.2 0.1 fusion.81
  13.3 0.2 fusion.68
  13.5 0.2 stack.8
  13.7 1.3 %divide_convert_fusion.weigh_ref = bf16[13,2048]{1,0:T(8,128)(2,1)} fusion(f32[13,2048]{1,0:T(8,128)S(1)} %stack.8, f32[]{:T(128)} %fusion.49, f32[2048]{0:T(1024)S(1)} %get-tuple-element.24), kind=kLoop, calls=%fused_computation.31 | loop fusion | flops 79872 | bytes 167940 | tf_op jit(solution)/shard_map/convert_element_type | solution.py:84
  15.0 0.6 copy.25
  15.6 0.6 copy.26
  16.2 0.4 copy.18
  16.6 1.0 broadcast_multiply_fusion.cy_ref
  17.6 3.9 %collective-permute-done.1.right_ref = bf16[1024,256]{1,0:T(8,128)(2,1)S(1)} collective-permute-done((bf16[1024,256]{1,0:T(8,128)(2,1)S(1)}, bf16[1024,256]{1,0:T(8,128)(2,1)S(1)}, u32[]{:S(2)}, u32[]{:S(2)}) %collective-permute-start.1) | collective-permute-done | bytes 524320 | tf_op jit(solution)/shard_map/ppermute | solution.py:210
  21.6 3.1 %collective-permute-done.left_ref = bf16[1024,256]{1,0:T(8,128)(2,1)S(1)} collective-permute-done((bf16[1024,256]{1,0:T(8,128)(2,1)S(1)}, bf16[1024,256]{1,0:T(8,128)(2,1)S(1)}, u32[]{:S(2)}, u32[]{:S(2)}) %collective-permute-start) | collective-permute-done | bytes 524320 | tf_op jit(solution)/shard_map/ppermute | solution.py:209
  24.6 0.8 copy-done.3
  25.5 16.1 %shard_map.59 = (bf16[2048,1024]{1,0:T(8,128)(2,1)}, f32[13,1024]{1,0:T(8,128)}) custom-call(bf16[2048,1024]{1,0:T(8,128)(2,1)} %bitcast.53, bf16[1024,256]{1,0:T(8,128)(2,1)} %copy-done.3, bf16[1024,256]{1,0:T(8,128)(2,1)} %copy-done.2, f32[2048,1]{1,0:T(8,128)} %broadcast_multiply_fusion.cy_ref, f32[1,1024]{1,0:T(1,128)} %bitcast.63, f32[1,1024]{1,0:T(1,128)} %bitcast.64, ...), custom_call_target="tpu_custom_call" | custom-call | tf_op jit(solution)/shard_map/pallas_call | solution.py:180
  41.6 4.2 %psum.28 = f32[13,1024]{1,0:T(8,128)S(1)} all-reduce(f32[13,1024]{1,0:T(8,128)} %get-tuple-element.5), channel_id=1, replica_groups=mesh['sz'=8,'sy'=4,'sx'=4,'vel'=2] {'vel'}, use_global_device_ids=true, to_apply=%region_1.2 | all-reduce | flops 13312 | bytes 106496 | tf_op jit(solution)/shard_map/psum | solution.py:221
  45.9 2.5 %collective-permute-start.2 = (f32[16,3,256]{2,1,0:T(4,128)S(1)}, f32[16,3,256]{2,1,0:T(4,128)S(1)}, u32[]{:S(2)}, u32[]{:S(2)}) collective-permute-start(f32[16,3,256]{2,1,0:T(4,128)S(1)} %get-tuple-element.16), channel_id=1, source_target_pairs={{0,2},{2,4},{4,6},{6,8},{8,10},{10,12},{12,14},{14,16},{16,18},{18... | collective-permute-start | bytes 147464 | tf_op jit(solution)/shard_map/ppermute | solution.py:116
  48.4 5.2 %collective-permute-start.3 = (f32[16,3,256]{2,1,0:T(4,128)S(1)}, f32[16,3,256]{2,1,0:T(4,128)S(1)}, u32[]{:S(2)}, u32[]{:S(2)}) collective-permute-start(f32[16,3,256]{2,1,0:T(4,128)S(1)} %get-tuple-element.17), channel_id=1, source_target_pairs={{2,0},{4,2},{6,4},{8,6},{10,8},{12,10},{14,12},{16,14},{18,16},{20... | collective-permute-start | bytes 147464 | tf_op jit(solution)/shard_map/ppermute | solution.py:117
  53.6 0.6 fusion.79
  54.2 12.5 %psum.29 = f32[]{:T(128)} all-reduce(f32[]{:T(128)} %fusion.79), channel_id=1, replica_groups=mesh['sz'=8,'sy'=4,'sx'=4,'vel'=2] {'sx'}, use_global_device_ids=true, to_apply=%region_3.4 | all-reduce | flops 1 | bytes 8 | tf_op jit(solution)/shard_map/psum | solution.py:225
  66.6 9.7 %psum.30 = f32[]{:T(128)} all-reduce(f32[]{:T(128)} %psum.29), channel_id=1, replica_groups=mesh['sz'=8,'sy'=4,'sx'=4,'vel'=2] {'sy'}, use_global_device_ids=true, to_apply=%region_4.5 | all-reduce | flops 1 | bytes 8 | tf_op jit(solution)/shard_map/psum | solution.py:225
  76.3 26.9 %psum.31 = f32[]{:T(128)} all-reduce(f32[]{:T(128)} %psum.30), channel_id=1, replica_groups=mesh['sz'=8,'sy'=4,'sx'=4,'vel'=2] {'sz'}, use_global_device_ids=true, to_apply=%region_5.6 | all-reduce | flops 1 | bytes 8 | tf_op jit(solution)/shard_map/psum | solution.py:225
  103.9 0.0 collective-permute-done.2
  104.0 0.1 broadcast_multiply_fusion.2
  104.1 0.3 reshape.374
  104.4 0.5 fusion.2
  104.9 0.4 reshape.375
  105.4 0.2 reshape.376
  105.6 0.4 fusion.5
  106.0 0.3 reshape.377
  106.3 0.1 fusion.11
  106.4 0.2 reshape.378
  106.6 0.3 fusion.8
  106.9 0.2 reshape.379
  107.1 0.7 broadcast_multiply_fusion.3
  107.9 1.3 %fusion.15 = f32[2048,1024]{1,0:T(8,128)S(1)} fusion(bf16[13,1024]{1,0:T(8,128)(2,1)S(1)} %bitcast.55, f32[13,2048]{1,0:T(8,128)S(1)} %stack.8, f32[2048]{0:T(1024)S(1)} %get-tuple-element.23), kind=kOutput, calls=%fused_computation.42 | convolution fusion | flops 54579200 | bytes 8529920 | tf_op jit(solution)/shard_map/dot_general | solution.py:229
  109.2 0.9 copy-done.1
  110.1 3.5 %multiply_convert_fusion = bf16[2048,1024]{1,0:T(8,128)(2,1)} fusion(f32[2048,1024]{1,0:T(8,128)S(1)} %fusion.15, bf16[2048,1024]{1,0:T(8,128)(2,1)S(1)} %copy-done.1, f32[1024]{0:T(1024)S(1)} %bitcast.62), kind=kLoop, calls=%fused_computation | loop fusion | flops 8388608 | bytes 16781312 | tf_op jit(solution)/shard_map/convert_element_type | solution.py:230
  113.6 7.8 %reshape.381 = bf16[2048,4,256]{2,1,0:T(4,128)(2,1)} reshape(bf16[2048,1024]{1,0:T(8,128)(2,1)} %multiply_convert_fusion) | data formatting | bytes 8388608 | tf_op jit(solution)/shard_map/reshape | solution.py:231
  (32 shorter events, 0.4 us)
Async XLA Ops:
  0.6 12.9 %copy-start.6 = (s32[4,256]{1,0:T(4,128)S(1)}, s32[4,256]{1,0:T(4,128)}, u32[]{:S(2)}) copy-start(s32[4,256]{1,0:T(4,128)} %param.6) | copy-start | bytes 12292
  0.6 14.4 %copy-start.5 = (s32[4,256]{1,0:T(4,128)S(1)}, s32[4,256]{1,0:T(4,128)}, u32[]{:S(2)}) copy-start(s32[4,256]{1,0:T(4,128)} %param.7) | copy-start | bytes 12292
  0.7 14.4 %copy-start.4 = (f32[4,256]{1,0:T(4,128)S(1)}, f32[4,256]{1,0:T(4,128)}, u32[]{:S(2)}) copy-start(f32[4,256]{1,0:T(4,128)} %param.5) | copy-start | bytes 12292
  3.9 2.0 %copy-start = (bf16[256,8,4,256]{3,1,2,0:T(8,128)(2,1)}, bf16[256,8,4,256]{3,1,2,0:T(8,128)(2,1)S(1)}, u32[]{:S(2)}) copy-start(bf16[256,8,4,256]{3,1,2,0:T(8,128)(2,1)S(1)} %copy.24) | copy-start | bytes 12582916
  6.0 15.6 %collective-permute-start.1 = (bf16[1024,256]{1,0:T(8,128)(2,1)S(1)}, bf16[1024,256]{1,0:T(8,128)(2,1)S(1)}, u32[]{:S(2)}, u32[]{:S(2)}) collective-permute-start(bf16[1024,256]{1,0:T(8,128)(2,1)S(1)} %get-tuple-element.10), channel_id=1, source_target_pairs={{2,0},{4,2},{6,4},{8,6},{10,8},{12,10},{14,12},{16,14},{18,16},{20... | collective-permute-start | bytes 1572872 | tf_op jit(solution)/shard_map/ppermute | solution.py:210
  8.5 16.2 %collective-permute-start = (bf16[1024,256]{1,0:T(8,128)(2,1)S(1)}, bf16[1024,256]{1,0:T(8,128)(2,1)S(1)}, u32[]{:S(2)}, u32[]{:S(2)}) collective-permute-start(bf16[1024,256]{1,0:T(8,128)(2,1)S(1)} %get-tuple-element.11), channel_id=1, source_target_pairs={{0,2},{2,4},{4,6},{6,8},{8,10},{10,12},{12,14},{14,16},{16,18},{18... | collective-permute-start | bytes 1572872 | tf_op jit(solution)/shard_map/ppermute | solution.py:209
  21.6 3.1 %copy-start.2 = (bf16[1024,256]{1,0:T(8,128)(2,1)}, bf16[1024,256]{1,0:T(8,128)(2,1)S(1)}, u32[]{:S(2)}) copy-start(bf16[1024,256]{1,0:T(8,128)(2,1)S(1)} %collective-permute-done.1.right_ref) | copy-start | bytes 1572868
  24.6 0.8 copy-start.3
  45.9 58.1 %collective-permute-start.2 = (f32[16,3,256]{2,1,0:T(4,128)S(1)}, f32[16,3,256]{2,1,0:T(4,128)S(1)}, u32[]{:S(2)}, u32[]{:S(2)}) collective-permute-start(f32[16,3,256]{2,1,0:T(4,128)S(1)} %get-tuple-element.16), channel_id=1, source_target_pairs={{0,2},{2,4},{4,6},{6,8},{8,10},{10,12},{12,14},{14,16},{16,18},{18... | collective-permute-start | bytes 147464 | tf_op jit(solution)/shard_map/ppermute | solution.py:116
  48.4 55.6 %collective-permute-start.3 = (f32[16,3,256]{2,1,0:T(4,128)S(1)}, f32[16,3,256]{2,1,0:T(4,128)S(1)}, u32[]{:S(2)}, u32[]{:S(2)}) collective-permute-start(f32[16,3,256]{2,1,0:T(4,128)S(1)} %get-tuple-element.17), channel_id=1, source_target_pairs={{2,0},{4,2},{6,4},{8,6},{10,8},{12,10},{14,12},{16,14},{18,16},{20... | collective-permute-start | bytes 147464 | tf_op jit(solution)/shard_map/ppermute | solution.py:117
  107.9 2.2 %copy-start.1 = (bf16[2048,1024]{1,0:T(8,128)(2,1)S(1)}, bf16[2048,1024]{1,0:T(8,128)(2,1)}, u32[]{:S(2)}) copy-start(bf16[2048,1024]{1,0:T(8,128)(2,1)} %get-tuple-element.4) | copy-start | bytes 12582916

commit v10 on v9

--- a/solution.py
+++ b/solution.py
@@ -171,7 +171,7 @@
         part_ref[...] += partial
 
 
-def advance(adj, left, right, cy, coll, fluid, weigh, block=256):
+def advance(adj, left, right, cy, coll, fluid, weigh, block=128):
     nv, lanes = adj.shape
     nm = weigh.shape[0]
     grid = (nv // block,)

time: 122 us -> 124 us (1.016)
  Pallas kernels: 16.1 us -> 18 us
    pallas_call x1, Pallas kernels: 16.1 us -> 18 us  [advance(): pl.pallas_call(advance_kernel, grid=grid, in_specs=[pl.BlockSpec((block,...]
where the time goes in v10:
time: 124 us; the launch traced here: 123 us
  blocking collectives  53.3 us (43%)
  local copies, waits for them, and re-layouts  18.3 us (15%)
  Pallas kernels  18 us (15%)
  starting transfers between devices  13.5 us (11%)
  other arithmetic  10.2 us (8%)
  waiting for transfers between devices  7.01 us (6%)
  between operations  1.68 us (1%)
  matrix products  1.28 us (1%)
    psum x3, blocking collectives, on_device(): squares = lax.psum(squares, axis)  49.1 us
    pallas_call x1, Pallas kernels, advance(): pl.pallas_call(advance_kernel, grid=grid, in_specs=[pl.BlockSpec((block,...  18 us
    unnamed x20, local copies, waits for them, and re-layouts  8.19 us
    reshape x1, local copies, waits for them, and re-layouts, on_device(): return (corrected.reshape(local_vel, width, plane), fields * scale)  7.83 us
    ppermute x1, starting transfers between devices, sweep_all(): lax.ppermute(pack[:, :depth], SPACE_AXES, [(i + 1, i) for i in range(ends)])  5.18 us
    psum x1, blocking collectives, on_device(): moments = lax.psum(partial_value, 'vel').reshape(NM, width, plane)  4.19 us
    ppermute x1, waiting for transfers between devices, on_device(): right = lax.ppermute(head, SPACE_AXES, [(i + 1, i) for i in range(ends)])  3.92 us
    convert_element_type x1, other arithmetic, on_device(): (fluid.reshape(1, width * plane) * (starred_flat + added)).astype(jnp.bfl...  3.55 us
  transfers between devices with their start and end apart: 4, of which 2 were waited for; matrix products, arithmetic and copies ran while one was open for 5% of the time, Pallas kernels for 0%

profile of v10, /device:TPU:10, one launch (start us, length us, event | category | flops | bytes accessed | tf_op | source)
XLA Modules:
  0.0 123.3 jit_solution(3147290017584366502)
XLA Ops:
  0.7 3.2 %copy.24 = bf16[256,8,4,256]{3,1,2,0:T(8,128)(2,1)S(1)} copy(bf16[256,8,4,256]{3,2,1,0:T(4,128)(2,1)} %bitcast.54) | data formatting | bytes 8388608
  3.9 0.0 copy-start
  3.9 2.0 %copy-done = bf16[256,8,4,256]{3,1,2,0:T(8,128)(2,1)} copy-done((bf16[256,8,4,256]{3,1,2,0:T(8,128)(2,1)}, bf16[256,8,4,256]{3,1,2,0:T(8,128)(2,1)S(1)}, u32[]{:S(2)}) %copy-start) | copy-done | bytes 4194328
  5.9 0.1 slice_bitcast_fusion
  6.0 2.4 %collective-permute-start.1 = (bf16[1024,256]{1,0:T(8,128)(2,1)S(1)}, bf16[1024,256]{1,0:T(8,128)(2,1)S(1)}, u32[]{:S(2)}, u32[]{:S(2)}) collective-permute-start(bf16[1024,256]{1,0:T(8,128)(2,1)S(1)} %get-tuple-element.10), channel_id=1, source_target_pairs={{2,0},{4,2},{6,4},{8,6},{10,8},{12,10},{14,12},{16,14},{18,16},{20... | collective-permute-start | bytes 1572872 | tf_op jit(solution)/shard_map/ppermute | solution.py:210
  8.5 3.4 %collective-permute-start = (bf16[1024,256]{1,0:T(8,128)(2,1)S(1)}, bf16[1024,256]{1,0:T(8,128)(2,1)S(1)}, u32[]{:S(2)}, u32[]{:S(2)}) collective-permute-start(bf16[1024,256]{1,0:T(8,128)(2,1)S(1)} %get-tuple-element.11), channel_id=1, source_target_pairs={{0,2},{2,4},{4,6},{6,8},{8,10},{10,12},{12,14},{14,16},{16,18},{18... | collective-permute-start | bytes 1572872 | tf_op jit(solution)/shard_map/ppermute | solution.py:209
  11.9 0.6 fusion.49
  12.5 0.1 convert_add_fusion
  12.5 0.2 multiply_multiply_fusion.1
  12.7 0.2 subtract_multiply_fusion
  12.9 0.2 add_multiply_fusion
  13.0 0.1 broadcast_multiply_fusion.4
  13.2 0.1 fusion.81
  13.3 0.2 fusion.68
  13.5 0.2 stack.8
  13.7 1.3 %divide_convert_fusion.weigh_ref = bf16[13,2048]{1,0:T(8,128)(2,1)} fusion(f32[13,2048]{1,0:T(8,128)S(1)} %stack.8, f32[]{:T(128)} %fusion.49, f32[2048]{0:T(1024)S(1)} %get-tuple-element.24), kind=kLoop, calls=%fused_computation.31 | loop fusion | flops 79872 | bytes 167940 | tf_op jit(solution)/shard_map/convert_element_type | solution.py:84
  15.0 0.6 copy.25
  15.6 0.6 copy.26
  16.2 0.4 copy.18
  16.6 1.0 broadcast_multiply_fusion.cy_ref
  17.6 3.9 %collective-permute-done.1.right_ref = bf16[1024,256]{1,0:T(8,128)(2,1)S(1)} collective-permute-done((bf16[1024,256]{1,0:T(8,128)(2,1)S(1)}, bf16[1024,256]{1,0:T(8,128)(2,1)S(1)}, u32[]{:S(2)}, u32[]{:S(2)}) %collective-permute-start.1) | collective-permute-done | bytes 524320 | tf_op jit(solution)/shard_map/ppermute | solution.py:210
  21.6 3.1 %collective-permute-done.left_ref = bf16[1024,256]{1,0:T(8,128)(2,1)S(1)} collective-permute-done((bf16[1024,256]{1,0:T(8,128)(2,1)S(1)}, bf16[1024,256]{1,0:T(8,128)(2,1)S(1)}, u32[]{:S(2)}, u32[]{:S(2)}) %collective-permute-start) | collective-permute-done | bytes 524320 | tf_op jit(solution)/shard_map/ppermute | solution.py:209
  24.6 0.8 copy-done.3
  25.5 18.0 %shard_map.59 = (bf16[2048,1024]{1,0:T(8,128)(2,1)}, f32[13,1024]{1,0:T(8,128)}) custom-call(bf16[2048,1024]{1,0:T(8,128)(2,1)} %bitcast.53, bf16[1024,256]{1,0:T(8,128)(2,1)} %copy-done.3, bf16[1024,256]{1,0:T(8,128)(2,1)} %copy-done.2, f32[2048,1]{1,0:T(8,128)} %broadcast_multiply_fusion.cy_ref, f32[1,1024]{1,0:T(1,128)} %bitcast.63, f32[1,1024]{1,0:T(1,128)} %bitcast.64, ...), custom_call_target="tpu_custom_call" | custom-call | tf_op jit(solution)/shard_map/pallas_call | solution.py:180
  43.5 4.2 %psum.28 = f32[13,1024]{1,0:T(8,128)S(1)} all-reduce(f32[13,1024]{1,0:T(8,128)} %get-tuple-element.5), channel_id=1, replica_groups=mesh['sz'=8,'sy'=4,'sx'=4,'vel'=2] {'vel'}, use_global_device_ids=true, to_apply=%region_1.2 | all-reduce | flops 13312 | bytes 106496 | tf_op jit(solution)/shard_map/psum | solution.py:221
  47.8 2.5 %collective-permute-start.2 = (f32[16,3,256]{2,1,0:T(4,128)S(1)}, f32[16,3,256]{2,1,0:T(4,128)S(1)}, u32[]{:S(2)}, u32[]{:S(2)}) collective-permute-start(f32[16,3,256]{2,1,0:T(4,128)S(1)} %get-tuple-element.16), channel_id=1, source_target_pairs={{0,2},{2,4},{4,6},{6,8},{8,10},{10,12},{12,14},{14,16},{16,18},{18... | collective-permute-start | bytes 147464 | tf_op jit(solution)/shard_map/ppermute | solution.py:116
  50.3 5.2 %collective-permute-start.3 = (f32[16,3,256]{2,1,0:T(4,128)S(1)}, f32[16,3,256]{2,1,0:T(4,128)S(1)}, u32[]{:S(2)}, u32[]{:S(2)}) collective-permute-start(f32[16,3,256]{2,1,0:T(4,128)S(1)} %get-tuple-element.17), channel_id=1, source_target_pairs={{2,0},{4,2},{6,4},{8,6},{10,8},{12,10},{14,12},{16,14},{18,16},{20... | collective-permute-start | bytes 147464 | tf_op jit(solution)/shard_map/ppermute | solution.py:117
  55.5 0.6 fusion.79
  56.1 12.5 %psum.29 = f32[]{:T(128)} all-reduce(f32[]{:T(128)} %fusion.79), channel_id=1, replica_groups=mesh['sz'=8,'sy'=4,'sx'=4,'vel'=2] {'sx'}, use_global_device_ids=true, to_apply=%region_3.4 | all-reduce | flops 1 | bytes 8 | tf_op jit(solution)/shard_map/psum | solution.py:225
  68.5 9.7 %psum.30 = f32[]{:T(128)} all-reduce(f32[]{:T(128)} %psum.29), channel_id=1, replica_groups=mesh['sz'=8,'sy'=4,'sx'=4,'vel'=2] {'sy'}, use_global_device_ids=true, to_apply=%region_4.5 | all-reduce | flops 1 | bytes 8 | tf_op jit(solution)/shard_map/psum | solution.py:225
  78.2 26.9 %psum.31 = f32[]{:T(128)} all-reduce(f32[]{:T(128)} %psum.30), channel_id=1, replica_groups=mesh['sz'=8,'sy'=4,'sx'=4,'vel'=2] {'sz'}, use_global_device_ids=true, to_apply=%region_5.6 | all-reduce | flops 1 | bytes 8 | tf_op jit(solution)/shard_map/psum | solution.py:225
  105.8 0.0 collective-permute-done.2
  106.0 0.1 broadcast_multiply_fusion.2
  106.1 0.3 reshape.374
  106.3 0.5 fusion.2
  106.8 0.4 reshape.375
  107.3 0.2 reshape.376
  107.5 0.4 fusion.5
  107.9 0.3 reshape.377
  108.2 0.1 fusion.11
  108.3 0.2 reshape.378
  108.5 0.3 fusion.8
  108.8 0.2 reshape.379
  109.1 0.7 broadcast_multiply_fusion.3
  109.8 1.3 %fusion.15 = f32[2048,1024]{1,0:T(8,128)S(1)} fusion(bf16[13,1024]{1,0:T(8,128)(2,1)S(1)} %bitcast.55, f32[13,2048]{1,0:T(8,128)S(1)} %stack.8, f32[2048]{0:T(1024)S(1)} %get-tuple-element.23), kind=kOutput, calls=%fused_computation.42 | convolution fusion | flops 54579200 | bytes 8529920 | tf_op jit(solution)/shard_map/dot_general | solution.py:229
  111.1 0.9 copy-done.1
  112.0 3.5 %multiply_convert_fusion = bf16[2048,1024]{1,0:T(8,128)(2,1)} fusion(f32[2048,1024]{1,0:T(8,128)S(1)} %fusion.15, bf16[2048,1024]{1,0:T(8,128)(2,1)S(1)} %copy-done.1, f32[1024]{0:T(1024)S(1)} %bitcast.62), kind=kLoop, calls=%fused_computation | loop fusion | flops 8388608 | bytes 16781312 | tf_op jit(solution)/shard_map/convert_element_type | solution.py:230
  115.5 7.8 %reshape.381 = bf16[2048,4,256]{2,1,0:T(4,128)(2,1)} reshape(bf16[2048,1024]{1,0:T(8,128)(2,1)} %multiply_convert_fusion) | data formatting | bytes 8388608 | tf_op jit(solution)/shard_map/reshape | solution.py:231
  (32 shorter events, 0.4 us)
Async XLA Ops:
  0.6 12.9 %copy-start.6 = (s32[4,256]{1,0:T(4,128)S(1)}, s32[4,256]{1,0:T(4,128)}, u32[]{:S(2)}) copy-start(s32[4,256]{1,0:T(4,128)} %param.6) | copy-start | bytes 12292
  0.6 14.4 %copy-start.5 = (s32[4,256]{1,0:T(4,128)S(1)}, s32[4,256]{1,0:T(4,128)}, u32[]{:S(2)}) copy-start(s32[4,256]{1,0:T(4,128)} %param.7) | copy-start | bytes 12292
  0.7 14.4 %copy-start.4 = (f32[4,256]{1,0:T(4,128)S(1)}, f32[4,256]{1,0:T(4,128)}, u32[]{:S(2)}) copy-start(f32[4,256]{1,0:T(4,128)} %param.5) | copy-start | bytes 12292
  3.9 2.0 %copy-start = (bf16[256,8,4,256]{3,1,2,0:T(8,128)(2,1)}, bf16[256,8,4,256]{3,1,2,0:T(8,128)(2,1)S(1)}, u32[]{:S(2)}) copy-start(bf16[256,8,4,256]{3,1,2,0:T(8,128)(2,1)S(1)} %copy.24) | copy-start | bytes 12582916
  6.0 15.6 %collective-permute-start.1 = (bf16[1024,256]{1,0:T(8,128)(2,1)S(1)}, bf16[1024,256]{1,0:T(8,128)(2,1)S(1)}, u32[]{:S(2)}, u32[]{:S(2)}) collective-permute-start(bf16[1024,256]{1,0:T(8,128)(2,1)S(1)} %get-tuple-element.10), channel_id=1, source_target_pairs={{2,0},{4,2},{6,4},{8,6},{10,8},{12,10},{14,12},{16,14},{18,16},{20... | collective-permute-start | bytes 1572872 | tf_op jit(solution)/shard_map/ppermute | solution.py:210
  8.5 16.2 %collective-permute-start = (bf16[1024,256]{1,0:T(8,128)(2,1)S(1)}, bf16[1024,256]{1,0:T(8,128)(2,1)S(1)}, u32[]{:S(2)}, u32[]{:S(2)}) collective-permute-start(bf16[1024,256]{1,0:T(8,128)(2,1)S(1)} %get-tuple-element.11), channel_id=1, source_target_pairs={{0,2},{2,4},{4,6},{6,8},{8,10},{10,12},{12,14},{14,16},{16,18},{18... | collective-permute-start | bytes 1572872 | tf_op jit(solution)/shard_map/ppermute | solution.py:209
  21.6 3.1 %copy-start.2 = (bf16[1024,256]{1,0:T(8,128)(2,1)}, bf16[1024,256]{1,0:T(8,128)(2,1)S(1)}, u32[]{:S(2)}) copy-start(bf16[1024,256]{1,0:T(8,128)(2,1)S(1)} %collective-permute-done.1.right_ref) | copy-start | bytes 1572868
  24.6 0.8 copy-start.3
  47.8 58.1 %collective-permute-start.2 = (f32[16,3,256]{2,1,0:T(4,128)S(1)}, f32[16,3,256]{2,1,0:T(4,128)S(1)}, u32[]{:S(2)}, u32[]{:S(2)}) collective-permute-start(f32[16,3,256]{2,1,0:T(4,128)S(1)} %get-tuple-element.16), channel_id=1, source_target_pairs={{0,2},{2,4},{4,6},{6,8},{8,10},{10,12},{12,14},{14,16},{16,18},{18... | collective-permute-start | bytes 147464 | tf_op jit(solution)/shard_map/ppermute | solution.py:116
  50.3 55.6 %collective-permute-start.3 = (f32[16,3,256]{2,1,0:T(4,128)S(1)}, f32[16,3,256]{2,1,0:T(4,128)S(1)}, u32[]{:S(2)}, u32[]{:S(2)}) collective-permute-start(f32[16,3,256]{2,1,0:T(4,128)S(1)} %get-tuple-element.17), channel_id=1, source_target_pairs={{2,0},{4,2},{6,4},{8,6},{10,8},{12,10},{14,12},{16,14},{18,16},{20... | collective-permute-start | bytes 147464 | tf_op jit(solution)/shard_map/ppermute | solution.py:117
  109.8 2.2 %copy-start.1 = (bf16[2048,1024]{1,0:T(8,128)(2,1)S(1)}, bf16[2048,1024]{1,0:T(8,128)(2,1)}, u32[]{:S(2)}) copy-start(bf16[2048,1024]{1,0:T(8,128)(2,1)} %get-tuple-element.4) | copy-start | bytes 12582916

commit v11 on v8

--- a/solution.py
+++ b/solution.py
@@ -194,6 +194,33 @@
     )(adj, left, right, cx, cy, cz, coll, fluid, weigh)
 
 
+def correct_kernel(star_ref, lift_ref, delta_ref, fluid_ref, out_ref):
+    added = jnp.dot(lift_ref[...], delta_ref[...], preferred_element_type=jnp.float32)
+    corrected = (fluid_ref[...] * (star_ref[...].astype(jnp.float32) + added)).astype(jnp.bfloat16)
+    for x in range(out_ref.shape[1]):
+        out_ref[:, x, :] = corrected[:, x * PLANE : (x + 1) * PLANE]
+
+
+def correct(starred, lift, delta, fluid, width, block=256):
+    nv, lanes = starred.shape
+    nm = lift.shape[1]
+    row = lambda i: (i, 0)
+    fixed = lambda i: (0, 0)
+    return pl.pallas_call(
+        correct_kernel,
+        grid=(nv // block,),
+        in_specs=[
+            pl.BlockSpec((block, lanes), row),
+            pl.BlockSpec((block, nm), row),
+            pl.BlockSpec((nm, lanes), fixed),
+            pl.BlockSpec((1, lanes), fixed),
+        ],
+        out_specs=pl.BlockSpec((block, width, PLANE), lambda i: (i, 0, 0)),
+        out_shape=jax.ShapeDtypeStruct((nv, width, PLANE), jnp.bfloat16),
+        compiler_params=pltpu.CompilerParams(dimension_semantics=("arbitrary",)),
+    )(starred, lift, delta, fluid)
+
+
 def on_device(adjoint, collision, solid, codes):
     local_vel, width, plane = adjoint.shape
     start = lax.axis_index("vel") * local_vel
@@ -227,9 +254,8 @@
     scale = lax.rsqrt(squares / cells_all + 1e-06)
     fields = sweep_all(moments, fluid, collision, wall_level(codes))
     delta = ((fields - moments) * scale).astype(jnp.bfloat16).reshape(NM, width * plane)
-    added = jnp.dot(lift, delta, preferred_element_type=jnp.float32)
-    corrected = (fluid.reshape(1, width * plane) * (starred_flat + added)).astype(jnp.bfloat16)
-    return (corrected.reshape(local_vel, width, plane), fields * scale)
+    corrected = correct(starred_flat, lift, delta, fluid.reshape(1, width * plane), width)
+    return (corrected, fields * scale)
 
 
 def axis_count(axes):

time: 122 us -> 114 us (0.934)
  Pallas kernels: 15.8 us -> 25.8 us
  local copies, waits for them, and re-layouts: 19 us -> 12 us
  blocking collectives: 53.5 us -> 49.4 us
  other arithmetic: 12.5 us -> 8.94 us
  starting transfers between devices: 13.5 us -> 11.7 us
  matrix products: 1.28 us -> 0 us
    pallas_call x0 -> x1, Pallas kernels: none -> 10.1 us  [correct(): pl.pallas_call(correct_kernel, grid=(nv // block,), in_specs=[pl.BlockSpe...]
    reshape x1 -> x0, local copies, waits for them, and re-layouts: 7.83 us -> none  [on_device(): return (corrected.reshape(local_vel, width, plane), fields * scale)]
    psum x3, blocking collectives: 49.3 us -> 45.2 us  [on_device(): squares = lax.psum(squares, axis)]
    convert_element_type x2 -> x1, other arithmetic: 4.83 us -> 1.29 us  [tables(): jnp.transpose(0.1 * basis * jnp.exp(-0.25 * speed)).astype(jnp.bfloat16)]
    ppermute x1, starting transfers between devices: 5.18 us -> 2.74 us  [sweep_all(): lax.ppermute(pack[:, :depth], SPACE_AXES, [(i + 1, i) for i in range(ends)])]
    ppermute x1, waiting for transfers between devices: 0.93 us -> 3.12 us  [on_device(): right = lax.ppermute(head, SPACE_AXES, [(i + 1, i) for i in range(ends)])]
    ppermute x1, waiting for transfers between devices: 3.08 us -> 0.94 us  [on_device(): left = lax.ppermute(tail, SPACE_AXES, [(i, i + 1) for i in range(ends)])]
    dot_general x1 -> x0, matrix products: 1.28 us -> none  [on_device(): added = jnp.dot(lift, delta, preferred_element_type=jnp.float32)]
  transfers between devices with their start and end apart: 4 -> 4, of which waited for: 2 -> 2; matrix products, arithmetic and copies ran while one was open for 8% -> 9% of each run, Pallas kernels for 0% -> 0%
where the time goes in v11:
time: 114 us
  blocking collectives  49.4 us (43%)
  Pallas kernels  25.8 us (23%)
  local copies, waits for them, and re-layouts  12 us (11%)
  starting transfers between devices  11.7 us (10%)
  other arithmetic  8.94 us (8%)
  waiting for transfers between devices  4.07 us (4%)
  between operations  1.65 us (1%)
    psum x3, blocking collectives, on_device(): squares = lax.psum(squares, axis)  45.2 us
    pallas_call x1, Pallas kernels, advance(): pl.pallas_call(advance_kernel, grid=grid, in_specs=[pl.BlockSpec((block,...  15.8 us
    pallas_call x1, Pallas kernels, correct(): pl.pallas_call(correct_kernel, grid=(nv // block,), in_specs=[pl.BlockSpe...  10.1 us
    unnamed x17, local copies, waits for them, and re-layouts  7.92 us
    psum x1, blocking collectives, on_device(): moments = lax.psum(partial_value, 'vel').reshape(NM, width, plane)  4.2 us
    ppermute x1, starting transfers between devices, on_device(): left = lax.ppermute(tail, SPACE_AXES, [(i, i + 1) for i in range(ends)])  3.4 us
    ppermute x1, waiting for transfers between devices, on_device(): right = lax.ppermute(head, SPACE_AXES, [(i + 1, i) for i in range(ends)])  3.12 us
    ppermute x1, starting transfers between devices, sweep_all(): lax.ppermute(pack[:, width - depth:], SPACE_AXES, [(i, i + 1) for i in ra...  3.11 us
  transfers between devices with their start and end apart: 4, of which 2 were waited for; matrix products, arithmetic and copies ran while one was open for 9% of the time, Pallas kernels for 0%

profile of v11, /device:TPU:10, one launch (start us, length us, event | category | flops | bytes accessed | tf_op | source)
XLA Modules:
  0.0 113.6 jit_solution(2723524938464353016)
XLA Ops:
  0.6 3.2 %copy.34 = bf16[256,8,4,256]{3,1,2,0:T(8,128)(2,1)S(1)} copy(bf16[256,8,4,256]{3,2,1,0:T(4,128)(2,1)} %bitcast.51) | data formatting | bytes 8388608
  3.9 2.0 %copy-done = bf16[256,8,4,256]{3,1,2,0:T(8,128)(2,1)} copy-done((bf16[256,8,4,256]{3,1,2,0:T(8,128)(2,1)}, bf16[256,8,4,256]{3,1,2,0:T(8,128)(2,1)S(1)}, u32[]{:S(2)}) %copy-start) | copy-done | bytes 4194328
  5.9 0.1 slice_bitcast_fusion
  6.0 3.4 %collective-permute-start = (bf16[1024,256]{1,0:T(8,128)(2,1)S(1)}, bf16[1024,256]{1,0:T(8,128)(2,1)S(1)}, u32[]{:S(2)}, u32[]{:S(2)}) collective-permute-start(bf16[1024,256]{1,0:T(8,128)(2,1)S(1)} %get-tuple-element.11), channel_id=1, source_target_pairs={{0,2},{2,4},{4,6},{6,8},{8,10},{10,12},{12,14},{14,16},{16,18},{18... | collective-permute-start | bytes 1572872 | tf_op jit(solution)/shard_map/ppermute | solution.py:235
  9.4 2.4 %collective-permute-start.1 = (bf16[1024,256]{1,0:T(8,128)(2,1)S(1)}, bf16[1024,256]{1,0:T(8,128)(2,1)S(1)}, u32[]{:S(2)}, u32[]{:S(2)}) collective-permute-start(bf16[1024,256]{1,0:T(8,128)(2,1)S(1)} %get-tuple-element.10), channel_id=1, source_target_pairs={{2,0},{4,2},{6,4},{8,6},{10,8},{12,10},{14,12},{16,14},{18,16},{20... | collective-permute-start | bytes 1572872 | tf_op jit(solution)/shard_map/ppermute | solution.py:236
  11.8 0.2 fusion.70
  12.0 0.2 multiply_multiply_fusion.1
  12.2 0.2 subtract_multiply_fusion
  12.3 0.2 add_multiply_fusion
  12.5 0.1 broadcast_multiply_fusion.6
  12.6 0.1 fusion.86
  12.8 0.6 fusion.47
  13.4 0.1 fusion.65
  13.6 0.4 copy.30
  14.0 1.1 broadcast_multiply_fusion.cz_ref
  15.0 0.4 copy.26
  15.4 1.0 broadcast_multiply_fusion.2.cx_ref
  16.5 0.2 stack.8
  16.7 1.3 %multiply_convert_fusion = (bf16[13,2048]{1,0:T(8,128)(2,1)S(1)}, bf16[13,2048]{1,0:T(8,128)(2,1)}) fusion(f32[13,2048]{1,0:T(8,128)S(1)} %stack.8, f32[2048]{0:T(1024)S(1)} %get-tuple-element.26, f32[]{:T(128)} %fusion.47, f32[2048]{0:T(1024)S(1)} %get-tuple-element.27), kind=kLoop, calls=%fused_computation.31 | loop fusion | flops 133120 | bytes 229380 | tf_op jit(solution)/shard_map/convert_element_type | solution.py:85
  18.0 0.4 copy.28
  18.3 0.6 copy.36
  18.9 0.6 copy.35
  19.5 1.1 broadcast_multiply_fusion.1.cy_ref
  20.6 0.9 collective-permute-done.left_ref
  21.5 3.1 %collective-permute-done.1.right_ref = bf16[1024,256]{1,0:T(8,128)(2,1)S(1)} collective-permute-done((bf16[1024,256]{1,0:T(8,128)(2,1)S(1)}, bf16[1024,256]{1,0:T(8,128)(2,1)S(1)}, u32[]{:S(2)}, u32[]{:S(2)}) %collective-permute-start.1) | collective-permute-done | bytes 524320 | tf_op jit(solution)/shard_map/ppermute | solution.py:236
  24.7 0.8 copy-done.2
  25.5 15.8 %shard_map.59 = (bf16[2048,1024]{1,0:T(8,128)(2,1)}, f32[13,1024]{1,0:T(8,128)}) custom-call(bf16[2048,1024]{1,0:T(8,128)(2,1)} %bitcast.50, bf16[1024,256]{1,0:T(8,128)(2,1)} %copy-done.1, bf16[1024,256]{1,0:T(8,128)(2,1)} %copy-done.2, f32[2048,1]{1,0:T(8,128)} %broadcast_multiply_fusion.2.cx_ref, f32[2048,1]{1,0:T(8,128)} %broadcast_multiply_fusion.1.cy_ref, ...), custom_call_target="tpu_custom_call" | custom-call | tf_op jit(solution)/shard_map/pallas_call | solution.py:177
  41.3 4.2 %psum.28 = f32[13,1024]{1,0:T(8,128)S(1)} all-reduce(f32[13,1024]{1,0:T(8,128)} %get-tuple-element.5), channel_id=1, replica_groups=mesh['sz'=8,'sy'=4,'sx'=4,'vel'=2] {'vel'}, use_global_device_ids=true, to_apply=%region_1.2 | all-reduce | flops 13312 | bytes 106496 | tf_op jit(solution)/shard_map/psum | solution.py:249
  45.6 3.1 %collective-permute-start.2 = (f32[16,3,256]{2,1,0:T(4,128)S(1)}, f32[16,3,256]{2,1,0:T(4,128)S(1)}, u32[]{:S(2)}, u32[]{:S(2)}) collective-permute-start(f32[16,3,256]{2,1,0:T(4,128)S(1)} %get-tuple-element.18), channel_id=1, source_target_pairs={{0,2},{2,4},{4,6},{6,8},{8,10},{10,12},{12,14},{14,16},{16,18},{18... | collective-permute-start | bytes 147464 | tf_op jit(solution)/shard_map/ppermute | solution.py:116
  48.7 2.7 %collective-permute-start.3 = (f32[16,3,256]{2,1,0:T(4,128)S(1)}, f32[16,3,256]{2,1,0:T(4,128)S(1)}, u32[]{:S(2)}, u32[]{:S(2)}) collective-permute-start(f32[16,3,256]{2,1,0:T(4,128)S(1)} %get-tuple-element.19), channel_id=1, source_target_pairs={{2,0},{4,2},{6,4},{8,6},{10,8},{12,10},{14,12},{16,14},{18,16},{20... | collective-permute-start | bytes 147464 | tf_op jit(solution)/shard_map/ppermute | solution.py:117
  51.4 0.6 fusion.84
  52.0 11.6 %psum.29 = f32[]{:T(128)} all-reduce(f32[]{:T(128)} %fusion.84), channel_id=1, replica_groups=mesh['sz'=8,'sy'=4,'sx'=4,'vel'=2] {'sx'}, use_global_device_ids=true, to_apply=%region_3.4 | all-reduce | flops 1 | bytes 8 | tf_op jit(solution)/shard_map/psum | solution.py:253
  63.6 9.6 %psum.30 = f32[]{:T(128)} all-reduce(f32[]{:T(128)} %psum.29), channel_id=1, replica_groups=mesh['sz'=8,'sy'=4,'sx'=4,'vel'=2] {'sy'}, use_global_device_ids=true, to_apply=%region_4.5 | all-reduce | flops 1 | bytes 8 | tf_op jit(solution)/shard_map/psum | solution.py:253
  73.2 1.1 copy.31
  74.3 24.0 %psum.31 = f32[]{:T(128)} all-reduce(f32[]{:T(128)} %psum.30), channel_id=1, replica_groups=mesh['sz'=8,'sy'=4,'sx'=4,'vel'=2] {'sz'}, use_global_device_ids=true, to_apply=%region_5.6 | all-reduce | flops 1 | bytes 8 | tf_op jit(solution)/shard_map/psum | solution.py:253
  99.2 0.3 reshape.474
  99.5 0.5 fusion.2
  100.0 0.4 reshape.475
  100.5 0.2 reshape.476
  100.7 0.4 fusion.5
  101.1 0.3 reshape.477
  101.4 0.1 fusion.11
  101.5 0.2 reshape.478
  101.7 0.3 fusion.8
  102.0 0.2 reshape.479
  102.2 0.7 broadcast_multiply_fusion.5
  102.9 0.6 copy.37
  103.5 10.1 %shard_map.60 = bf16[2048,4,256]{2,1,0:T(4,128)(2,1)} custom-call(bf16[2048,1024]{1,0:T(8,128)(2,1)} %get-tuple-element.4.star_ref, bf16[2048,13]{1,0:T(8,128)(2,1)} %bitcast.52, bf16[13,1024]{1,0:T(8,128)(2,1)} %bitcast.53, f32[1,1024]{1,0:T(1,128)} %bitcast.61), custom_call_target="tpu_custom_call" | custom-call | tf_op jit(solution)/shard_map/pallas_call | solution.py:209
  (33 shorter events, 0.5 us)
Async XLA Ops:
  3.9 2.0 %copy-start = (bf16[256,8,4,256]{3,1,2,0:T(8,128)(2,1)}, bf16[256,8,4,256]{3,1,2,0:T(8,128)(2,1)S(1)}, u32[]{:S(2)}) copy-start(bf16[256,8,4,256]{3,1,2,0:T(8,128)(2,1)S(1)} %copy.34) | copy-start | bytes 12582916
  5.9 10.6 %copy-start.4 = (s32[4,256]{1,0:T(4,128)S(1)}, s32[4,256]{1,0:T(4,128)}, u32[]{:S(2)}) copy-start(s32[4,256]{1,0:T(4,128)} %param.6) | copy-start | bytes 12292
  5.9 12.1 %copy-start.5 = (s32[4,256]{1,0:T(4,128)S(1)}, s32[4,256]{1,0:T(4,128)}, u32[]{:S(2)}) copy-start(s32[4,256]{1,0:T(4,128)} %param.7) | copy-start | bytes 12292
  6.0 13.0 %copy-start.3 = (f32[4,256]{1,0:T(4,128)S(1)}, f32[4,256]{1,0:T(4,128)}, u32[]{:S(2)}) copy-start(f32[4,256]{1,0:T(4,128)} %param.5) | copy-start | bytes 12292
  6.0 15.6 %collective-permute-start = (bf16[1024,256]{1,0:T(8,128)(2,1)S(1)}, bf16[1024,256]{1,0:T(8,128)(2,1)S(1)}, u32[]{:S(2)}, u32[]{:S(2)}) collective-permute-start(bf16[1024,256]{1,0:T(8,128)(2,1)S(1)} %get-tuple-element.11), channel_id=1, source_target_pairs={{0,2},{2,4},{4,6},{6,8},{8,10},{10,12},{12,14},{14,16},{16,18},{18... | collective-permute-start | bytes 1572872 | tf_op jit(solution)/shard_map/ppermute | solution.py:235
  9.4 15.3 %collective-permute-start.1 = (bf16[1024,256]{1,0:T(8,128)(2,1)S(1)}, bf16[1024,256]{1,0:T(8,128)(2,1)S(1)}, u32[]{:S(2)}, u32[]{:S(2)}) collective-permute-start(bf16[1024,256]{1,0:T(8,128)(2,1)S(1)} %get-tuple-element.10), channel_id=1, source_target_pairs={{2,0},{4,2},{6,4},{8,6},{10,8},{12,10},{14,12},{16,14},{18,16},{20... | collective-permute-start | bytes 1572872 | tf_op jit(solution)/shard_map/ppermute | solution.py:236
  21.5 3.1 %copy-start.1 = (bf16[1024,256]{1,0:T(8,128)(2,1)}, bf16[1024,256]{1,0:T(8,128)(2,1)S(1)}, u32[]{:S(2)}) copy-start(bf16[1024,256]{1,0:T(8,128)(2,1)S(1)} %collective-permute-done.left_ref) | copy-start | bytes 1572868
  24.7 0.9 copy-start.2
  45.6 53.4 %collective-permute-start.2 = (f32[16,3,256]{2,1,0:T(4,128)S(1)}, f32[16,3,256]{2,1,0:T(4,128)S(1)}, u32[]{:S(2)}, u32[]{:S(2)}) collective-permute-start(f32[16,3,256]{2,1,0:T(4,128)S(1)} %get-tuple-element.18), channel_id=1, source_target_pairs={{0,2},{2,4},{4,6},{6,8},{8,10},{10,12},{12,14},{14,16},{16,18},{18... | collective-permute-start | bytes 147464 | tf_op jit(solution)/shard_map/ppermute | solution.py:116
  48.7 50.3 %collective-permute-start.3 = (f32[16,3,256]{2,1,0:T(4,128)S(1)}, f32[16,3,256]{2,1,0:T(4,128)S(1)}, u32[]{:S(2)}, u32[]{:S(2)}) collective-permute-start(f32[16,3,256]{2,1,0:T(4,128)S(1)} %get-tuple-element.19), channel_id=1, source_target_pairs={{2,0},{4,2},{6,4},{8,6},{10,8},{12,10},{14,12},{16,14},{18,16},{20... | collective-permute-start | bytes 147464 | tf_op jit(solution)/shard_map/ppermute | solution.py:117

commit v12 on v11

--- a/solution.py
+++ b/solution.py
@@ -224,7 +224,11 @@
 def on_device(adjoint, collision, solid, codes):
     local_vel, width, plane = adjoint.shape
     start = lax.axis_index("vel") * local_vel
-    speed_x, speed_y, speed_z, weigh, lift = tables(start, local_vel)
+    every = tables(0, NV1**3)
+    speed_x, speed_y, speed_z, lift = (
+        lax.dynamic_slice_in_dim(table, start, local_vel, 0) for table in (every[0], every[1], every[2], every[4])
+    )
+    weigh = lax.dynamic_slice_in_dim(every[3], start, local_vel, 1)
     count = axis_count(SPACE_AXES)
     ends = count - 1
     flat = lax.optimization_barrier(adjoint.reshape(local_vel, width * plane))

time: 114 us -> 114 us (level)
  other arithmetic: 8.94 us -> 5.31 us
  local copies, waits for them, and re-layouts: 12 us -> 15.2 us
    reshape x0 -> x3, local copies, waits for them, and re-layouts: none -> 4.11 us  [the longest x1 1.38 us: on_device(): speed_y.reshape(local_vel, 1)]
    mul x2 -> x1, other arithmetic: 1.19 us -> 0.01 us  [velocity_axes(): along_x = ((index % NV1).astype(jnp.float32) - centre) * spacing]
    mul x2, other arithmetic: 1.21 us -> 0.07 us  [velocity_axes(): along_z = ((index // NV1 % NV1).astype(jnp.float32) - centre) * spacing]
    unnamed x17 -> x18, local copies, waits for them, and re-layouts: 7.92 us -> 8.93 us
where the time goes in v12:
time: 114 us
  blocking collectives  49.4 us (43%)
  Pallas kernels  25.8 us (23%)
  local copies, waits for them, and re-layouts  15.2 us (13%)
  starting transfers between devices  11.7 us (10%)
  other arithmetic  5.31 us (5%)
  waiting for transfers between devices  4.45 us (4%)
  between operations  1.71 us (2%)
    psum x3, blocking collectives, on_device(): squares = lax.psum(squares, axis)  45.2 us
    pallas_call x1, Pallas kernels, advance(): pl.pallas_call(advance_kernel, grid=grid, in_specs=[pl.BlockSpec((block,...  15.8 us
    pallas_call x1, Pallas kernels, correct(): pl.pallas_call(correct_kernel, grid=(nv // block,), in_specs=[pl.BlockSpe...  10.1 us
    unnamed x18, local copies, waits for them, and re-layouts  8.93 us
    psum x1, blocking collectives, on_device(): moments = lax.psum(partial_value, 'vel').reshape(NM, width, plane)  4.2 us
    ppermute x1, starting transfers between devices, on_device(): left = lax.ppermute(tail, SPACE_AXES, [(i, i + 1) for i in range(ends)])  3.4 us
    ppermute x1, waiting for transfers between devices, on_device(): right = lax.ppermute(head, SPACE_AXES, [(i + 1, i) for i in range(ends)])  3.12 us
    ppermute x1, starting transfers between devices, sweep_all(): lax.ppermute(pack[:, width - depth:], SPACE_AXES, [(i, i + 1) for i in ra...  3.11 us
  transfers between devices with their start and end apart: 4, of which 2 were waited for; matrix products, arithmetic and copies ran while one was open for 9% of the time, Pallas kernels for 0%

profile of v12, /device:TPU:10, one launch (start us, length us, event | category | flops | bytes accessed | tf_op | source)
XLA Modules:
  0.0 113.6 jit_solution(17482830807389068750)
XLA Ops:
  0.6 3.2 %copy.38 = bf16[256,8,4,256]{3,1,2,0:T(8,128)(2,1)S(1)} copy(bf16[256,8,4,256]{3,2,1,0:T(4,128)(2,1)} %bitcast.54) | data formatting | bytes 8388608
  3.9 0.0 copy-start
  3.9 0.0 copy-start.4
  3.9 0.0 copy-start.5
  3.9 2.0 %copy-done = bf16[256,8,4,256]{3,1,2,0:T(8,128)(2,1)} copy-done((bf16[256,8,4,256]{3,1,2,0:T(8,128)(2,1)}, bf16[256,8,4,256]{3,1,2,0:T(8,128)(2,1)S(1)}, u32[]{:S(2)}) %copy-start) | copy-done | bytes 4194328
  5.9 0.1 slice_bitcast_fusion
  6.0 3.4 %collective-permute-start = (bf16[1024,256]{1,0:T(8,128)(2,1)S(1)}, bf16[1024,256]{1,0:T(8,128)(2,1)S(1)}, u32[]{:S(2)}, u32[]{:S(2)}) collective-permute-start(bf16[1024,256]{1,0:T(8,128)(2,1)S(1)} %get-tuple-element.11), channel_id=1, source_target_pairs={{0,2},{2,4},{4,6},{6,8},{8,10},{10,12},{12,14},{14,16},{16,18},{18... | collective-permute-start | bytes 1572872 | tf_op jit(solution)/shard_map/ppermute | solution.py:239
  9.4 2.4 %collective-permute-start.1 = (bf16[1024,256]{1,0:T(8,128)(2,1)S(1)}, bf16[1024,256]{1,0:T(8,128)(2,1)S(1)}, u32[]{:S(2)}, u32[]{:S(2)}) collective-permute-start(bf16[1024,256]{1,0:T(8,128)(2,1)S(1)} %get-tuple-element.10), channel_id=1, source_target_pairs={{2,0},{4,2},{6,4},{8,6},{10,8},{12,10},{14,12},{16,14},{18,16},{20... | collective-permute-start | bytes 1572872 | tf_op jit(solution)/shard_map/ppermute | solution.py:240
  11.8 0.1 fusion.34
  11.9 0.1 multiply_multiply_fusion
  12.0 0.1 multiply_multiply_fusion.2
  12.1 0.1 subtract_multiply_fusion.1
  12.2 0.1 broadcast_multiply_fusion.3
  12.3 0.1 fusion.50
  12.5 1.3 %copy.31.cx_ref = f32[2048,1]{1,0:T(8,128)} copy(f32[2048,1]{0,1:T(1,128)S(1)} %bitcast.65) | data formatting | bytes 16384 | tf_op jit(solution)/shard_map/reshape | solution.py:246
  13.9 1.4 %copy.32.cy_ref = f32[2048,1]{1,0:T(8,128)} copy(f32[2048,1]{0,1:T(1,128)S(1)} %bitcast.66) | data formatting | bytes 16384 | tf_op jit(solution)/shard_map/reshape | solution.py:247
  15.3 1.4 %copy.33.cz_ref = f32[2048,1]{1,0:T(8,128)} copy(f32[2048,1]{0,1:T(1,128)S(1)} %bitcast.67) | data formatting | bytes 16384 | tf_op jit(solution)/shard_map/reshape | solution.py:248
  16.7 0.6 copy.40
  17.3 0.6 copy.39
  17.9 0.3 stack.8
  18.2 0.7 fusion.47
  18.9 1.3 %multiply_convert_fusion = (bf16[13,2048]{1,0:T(8,128)(2,1)S(1)}, bf16[13,2048]{1,0:T(8,128)(2,1)}) fusion(f32[13,4096]{1,0:T(8,128)S(1)} %stack.8, s32[]{:T(128)S(6)} %select_n.297, f32[2048]{0:T(1024)S(1)} %dynamic-slice.6, f32[]{:T(128)} %fusion.47, f32[2048]{0:T(1024)S(1)} %dynamic-slice.4), kind=kLoop, calls=%fused_computation.28 | loop fusion | flops 133120 | bytes 229384 | tf_op jit(solution)/shard_map/convert_element_type | solution.py:85
  20.2 1.3 %collective-permute-done.left_ref = bf16[1024,256]{1,0:T(8,128)(2,1)S(1)} collective-permute-done((bf16[1024,256]{1,0:T(8,128)(2,1)S(1)}, bf16[1024,256]{1,0:T(8,128)(2,1)S(1)}, u32[]{:S(2)}, u32[]{:S(2)}) %collective-permute-start) | collective-permute-done | bytes 524320 | tf_op jit(solution)/shard_map/ppermute | solution.py:239
  21.5 3.1 %collective-permute-done.1.right_ref = bf16[1024,256]{1,0:T(8,128)(2,1)S(1)} collective-permute-done((bf16[1024,256]{1,0:T(8,128)(2,1)S(1)}, bf16[1024,256]{1,0:T(8,128)(2,1)S(1)}, u32[]{:S(2)}, u32[]{:S(2)}) %collective-permute-start.1) | collective-permute-done | bytes 524320 | tf_op jit(solution)/shard_map/ppermute | solution.py:240
  24.6 0.8 copy-done.2
  25.5 15.8 %shard_map.59 = (bf16[2048,1024]{1,0:T(8,128)(2,1)}, f32[13,1024]{1,0:T(8,128)}) custom-call(bf16[2048,1024]{1,0:T(8,128)(2,1)} %bitcast.53, bf16[1024,256]{1,0:T(8,128)(2,1)} %copy-done.1, bf16[1024,256]{1,0:T(8,128)(2,1)} %copy-done.2, f32[2048,1]{1,0:T(8,128)} %copy.31.cx_ref, f32[2048,1]{1,0:T(8,128)} %copy.32.cy_ref, f32[2048,1]{1,0:T(8,128)} %copy.33.cz_ref, ...), custom_call_target="tpu_custom_call" | custom-call | tf_op jit(solution)/shard_map/pallas_call | solution.py:177
  41.2 4.2 %psum.28 = f32[13,1024]{1,0:T(8,128)S(1)} all-reduce(f32[13,1024]{1,0:T(8,128)} %get-tuple-element.5), channel_id=1, replica_groups=mesh['sz'=8,'sy'=4,'sx'=4,'vel'=2] {'vel'}, use_global_device_ids=true, to_apply=%region_1.2 | all-reduce | flops 13312 | bytes 106496 | tf_op jit(solution)/shard_map/psum | solution.py:253
  45.6 3.1 %collective-permute-start.2 = (f32[16,3,256]{2,1,0:T(4,128)S(1)}, f32[16,3,256]{2,1,0:T(4,128)S(1)}, u32[]{:S(2)}, u32[]{:S(2)}) collective-permute-start(f32[16,3,256]{2,1,0:T(4,128)S(1)} %get-tuple-element.18), channel_id=1, source_target_pairs={{0,2},{2,4},{4,6},{6,8},{8,10},{10,12},{12,14},{14,16},{16,18},{18... | collective-permute-start | bytes 147464 | tf_op jit(solution)/shard_map/ppermute | solution.py:116
  48.7 2.7 %collective-permute-start.3 = (f32[16,3,256]{2,1,0:T(4,128)S(1)}, f32[16,3,256]{2,1,0:T(4,128)S(1)}, u32[]{:S(2)}, u32[]{:S(2)}) collective-permute-start(f32[16,3,256]{2,1,0:T(4,128)S(1)} %get-tuple-element.19), channel_id=1, source_target_pairs={{2,0},{4,2},{6,4},{8,6},{10,8},{12,10},{14,12},{16,14},{18,16},{20... | collective-permute-start | bytes 147464 | tf_op jit(solution)/shard_map/ppermute | solution.py:117
  51.4 0.6 fusion.48
  52.0 11.6 %psum.29 = f32[]{:T(128)} all-reduce(f32[]{:T(128)} %fusion.48), channel_id=1, replica_groups=mesh['sz'=8,'sy'=4,'sx'=4,'vel'=2] {'sx'}, use_global_device_ids=true, to_apply=%region_3.4 | all-reduce | flops 1 | bytes 8 | tf_op jit(solution)/shard_map/psum | solution.py:257
  63.6 9.6 %psum.30 = f32[]{:T(128)} all-reduce(f32[]{:T(128)} %psum.29), channel_id=1, replica_groups=mesh['sz'=8,'sy'=4,'sx'=4,'vel'=2] {'sy'}, use_global_device_ids=true, to_apply=%region_4.5 | all-reduce | flops 1 | bytes 8 | tf_op jit(solution)/shard_map/psum | solution.py:257
  73.2 1.0 copy.37
  74.3 24.0 %psum.31 = f32[]{:T(128)} all-reduce(f32[]{:T(128)} %psum.30), channel_id=1, replica_groups=mesh['sz'=8,'sy'=4,'sx'=4,'vel'=2] {'sz'}, use_global_device_ids=true, to_apply=%region_5.6 | all-reduce | flops 1 | bytes 8 | tf_op jit(solution)/shard_map/psum | solution.py:257
  99.1 0.1 broadcast_multiply_fusion.1
  99.2 0.3 reshape.296
  99.5 0.5 fusion.2
  100.0 0.4 reshape.297
  100.4 0.2 reshape.298
  100.7 0.4 fusion.5
  101.1 0.3 reshape.299
  101.4 0.1 fusion.11
  101.5 0.2 reshape.300
  101.7 0.3 fusion.8
  102.0 0.2 reshape.301
  102.2 0.7 broadcast_multiply_fusion.2
  102.9 0.6 copy.41
  103.5 10.1 %shard_map.60 = bf16[2048,4,256]{2,1,0:T(4,128)(2,1)} custom-call(bf16[2048,1024]{1,0:T(8,128)(2,1)} %get-tuple-element.4.star_ref, bf16[2048,13]{1,0:T(8,128)(2,1)} %bitcast.55, bf16[13,1024]{1,0:T(8,128)(2,1)} %bitcast.56, f32[1,1024]{1,0:T(1,128)} %bitcast.64), custom_call_target="tpu_custom_call" | custom-call | tf_op jit(solution)/shard_map/pallas_call | solution.py:209
  (37 shorter events, 0.4 us)
Async XLA Ops:
  3.9 2.0 %copy-start = (bf16[256,8,4,256]{3,1,2,0:T(8,128)(2,1)}, bf16[256,8,4,256]{3,1,2,0:T(8,128)(2,1)S(1)}, u32[]{:S(2)}) copy-start(bf16[256,8,4,256]{3,1,2,0:T(8,128)(2,1)S(1)} %copy.38) | copy-start | bytes 12582916
  3.9 11.4 %copy-start.4 = (s32[4,256]{1,0:T(4,128)S(1)}, s32[4,256]{1,0:T(4,128)}, u32[]{:S(2)}) copy-start(s32[4,256]{1,0:T(4,128)} %param.6) | copy-start | bytes 12292
  3.9 11.4 %copy-start.5 = (s32[4,256]{1,0:T(4,128)S(1)}, s32[4,256]{1,0:T(4,128)}, u32[]{:S(2)}) copy-start(s32[4,256]{1,0:T(4,128)} %param.7) | copy-start | bytes 12292
  3.9 13.4 %copy-start.3 = (f32[4,256]{1,0:T(4,128)S(1)}, f32[4,256]{1,0:T(4,128)}, u32[]{:S(2)}) copy-start(f32[4,256]{1,0:T(4,128)} %param.5) | copy-start | bytes 12292
  6.0 15.6 %collective-permute-start = (bf16[1024,256]{1,0:T(8,128)(2,1)S(1)}, bf16[1024,256]{1,0:T(8,128)(2,1)S(1)}, u32[]{:S(2)}, u32[]{:S(2)}) collective-permute-start(bf16[1024,256]{1,0:T(8,128)(2,1)S(1)} %get-tuple-element.11), channel_id=1, source_target_pairs={{0,2},{2,4},{4,6},{6,8},{8,10},{10,12},{12,14},{14,16},{16,18},{18... | collective-permute-start | bytes 1572872 | tf_op jit(solution)/shard_map/ppermute | solution.py:239
  9.4 15.3 %collective-permute-start.1 = (bf16[1024,256]{1,0:T(8,128)(2,1)S(1)}, bf16[1024,256]{1,0:T(8,128)(2,1)S(1)}, u32[]{:S(2)}, u32[]{:S(2)}) collective-permute-start(bf16[1024,256]{1,0:T(8,128)(2,1)S(1)} %get-tuple-element.10), channel_id=1, source_target_pairs={{2,0},{4,2},{6,4},{8,6},{10,8},{12,10},{14,12},{16,14},{18,16},{20... | collective-permute-start | bytes 1572872 | tf_op jit(solution)/shard_map/ppermute | solution.py:240
  21.5 3.1 %copy-start.1 = (bf16[1024,256]{1,0:T(8,128)(2,1)}, bf16[1024,256]{1,0:T(8,128)(2,1)S(1)}, u32[]{:S(2)}) copy-start(bf16[1024,256]{1,0:T(8,128)(2,1)S(1)} %collective-permute-done.left_ref) | copy-start | bytes 1572868
  24.6 0.8 copy-start.2
  45.6 53.4 %collective-permute-start.2 = (f32[16,3,256]{2,1,0:T(4,128)S(1)}, f32[16,3,256]{2,1,0:T(4,128)S(1)}, u32[]{:S(2)}, u32[]{:S(2)}) collective-permute-start(f32[16,3,256]{2,1,0:T(4,128)S(1)} %get-tuple-element.18), channel_id=1, source_target_pairs={{0,2},{2,4},{4,6},{6,8},{8,10},{10,12},{12,14},{14,16},{16,18},{18... | collective-permute-start | bytes 147464 | tf_op jit(solution)/shard_map/ppermute | solution.py:116
  48.7 50.3 %collective-permute-start.3 = (f32[16,3,256]{2,1,0:T(4,128)S(1)}, f32[16,3,256]{2,1,0:T(4,128)S(1)}, u32[]{:S(2)}, u32[]{:S(2)}) collective-permute-start(f32[16,3,256]{2,1,0:T(4,128)S(1)} %get-tuple-element.19), channel_id=1, source_target_pairs={{2,0},{4,2},{6,4},{8,6},{10,8},{12,10},{14,12},{16,14},{18,16},{20... | collective-permute-start | bytes 147464 | tf_op jit(solution)/shard_map/ppermute | solution.py:117

commit v13 on v12

--- a/solution.py
+++ b/solution.py
@@ -250,7 +250,7 @@
         fluid.reshape(1, width * plane),
         weigh,
     )
-    moments = lax.psum(partial_value, "vel").reshape(NM, width, plane)
+    moments = (partial_value + lax.ppermute(partial_value, "vel", [(0, 1), (1, 0)])).reshape(NM, width, plane)
     cells_all = width * axis_count(SPACE_AXES) * plane
     squares = jnp.sum(moments[0] * moments[0])
     for axis in SPACE_AXES[::-1]:

time: 114 us -> 112 us (0.982)
  blocking collectives: 49.4 us -> 45.2 us
  waiting for transfers between devices: 4.45 us -> 6.06 us
    psum x1 -> x0, blocking collectives: 4.2 us -> none  [on_device(): moments = lax.psum(partial_value, 'vel').reshape(NM, width, plane)]
    ppermute x0 -> x1, waiting for transfers between devices: none -> 1.43 us  [on_device(): lax.ppermute(partial_value, 'vel', [(0, 1), (1, 0)])]
  transfers between devices with their start and end apart: 4 -> 5, of which waited for: 2 -> 3; matrix products, arithmetic and copies ran while one was open for 9% -> 9% of each run, Pallas kernels for 0% -> 0%
where the time goes in v13:
time: 112 us
  blocking collectives  45.2 us (40%)
  Pallas kernels  25.9 us (23%)
  local copies, waits for them, and re-layouts  15.2 us (14%)
  starting transfers between devices  11.8 us (11%)
  waiting for transfers between devices  6.06 us (5%)
  other arithmetic  6.03 us (5%)
  between operations  1.7 us (2%)
    psum x3, blocking collectives, on_device(): squares = lax.psum(squares, axis)  45.2 us
    pallas_call x1, Pallas kernels, advance(): pl.pallas_call(advance_kernel, grid=grid, in_specs=[pl.BlockSpec((block,...  15.8 us
    pallas_call x1, Pallas kernels, correct(): pl.pallas_call(correct_kernel, grid=(nv // block,), in_specs=[pl.BlockSpe...  10.1 us
    unnamed x18, local copies, waits for them, and re-layouts  8.95 us
    ppermute x1, starting transfers between devices, on_device(): left = lax.ppermute(tail, SPACE_AXES, [(i, i + 1) for i in range(ends)])  3.4 us
    ppermute x1, waiting for transfers between devices, on_device(): right = lax.ppermute(head, SPACE_AXES, [(i + 1, i) for i in range(ends)])  3.12 us
    ppermute x1, starting transfers between devices, sweep_all(): lax.ppermute(pack[:, width - depth:], SPACE_AXES, [(i, i + 1) for i in ra...  3.11 us
    ppermute x1, starting transfers between devices, sweep_all(): lax.ppermute(pack[:, :depth], SPACE_AXES, [(i + 1, i) for i in range(ends)])  2.74 us
  transfers between devices with their start and end apart: 5, of which 3 were waited for; matrix products, arithmetic and copies ran while one was open for 9% of the time, Pallas kernels for 0%

profile of v13, /device:TPU:10, one launch (start us, length us, event | category | flops | bytes accessed | tf_op | source)
XLA Modules:
  0.0 111.8 jit_solution(13096580390899286128)
XLA Ops:
  0.6 3.2 %copy.38 = bf16[256,8,4,256]{3,1,2,0:T(8,128)(2,1)S(1)} copy(bf16[256,8,4,256]{3,2,1,0:T(4,128)(2,1)} %bitcast.54) | data formatting | bytes 8388608
  3.9 0.0 copy-start
  3.9 2.0 %copy-done = bf16[256,8,4,256]{3,1,2,0:T(8,128)(2,1)} copy-done((bf16[256,8,4,256]{3,1,2,0:T(8,128)(2,1)}, bf16[256,8,4,256]{3,1,2,0:T(8,128)(2,1)S(1)}, u32[]{:S(2)}) %copy-start) | copy-done | bytes 4194328
  5.9 0.1 slice_bitcast_fusion
  6.0 3.4 %collective-permute-start = (bf16[1024,256]{1,0:T(8,128)(2,1)S(1)}, bf16[1024,256]{1,0:T(8,128)(2,1)S(1)}, u32[]{:S(2)}, u32[]{:S(2)}) collective-permute-start(bf16[1024,256]{1,0:T(8,128)(2,1)S(1)} %get-tuple-element.11), channel_id=1, source_target_pairs={{0,2},{2,4},{4,6},{6,8},{8,10},{10,12},{12,14},{14,16},{16,18},{18... | collective-permute-start | bytes 1572872 | tf_op jit(solution)/shard_map/ppermute | solution.py:239
  9.4 2.4 %collective-permute-start.1 = (bf16[1024,256]{1,0:T(8,128)(2,1)S(1)}, bf16[1024,256]{1,0:T(8,128)(2,1)S(1)}, u32[]{:S(2)}, u32[]{:S(2)}) collective-permute-start(bf16[1024,256]{1,0:T(8,128)(2,1)S(1)} %get-tuple-element.10), channel_id=1, source_target_pairs={{2,0},{4,2},{6,4},{8,6},{10,8},{12,10},{14,12},{16,14},{18,16},{20... | collective-permute-start | bytes 1572872 | tf_op jit(solution)/shard_map/ppermute | solution.py:240
  11.8 0.1 fusion.34
  11.9 0.1 multiply_multiply_fusion
  12.0 0.1 multiply_multiply_fusion.2
  12.1 0.1 subtract_multiply_fusion.1
  12.2 0.1 broadcast_multiply_fusion.3
  12.3 0.1 fusion.50
  12.5 1.3 %copy.31.cx_ref = f32[2048,1]{1,0:T(8,128)} copy(f32[2048,1]{0,1:T(1,128)S(1)} %bitcast.65) | data formatting | bytes 16384 | tf_op jit(solution)/shard_map/reshape | solution.py:246
  13.9 1.4 %copy.32.cy_ref = f32[2048,1]{1,0:T(8,128)} copy(f32[2048,1]{0,1:T(1,128)S(1)} %bitcast.66) | data formatting | bytes 16384 | tf_op jit(solution)/shard_map/reshape | solution.py:247
  15.3 1.4 %copy.33.cz_ref = f32[2048,1]{1,0:T(8,128)} copy(f32[2048,1]{0,1:T(1,128)S(1)} %bitcast.67) | data formatting | bytes 16384 | tf_op jit(solution)/shard_map/reshape | solution.py:248
  16.7 0.6 copy.40
  17.3 0.6 copy.39
  17.9 0.3 stack.8
  18.2 0.6 fusion.47
  18.8 1.2 %multiply_convert_fusion = (bf16[13,2048]{1,0:T(8,128)(2,1)S(1)}, bf16[13,2048]{1,0:T(8,128)(2,1)}) fusion(f32[13,4096]{1,0:T(8,128)S(1)} %stack.8, s32[]{:T(128)S(6)} %select_n.297, f32[2048]{0:T(1024)S(1)} %dynamic-slice.6, f32[]{:T(128)} %fusion.47, f32[2048]{0:T(1024)S(1)} %dynamic-slice.4), kind=kLoop, calls=%fused_computation.28 | loop fusion | flops 133120 | bytes 229384 | tf_op jit(solution)/shard_map/convert_element_type | solution.py:85
  20.0 1.5 %collective-permute-done.left_ref = bf16[1024,256]{1,0:T(8,128)(2,1)S(1)} collective-permute-done((bf16[1024,256]{1,0:T(8,128)(2,1)S(1)}, bf16[1024,256]{1,0:T(8,128)(2,1)S(1)}, u32[]{:S(2)}, u32[]{:S(2)}) %collective-permute-start) | collective-permute-done | bytes 524320 | tf_op jit(solution)/shard_map/ppermute | solution.py:239
  21.5 3.1 %collective-permute-done.1.right_ref = bf16[1024,256]{1,0:T(8,128)(2,1)S(1)} collective-permute-done((bf16[1024,256]{1,0:T(8,128)(2,1)S(1)}, bf16[1024,256]{1,0:T(8,128)(2,1)S(1)}, u32[]{:S(2)}, u32[]{:S(2)}) %collective-permute-start.1) | collective-permute-done | bytes 524320 | tf_op jit(solution)/shard_map/ppermute | solution.py:240
  24.6 0.9 copy-done.2
  25.5 15.8 %shard_map.59 = (bf16[2048,1024]{1,0:T(8,128)(2,1)}, f32[13,1024]{1,0:T(8,128)}) custom-call(bf16[2048,1024]{1,0:T(8,128)(2,1)} %bitcast.53, bf16[1024,256]{1,0:T(8,128)(2,1)} %copy-done.1, bf16[1024,256]{1,0:T(8,128)(2,1)} %copy-done.2, f32[2048,1]{1,0:T(8,128)} %copy.31.cx_ref, f32[2048,1]{1,0:T(8,128)} %copy.32.cy_ref, f32[2048,1]{1,0:T(8,128)} %copy.33.cz_ref, ...), custom_call_target="tpu_custom_call" | custom-call | tf_op jit(solution)/shard_map/pallas_call | solution.py:177
  41.3 0.1 collective-permute-start.2
  41.4 1.4 %collective-permute-done.2 = f32[13,1024]{1,0:T(8,128)S(1)} collective-permute-done((f32[13,1024]{1,0:T(8,128)}, f32[13,1024]{1,0:T(8,128)S(1)}, u32[]{:S(2)}, u32[]{:S(2)}) %collective-permute-start.2) | collective-permute-done | bytes 53280 | tf_op jit(solution)/shard_map/ppermute | solution.py:253
  42.8 0.9 add.584
  43.8 3.1 %collective-permute-start.3 = (f32[16,3,256]{2,1,0:T(4,128)S(1)}, f32[16,3,256]{2,1,0:T(4,128)S(1)}, u32[]{:S(2)}, u32[]{:S(2)}) collective-permute-start(f32[16,3,256]{2,1,0:T(4,128)S(1)} %get-tuple-element.18), channel_id=1, source_target_pairs={{0,2},{2,4},{4,6},{6,8},{8,10},{10,12},{12,14},{14,16},{16,18},{18... | collective-permute-start | bytes 147464 | tf_op jit(solution)/shard_map/ppermute | solution.py:116
  46.9 2.7 %collective-permute-start.4 = (f32[16,3,256]{2,1,0:T(4,128)S(1)}, f32[16,3,256]{2,1,0:T(4,128)S(1)}, u32[]{:S(2)}, u32[]{:S(2)}) collective-permute-start(f32[16,3,256]{2,1,0:T(4,128)S(1)} %get-tuple-element.19), channel_id=1, source_target_pairs={{2,0},{4,2},{6,4},{8,6},{10,8},{12,10},{14,12},{16,14},{18,16},{20... | collective-permute-start | bytes 147464 | tf_op jit(solution)/shard_map/ppermute | solution.py:117
  49.6 0.6 fusion.48
  50.2 11.6 %psum.21 = f32[]{:T(128)} all-reduce(f32[]{:T(128)} %fusion.48), channel_id=1, replica_groups=mesh['sz'=8,'sy'=4,'sx'=4,'vel'=2] {'sx'}, use_global_device_ids=true, to_apply=%region_2.3 | all-reduce | flops 1 | bytes 8 | tf_op jit(solution)/shard_map/psum | solution.py:257
  61.8 9.6 %psum.22 = f32[]{:T(128)} all-reduce(f32[]{:T(128)} %psum.21), channel_id=1, replica_groups=mesh['sz'=8,'sy'=4,'sx'=4,'vel'=2] {'sy'}, use_global_device_ids=true, to_apply=%region_3.4 | all-reduce | flops 1 | bytes 8 | tf_op jit(solution)/shard_map/psum | solution.py:257
  71.4 1.1 copy.37
  72.5 24.0 %psum.23 = f32[]{:T(128)} all-reduce(f32[]{:T(128)} %psum.22), channel_id=1, replica_groups=mesh['sz'=8,'sy'=4,'sx'=4,'vel'=2] {'sz'}, use_global_device_ids=true, to_apply=%region_4.5 | all-reduce | flops 1 | bytes 8 | tf_op jit(solution)/shard_map/psum | solution.py:257
  97.3 0.1 broadcast_multiply_fusion.1
  97.4 0.3 reshape.296
  97.7 0.5 fusion.2
  98.2 0.4 reshape.297
  98.7 0.2 reshape.298
  98.9 0.4 fusion.5
  99.3 0.3 reshape.299
  99.6 0.1 fusion.11
  99.7 0.2 reshape.300
  99.9 0.3 fusion.8
  100.2 0.2 reshape.301
  100.4 0.7 broadcast_multiply_fusion.2
  101.1 0.6 copy.41
  101.7 10.1 %shard_map.60 = bf16[2048,4,256]{2,1,0:T(4,128)(2,1)} custom-call(bf16[2048,1024]{1,0:T(8,128)(2,1)} %get-tuple-element.4.star_ref, bf16[2048,13]{1,0:T(8,128)(2,1)} %bitcast.55, bf16[13,1024]{1,0:T(8,128)(2,1)} %bitcast.56, f32[1,1024]{1,0:T(1,128)} %bitcast.64), custom_call_target="tpu_custom_call" | custom-call | tf_op jit(solution)/shard_map/pallas_call | solution.py:209
  (39 shorter events, 0.4 us)
Async XLA Ops:
  3.9 2.0 %copy-start = (bf16[256,8,4,256]{3,1,2,0:T(8,128)(2,1)}, bf16[256,8,4,256]{3,1,2,0:T(8,128)(2,1)S(1)}, u32[]{:S(2)}) copy-start(bf16[256,8,4,256]{3,1,2,0:T(8,128)(2,1)S(1)} %copy.38) | copy-start | bytes 12582916
  3.9 11.4 %copy-start.4 = (s32[4,256]{1,0:T(4,128)S(1)}, s32[4,256]{1,0:T(4,128)}, u32[]{:S(2)}) copy-start(s32[4,256]{1,0:T(4,128)} %param.6) | copy-start | bytes 12292
  3.9 13.4 %copy-start.3 = (f32[4,256]{1,0:T(4,128)S(1)}, f32[4,256]{1,0:T(4,128)}, u32[]{:S(2)}) copy-start(f32[4,256]{1,0:T(4,128)} %param.5) | copy-start | bytes 12292
  6.0 15.6 %collective-permute-start = (bf16[1024,256]{1,0:T(8,128)(2,1)S(1)}, bf16[1024,256]{1,0:T(8,128)(2,1)S(1)}, u32[]{:S(2)}, u32[]{:S(2)}) collective-permute-start(bf16[1024,256]{1,0:T(8,128)(2,1)S(1)} %get-tuple-element.11), channel_id=1, source_target_pairs={{0,2},{2,4},{4,6},{6,8},{8,10},{10,12},{12,14},{14,16},{16,18},{18... | collective-permute-start | bytes 1572872 | tf_op jit(solution)/shard_map/ppermute | solution.py:239
  9.4 15.3 %collective-permute-start.1 = (bf16[1024,256]{1,0:T(8,128)(2,1)S(1)}, bf16[1024,256]{1,0:T(8,128)(2,1)S(1)}, u32[]{:S(2)}, u32[]{:S(2)}) collective-permute-start(bf16[1024,256]{1,0:T(8,128)(2,1)S(1)} %get-tuple-element.10), channel_id=1, source_target_pairs={{2,0},{4,2},{6,4},{8,6},{10,8},{12,10},{14,12},{16,14},{18,16},{20... | collective-permute-start | bytes 1572872 | tf_op jit(solution)/shard_map/ppermute | solution.py:240
  21.5 3.1 %copy-start.1 = (bf16[1024,256]{1,0:T(8,128)(2,1)}, bf16[1024,256]{1,0:T(8,128)(2,1)S(1)}, u32[]{:S(2)}) copy-start(bf16[1024,256]{1,0:T(8,128)(2,1)S(1)} %collective-permute-done.left_ref) | copy-start | bytes 1572868
  24.6 0.9 copy-start.2
  25.5 15.9 %copy-start.5 = (s32[4,256]{1,0:T(4,128)S(1)}, s32[4,256]{1,0:T(4,128)}, u32[]{:S(2)}) copy-start(s32[4,256]{1,0:T(4,128)} %param.7) | copy-start | bytes 12292
  41.3 1.6 %collective-permute-start.2 = (f32[13,1024]{1,0:T(8,128)}, f32[13,1024]{1,0:T(8,128)S(1)}, u32[]{:S(2)}, u32[]{:S(2)}) collective-permute-start(f32[13,1024]{1,0:T(8,128)} %get-tuple-element.5), channel_id=1, source_target_pairs={{0,1},{1,0},{2,3},{3,2},{4,5},{5,4},{6,7},{7,6},{8,9},{9,8},{10,11... | collective-permute-start | bytes 159752 | tf_op jit(solution)/shard_map/ppermute | solution.py:253
  43.8 53.4 %collective-permute-start.3 = (f32[16,3,256]{2,1,0:T(4,128)S(1)}, f32[16,3,256]{2,1,0:T(4,128)S(1)}, u32[]{:S(2)}, u32[]{:S(2)}) collective-permute-start(f32[16,3,256]{2,1,0:T(4,128)S(1)} %get-tuple-element.18), channel_id=1, source_target_pairs={{0,2},{2,4},{4,6},{6,8},{8,10},{10,12},{12,14},{14,16},{16,18},{18... | collective-permute-start | bytes 147464 | tf_op jit(solution)/shard_map/ppermute | solution.py:116
  46.9 50.3 %collective-permute-start.4 = (f32[16,3,256]{2,1,0:T(4,128)S(1)}, f32[16,3,256]{2,1,0:T(4,128)S(1)}, u32[]{:S(2)}, u32[]{:S(2)}) collective-permute-start(f32[16,3,256]{2,1,0:T(4,128)S(1)} %get-tuple-element.19), channel_id=1, source_target_pairs={{2,0},{4,2},{6,4},{8,6},{10,8},{12,10},{14,12},{16,14},{18,16},{20... | collective-permute-start | bytes 147464 | tf_op jit(solution)/shard_map/ppermute | solution.py:117

commit v14 on v13

--- a/solution.py
+++ b/solution.py
@@ -254,7 +254,7 @@
     cells_all = width * axis_count(SPACE_AXES) * plane
     squares = jnp.sum(moments[0] * moments[0])
     for axis in SPACE_AXES[::-1]:
-        squares = lax.psum(squares, axis)
+        squares = exchange_sum(squares, axis) if axis == SPACE_AXES[-1] else lax.psum(squares, axis)
     scale = lax.rsqrt(squares / cells_all + 1e-06)
     fields = sweep_all(moments, fluid, collision, wall_level(codes))
     delta = ((fields - moments) * scale).astype(jnp.bfloat16).reshape(NM, width * plane)

time: 112 us -> 114 us (1.018); the launches traced: 112 us -> 112 us
  blocking collectives: 45.2 us -> 33.5 us
  starting transfers between devices: 11.8 us -> 19.4 us
  waiting for transfers between devices: 6.06 us -> 8.63 us
  between operations: 1.7 us -> 3.5 us
    psum x3 -> x2, blocking collectives: 45.2 us -> 33.5 us  [on_device(): lax.psum(squares, axis)]
    ppermute x0 -> x2, starting transfers between devices: none -> 7.64 us  [exchange_sum(): lax.ppermute(value, axis, [(i, i ^ step) for i in range(count)])]
    ppermute x0 -> x2, waiting for transfers between devices: none -> 2.68 us  [exchange_sum(): lax.ppermute(value, axis, [(i, i ^ step) for i in range(count)])]
  transfers between devices with their start and end apart: 5 -> 7, of which waited for: 3 -> 5; matrix products, arithmetic and copies ran while one was open for 9% -> 9% of each run, Pallas kernels for 0% -> 0%
where the time goes in v14:
time: 114 us; the launch traced here: 112 us
  blocking collectives  33.5 us (29%)
  Pallas kernels  25.9 us (23%)
  starting transfers between devices  19.4 us (17%)
  local copies, waits for them, and re-layouts  15.2 us (13%)
  waiting for transfers between devices  8.63 us (8%)
  other arithmetic  6.12 us (5%)
  between operations  3.5 us (3%)
    psum x2, blocking collectives, on_device(): lax.psum(squares, axis)  33.5 us
    pallas_call x1, Pallas kernels, advance(): pl.pallas_call(advance_kernel, grid=grid, in_specs=[pl.BlockSpec((block,...  15.8 us
    pallas_call x1, Pallas kernels, correct(): pl.pallas_call(correct_kernel, grid=(nv // block,), in_specs=[pl.BlockSpe...  10.1 us
    unnamed x18, local copies, waits for them, and re-layouts  8.91 us
    ppermute x2, starting transfers between devices, exchange_sum(): lax.ppermute(value, axis, [(i, i ^ step) for i in range(count)])  7.64 us
    ppermute x1, starting transfers between devices, on_device(): left = lax.ppermute(tail, SPACE_AXES, [(i, i + 1) for i in range(ends)])  3.4 us
    ppermute x1, waiting for transfers between devices, on_device(): right = lax.ppermute(head, SPACE_AXES, [(i + 1, i) for i in range(ends)])  3.12 us
    ppermute x1, starting transfers between devices, sweep_all(): lax.ppermute(pack[:, width - depth:], SPACE_AXES, [(i, i + 1) for i in ra...  3.11 us
  transfers between devices with their start and end apart: 7, of which 5 were waited for; matrix products, arithmetic and copies ran while one was open for 9% of the time, Pallas kernels for 0%

profile of v14, /device:TPU:10, one launch (start us, length us, event | category | flops | bytes accessed | tf_op | source)
XLA Modules:
  0.0 112.2 jit_solution(10971377030471672973)
XLA Ops:
  0.6 3.2 %copy.38 = bf16[256,8,4,256]{3,1,2,0:T(8,128)(2,1)S(1)} copy(bf16[256,8,4,256]{3,2,1,0:T(4,128)(2,1)} %bitcast.54) | data formatting | bytes 8388608
  3.9 2.0 %copy-done = bf16[256,8,4,256]{3,1,2,0:T(8,128)(2,1)} copy-done((bf16[256,8,4,256]{3,1,2,0:T(8,128)(2,1)}, bf16[256,8,4,256]{3,1,2,0:T(8,128)(2,1)S(1)}, u32[]{:S(2)}) %copy-start) | copy-done | bytes 4194328
  5.9 0.1 slice_bitcast_fusion
  6.0 3.4 %collective-permute-start = (bf16[1024,256]{1,0:T(8,128)(2,1)S(1)}, bf16[1024,256]{1,0:T(8,128)(2,1)S(1)}, u32[]{:S(2)}, u32[]{:S(2)}) collective-permute-start(bf16[1024,256]{1,0:T(8,128)(2,1)S(1)} %get-tuple-element.11), channel_id=1, source_target_pairs={{0,2},{2,4},{4,6},{6,8},{8,10},{10,12},{12,14},{14,16},{16,18},{18... | collective-permute-start | bytes 1572872 | tf_op jit(solution)/shard_map/ppermute | solution.py:239
  9.4 2.4 %collective-permute-start.1 = (bf16[1024,256]{1,0:T(8,128)(2,1)S(1)}, bf16[1024,256]{1,0:T(8,128)(2,1)S(1)}, u32[]{:S(2)}, u32[]{:S(2)}) collective-permute-start(bf16[1024,256]{1,0:T(8,128)(2,1)S(1)} %get-tuple-element.10), channel_id=1, source_target_pairs={{2,0},{4,2},{6,4},{8,6},{10,8},{12,10},{14,12},{16,14},{18,16},{20... | collective-permute-start | bytes 1572872 | tf_op jit(solution)/shard_map/ppermute | solution.py:240
  11.9 0.1 multiply_multiply_fusion
  12.0 0.1 multiply_multiply_fusion.2
  12.1 0.1 subtract_multiply_fusion.1
  12.3 0.1 fusion.50
  12.5 1.3 %copy.31.cx_ref = f32[2048,1]{1,0:T(8,128)} copy(f32[2048,1]{0,1:T(1,128)S(1)} %bitcast.65) | data formatting | bytes 16384 | tf_op jit(solution)/shard_map/reshape | solution.py:246
  13.9 1.4 %copy.32.cy_ref = f32[2048,1]{1,0:T(8,128)} copy(f32[2048,1]{0,1:T(1,128)S(1)} %bitcast.66) | data formatting | bytes 16384 | tf_op jit(solution)/shard_map/reshape | solution.py:247
  15.3 1.4 %copy.33.cz_ref = f32[2048,1]{1,0:T(8,128)} copy(f32[2048,1]{0,1:T(1,128)S(1)} %bitcast.67) | data formatting | bytes 16384 | tf_op jit(solution)/shard_map/reshape | solution.py:248
  16.7 0.6 copy.40
  17.3 0.6 copy.39
  17.9 0.3 stack.8
  18.2 0.6 fusion.47
  18.9 1.3 %multiply_convert_fusion = (bf16[13,2048]{1,0:T(8,128)(2,1)S(1)}, bf16[13,2048]{1,0:T(8,128)(2,1)}) fusion(f32[13,4096]{1,0:T(8,128)S(1)} %stack.8, s32[]{:T(128)S(6)} %select_n.297, f32[2048]{0:T(1024)S(1)} %dynamic-slice.6, f32[]{:T(128)} %fusion.47, f32[2048]{0:T(1024)S(1)} %dynamic-slice.4), kind=kLoop, calls=%fused_computation.28 | loop fusion | flops 133120 | bytes 229384 | tf_op jit(solution)/shard_map/convert_element_type | solution.py:85
  20.1 1.4 %collective-permute-done.left_ref = bf16[1024,256]{1,0:T(8,128)(2,1)S(1)} collective-permute-done((bf16[1024,256]{1,0:T(8,128)(2,1)S(1)}, bf16[1024,256]{1,0:T(8,128)(2,1)S(1)}, u32[]{:S(2)}, u32[]{:S(2)}) %collective-permute-start) | collective-permute-done | bytes 524320 | tf_op jit(solution)/shard_map/ppermute | solution.py:239
  21.5 3.1 %collective-permute-done.1.right_ref = bf16[1024,256]{1,0:T(8,128)(2,1)S(1)} collective-permute-done((bf16[1024,256]{1,0:T(8,128)(2,1)S(1)}, bf16[1024,256]{1,0:T(8,128)(2,1)S(1)}, u32[]{:S(2)}, u32[]{:S(2)}) %collective-permute-start.1) | collective-permute-done | bytes 524320 | tf_op jit(solution)/shard_map/ppermute | solution.py:240
  24.6 0.8 copy-done.2
  25.5 15.8 %shard_map.59 = (bf16[2048,1024]{1,0:T(8,128)(2,1)}, f32[13,1024]{1,0:T(8,128)}) custom-call(bf16[2048,1024]{1,0:T(8,128)(2,1)} %bitcast.53, bf16[1024,256]{1,0:T(8,128)(2,1)} %copy-done.1, bf16[1024,256]{1,0:T(8,128)(2,1)} %copy-done.2, f32[2048,1]{1,0:T(8,128)} %copy.31.cx_ref, f32[2048,1]{1,0:T(8,128)} %copy.32.cy_ref, f32[2048,1]{1,0:T(8,128)} %copy.33.cz_ref, ...), custom_call_target="tpu_custom_call" | custom-call | tf_op jit(solution)/shard_map/pallas_call | solution.py:177
  41.3 0.1 collective-permute-start.2
  41.4 1.4 %collective-permute-done.2 = f32[13,1024]{1,0:T(8,128)S(1)} collective-permute-done((f32[13,1024]{1,0:T(8,128)}, f32[13,1024]{1,0:T(8,128)S(1)}, u32[]{:S(2)}, u32[]{:S(2)}) %collective-permute-start.2) | collective-permute-done | bytes 53280 | tf_op jit(solution)/shard_map/ppermute | solution.py:253
  42.8 0.9 add.588
  43.8 3.1 %collective-permute-start.3 = (f32[16,3,256]{2,1,0:T(4,128)S(1)}, f32[16,3,256]{2,1,0:T(4,128)S(1)}, u32[]{:S(2)}, u32[]{:S(2)}) collective-permute-start(f32[16,3,256]{2,1,0:T(4,128)S(1)} %get-tuple-element.18), channel_id=1, source_target_pairs={{0,2},{2,4},{4,6},{6,8},{8,10},{10,12},{12,14},{14,16},{16,18},{18... | collective-permute-start | bytes 147464 | tf_op jit(solution)/shard_map/ppermute | solution.py:116
  46.9 2.7 %collective-permute-start.4 = (f32[16,3,256]{2,1,0:T(4,128)S(1)}, f32[16,3,256]{2,1,0:T(4,128)S(1)}, u32[]{:S(2)}, u32[]{:S(2)}) collective-permute-start(f32[16,3,256]{2,1,0:T(4,128)S(1)} %get-tuple-element.19), channel_id=1, source_target_pairs={{2,0},{4,2},{6,4},{8,6},{10,8},{12,10},{14,12},{16,14},{18,16},{20... | collective-permute-start | bytes 147464 | tf_op jit(solution)/shard_map/ppermute | solution.py:117
  49.6 0.6 fusion.48
  50.2 3.3 %collective-permute-start.5 = (f32[]{:T(128)}, f32[]{:T(128)}, u32[]{:S(2)}, u32[]{:S(2)}) collective-permute-start(f32[]{:T(128)} %fusion.48), channel_id=1, source_target_pairs={{0,2},{2,0},{4,6},{6,4},{1,3},{3,1},{5,7},{7,5},{8,10},{10,8},{12,... | collective-permute-start | bytes 20 | tf_op jit(solution)/shard_map/ppermute | solution.py:46
  53.5 1.8 %collective-permute-done.5 = f32[]{:T(128)} collective-permute-done((f32[]{:T(128)}, f32[]{:T(128)}, u32[]{:S(2)}, u32[]{:S(2)}) %collective-permute-start.5) | collective-permute-done | bytes 36 | tf_op jit(solution)/shard_map/ppermute | solution.py:46
  56.5 4.4 %collective-permute-start.6 = (f32[]{:T(128)}, f32[]{:T(128)}, u32[]{:S(2)}, u32[]{:S(2)}) collective-permute-start(f32[]{:T(128)} %add.612), channel_id=1, source_target_pairs={{0,4},{2,6},{4,0},{6,2},{1,5},{3,7},{5,1},{7,3},{8,12},{10,14},{12... | collective-permute-start | bytes 20 | tf_op jit(solution)/shard_map/ppermute | solution.py:46
  60.9 0.9 collective-permute-done.6
  62.4 10.0 %psum.14 = f32[]{:T(128)} all-reduce(f32[]{:T(128)S(6)} %add.613), channel_id=1, replica_groups=mesh['sz'=8,'sy'=4,'sx'=4,'vel'=2] {'sy'}, use_global_device_ids=true, to_apply=%region_2.3 | all-reduce | flops 1 | bytes 8 | tf_op jit(solution)/shard_map/psum | solution.py:257
  72.4 1.0 copy.37
  73.4 23.5 %psum.15 = f32[]{:T(128)} all-reduce(f32[]{:T(128)} %psum.14), channel_id=1, replica_groups=mesh['sz'=8,'sy'=4,'sx'=4,'vel'=2] {'sz'}, use_global_device_ids=true, to_apply=%region_3.4 | all-reduce | flops 1 | bytes 8 | tf_op jit(solution)/shard_map/psum | solution.py:257
  97.7 0.1 broadcast_multiply_fusion.1
  97.8 0.3 reshape.296
  98.1 0.5 fusion.2
  98.6 0.4 reshape.297
  99.1 0.2 reshape.298
  99.3 0.4 fusion.5
  99.7 0.3 reshape.299
  100.0 0.1 fusion.11
  100.1 0.2 reshape.300
  100.3 0.3 fusion.8
  100.6 0.2 reshape.301
  100.8 0.7 broadcast_multiply_fusion.2
  101.5 0.6 copy.41
  102.1 10.1 %shard_map.60 = bf16[2048,4,256]{2,1,0:T(4,128)(2,1)} custom-call(bf16[2048,1024]{1,0:T(8,128)(2,1)} %get-tuple-element.4.star_ref, bf16[2048,13]{1,0:T(8,128)(2,1)} %bitcast.55, bf16[13,1024]{1,0:T(8,128)(2,1)} %bitcast.56, f32[1,1024]{1,0:T(1,128)} %bitcast.64), custom_call_target="tpu_custom_call" | custom-call | tf_op jit(solution)/shard_map/pallas_call | solution.py:209
  (42 shorter events, 0.5 us)
Async XLA Ops:
  3.9 2.0 %copy-start = (bf16[256,8,4,256]{3,1,2,0:T(8,128)(2,1)}, bf16[256,8,4,256]{3,1,2,0:T(8,128)(2,1)S(1)}, u32[]{:S(2)}) copy-start(bf16[256,8,4,256]{3,1,2,0:T(8,128)(2,1)S(1)} %copy.38) | copy-start | bytes 12582916
  3.9 11.4 %copy-start.4 = (s32[4,256]{1,0:T(4,128)S(1)}, s32[4,256]{1,0:T(4,128)}, u32[]{:S(2)}) copy-start(s32[4,256]{1,0:T(4,128)} %param.6) | copy-start | bytes 12292
  3.9 13.4 %copy-start.3 = (f32[4,256]{1,0:T(4,128)S(1)}, f32[4,256]{1,0:T(4,128)}, u32[]{:S(2)}) copy-start(f32[4,256]{1,0:T(4,128)} %param.5) | copy-start | bytes 12292
  6.0 15.6 %collective-permute-start = (bf16[1024,256]{1,0:T(8,128)(2,1)S(1)}, bf16[1024,256]{1,0:T(8,128)(2,1)S(1)}, u32[]{:S(2)}, u32[]{:S(2)}) collective-permute-start(bf16[1024,256]{1,0:T(8,128)(2,1)S(1)} %get-tuple-element.11), channel_id=1, source_target_pairs={{0,2},{2,4},{4,6},{6,8},{8,10},{10,12},{12,14},{14,16},{16,18},{18... | collective-permute-start | bytes 1572872 | tf_op jit(solution)/shard_map/ppermute | solution.py:239
  9.4 15.3 %collective-permute-start.1 = (bf16[1024,256]{1,0:T(8,128)(2,1)S(1)}, bf16[1024,256]{1,0:T(8,128)(2,1)S(1)}, u32[]{:S(2)}, u32[]{:S(2)}) collective-permute-start(bf16[1024,256]{1,0:T(8,128)(2,1)S(1)} %get-tuple-element.10), channel_id=1, source_target_pairs={{2,0},{4,2},{6,4},{8,6},{10,8},{12,10},{14,12},{16,14},{18,16},{20... | collective-permute-start | bytes 1572872 | tf_op jit(solution)/shard_map/ppermute | solution.py:240
  21.5 3.1 %copy-start.1 = (bf16[1024,256]{1,0:T(8,128)(2,1)}, bf16[1024,256]{1,0:T(8,128)(2,1)S(1)}, u32[]{:S(2)}) copy-start(bf16[1024,256]{1,0:T(8,128)(2,1)S(1)} %collective-permute-done.left_ref) | copy-start | bytes 1572868
  24.6 0.8 copy-start.2
  25.5 15.9 %copy-start.5 = (s32[4,256]{1,0:T(4,128)S(1)}, s32[4,256]{1,0:T(4,128)}, u32[]{:S(2)}) copy-start(s32[4,256]{1,0:T(4,128)} %param.7) | copy-start | bytes 12292
  41.3 1.6 %collective-permute-start.2 = (f32[13,1024]{1,0:T(8,128)}, f32[13,1024]{1,0:T(8,128)S(1)}, u32[]{:S(2)}, u32[]{:S(2)}) collective-permute-start(f32[13,1024]{1,0:T(8,128)} %get-tuple-element.5), channel_id=1, source_target_pairs={{0,1},{1,0},{2,3},{3,2},{4,5},{5,4},{6,7},{7,6},{8,9},{9,8},{10,11... | collective-permute-start | bytes 159752 | tf_op jit(solution)/shard_map/ppermute | solution.py:253
  43.8 53.9 %collective-permute-start.3 = (f32[16,3,256]{2,1,0:T(4,128)S(1)}, f32[16,3,256]{2,1,0:T(4,128)S(1)}, u32[]{:S(2)}, u32[]{:S(2)}) collective-permute-start(f32[16,3,256]{2,1,0:T(4,128)S(1)} %get-tuple-element.18), channel_id=1, source_target_pairs={{0,2},{2,4},{4,6},{6,8},{8,10},{10,12},{12,14},{14,16},{16,18},{18... | collective-permute-start | bytes 147464 | tf_op jit(solution)/shard_map/ppermute | solution.py:116
  46.9 50.8 %collective-permute-start.4 = (f32[16,3,256]{2,1,0:T(4,128)S(1)}, f32[16,3,256]{2,1,0:T(4,128)S(1)}, u32[]{:S(2)}, u32[]{:S(2)}) collective-permute-start(f32[16,3,256]{2,1,0:T(4,128)S(1)} %get-tuple-element.19), channel_id=1, source_target_pairs={{2,0},{4,2},{6,4},{8,6},{10,8},{12,10},{14,12},{16,14},{18,16},{20... | collective-permute-start | bytes 147464 | tf_op jit(solution)/shard_map/ppermute | solution.py:117
  50.2 5.1 %collective-permute-start.5 = (f32[]{:T(128)}, f32[]{:T(128)}, u32[]{:S(2)}, u32[]{:S(2)}) collective-permute-start(f32[]{:T(128)} %fusion.48), channel_id=1, source_target_pairs={{0,2},{2,0},{4,6},{6,4},{1,3},{3,1},{5,7},{7,5},{8,10},{10,8},{12,... | collective-permute-start | bytes 20 | tf_op jit(solution)/shard_map/ppermute | solution.py:46
  56.5 5.3 %collective-permute-start.6 = (f32[]{:T(128)}, f32[]{:T(128)}, u32[]{:S(2)}, u32[]{:S(2)}) collective-permute-start(f32[]{:T(128)} %add.612), channel_id=1, source_target_pairs={{0,4},{2,6},{4,0},{6,2},{1,5},{3,7},{5,1},{7,3},{8,12},{10,14},{12... | collective-permute-start | bytes 20 | tf_op jit(solution)/shard_map/ppermute | solution.py:46

commit v15 on v13

--- a/solution.py
+++ b/solution.py
@@ -168,7 +168,7 @@
         part_ref[...] += partial
 
 
-def advance(adj, left, right, cx, cy, cz, coll, fluid, weigh, block=256):
+def advance(adj, left, right, cx, cy, cz, coll, fluid, weigh, block=512):
     nv, lanes = adj.shape
     nm = weigh.shape[0]
     grid = (nv // block,)

time: 112 us -> 112 us (level)
  no operation moved by 1% of the time
where the time goes in v15:
time: 112 us
  blocking collectives  45.2 us (40%)
  Pallas kernels  25.8 us (23%)
  local copies, waits for them, and re-layouts  15.2 us (14%)
  starting transfers between devices  11.8 us (11%)
  waiting for transfers between devices  6.06 us (5%)
  other arithmetic  6.03 us (5%)
  between operations  1.7 us (2%)
    psum x3, blocking collectives, on_device(): squares = lax.psum(squares, axis)  45.2 us
    pallas_call x1, Pallas kernels, advance(): pl.pallas_call(advance_kernel, grid=grid, in_specs=[pl.BlockSpec((block,...  15.7 us
    pallas_call x1, Pallas kernels, correct(): pl.pallas_call(correct_kernel, grid=(nv // block,), in_specs=[pl.BlockSpe...  10.1 us
    unnamed x18, local copies, waits for them, and re-layouts  8.95 us
    ppermute x1, starting transfers between devices, on_device(): left = lax.ppermute(tail, SPACE_AXES, [(i, i + 1) for i in range(ends)])  3.4 us
    ppermute x1, waiting for transfers between devices, on_device(): right = lax.ppermute(head, SPACE_AXES, [(i + 1, i) for i in range(ends)])  3.12 us
    ppermute x1, starting transfers between devices, sweep_all(): lax.ppermute(pack[:, width - depth:], SPACE_AXES, [(i, i + 1) for i in ra...  3.11 us
    ppermute x1, starting transfers between devices, sweep_all(): lax.ppermute(pack[:, :depth], SPACE_AXES, [(i + 1, i) for i in range(ends)])  2.74 us
  transfers between devices with their start and end apart: 5, of which 3 were waited for; matrix products, arithmetic and copies ran while one was open for 9% of the time, Pallas kernels for 0%

profile of v15, /device:TPU:10, one launch (start us, length us, event | category | flops | bytes accessed | tf_op | source)
XLA Modules:
  0.0 111.7 jit_solution(7819801618826753083)
XLA Ops:
  0.6 3.2 %copy.38 = bf16[256,8,4,256]{3,1,2,0:T(8,128)(2,1)S(1)} copy(bf16[256,8,4,256]{3,2,1,0:T(4,128)(2,1)} %bitcast.54) | data formatting | bytes 8388608
  3.9 0.0 copy-start.4
  3.9 2.0 %copy-done = bf16[256,8,4,256]{3,1,2,0:T(8,128)(2,1)} copy-done((bf16[256,8,4,256]{3,1,2,0:T(8,128)(2,1)}, bf16[256,8,4,256]{3,1,2,0:T(8,128)(2,1)S(1)}, u32[]{:S(2)}) %copy-start) | copy-done | bytes 4194328
  5.9 0.1 slice_bitcast_fusion
  6.0 3.4 %collective-permute-start = (bf16[1024,256]{1,0:T(8,128)(2,1)S(1)}, bf16[1024,256]{1,0:T(8,128)(2,1)S(1)}, u32[]{:S(2)}, u32[]{:S(2)}) collective-permute-start(bf16[1024,256]{1,0:T(8,128)(2,1)S(1)} %get-tuple-element.11), channel_id=1, source_target_pairs={{0,2},{2,4},{4,6},{6,8},{8,10},{10,12},{12,14},{14,16},{16,18},{18... | collective-permute-start | bytes 1572872 | tf_op jit(solution)/shard_map/ppermute | solution.py:239
  9.4 2.4 %collective-permute-start.1 = (bf16[1024,256]{1,0:T(8,128)(2,1)S(1)}, bf16[1024,256]{1,0:T(8,128)(2,1)S(1)}, u32[]{:S(2)}, u32[]{:S(2)}) collective-permute-start(bf16[1024,256]{1,0:T(8,128)(2,1)S(1)} %get-tuple-element.10), channel_id=1, source_target_pairs={{2,0},{4,2},{6,4},{8,6},{10,8},{12,10},{14,12},{16,14},{18,16},{20... | collective-permute-start | bytes 1572872 | tf_op jit(solution)/shard_map/ppermute | solution.py:240
  11.8 0.1 fusion.34
  11.9 0.1 multiply_multiply_fusion
  12.0 0.1 multiply_multiply_fusion.2
  12.1 0.1 subtract_multiply_fusion.1
  12.2 0.1 broadcast_multiply_fusion.3
  12.3 0.1 fusion.50
  12.5 1.3 %copy.31.cx_ref = f32[2048,1]{1,0:T(8,128)} copy(f32[2048,1]{0,1:T(1,128)S(1)} %bitcast.65) | data formatting | bytes 16384 | tf_op jit(solution)/shard_map/reshape | solution.py:246
  13.9 1.4 %copy.32.cy_ref = f32[2048,1]{1,0:T(8,128)} copy(f32[2048,1]{0,1:T(1,128)S(1)} %bitcast.66) | data formatting | bytes 16384 | tf_op jit(solution)/shard_map/reshape | solution.py:247
  15.3 1.4 %copy.33.cz_ref = f32[2048,1]{1,0:T(8,128)} copy(f32[2048,1]{0,1:T(1,128)S(1)} %bitcast.67) | data formatting | bytes 16384 | tf_op jit(solution)/shard_map/reshape | solution.py:248
  16.7 0.6 copy.40
  17.3 0.6 copy.39
  17.9 0.3 stack.8
  18.2 0.6 fusion.47
  18.8 1.2 %multiply_convert_fusion = (bf16[13,2048]{1,0:T(8,128)(2,1)S(1)}, bf16[13,2048]{1,0:T(8,128)(2,1)}) fusion(f32[13,4096]{1,0:T(8,128)S(1)} %stack.8, s32[]{:T(128)S(6)} %select_n.297, f32[2048]{0:T(1024)S(1)} %dynamic-slice.6, f32[]{:T(128)} %fusion.47, f32[2048]{0:T(1024)S(1)} %dynamic-slice.4), kind=kLoop, calls=%fused_computation.28 | loop fusion | flops 133120 | bytes 229384 | tf_op jit(solution)/shard_map/convert_element_type | solution.py:85
  20.0 1.5 %collective-permute-done.left_ref = bf16[1024,256]{1,0:T(8,128)(2,1)S(1)} collective-permute-done((bf16[1024,256]{1,0:T(8,128)(2,1)S(1)}, bf16[1024,256]{1,0:T(8,128)(2,1)S(1)}, u32[]{:S(2)}, u32[]{:S(2)}) %collective-permute-start) | collective-permute-done | bytes 524320 | tf_op jit(solution)/shard_map/ppermute | solution.py:239
  21.5 3.1 %collective-permute-done.1.right_ref = bf16[1024,256]{1,0:T(8,128)(2,1)S(1)} collective-permute-done((bf16[1024,256]{1,0:T(8,128)(2,1)S(1)}, bf16[1024,256]{1,0:T(8,128)(2,1)S(1)}, u32[]{:S(2)}, u32[]{:S(2)}) %collective-permute-start.1) | collective-permute-done | bytes 524320 | tf_op jit(solution)/shard_map/ppermute | solution.py:240
  24.6 0.9 copy-done.2
  25.5 15.7 %shard_map.59 = (bf16[2048,1024]{1,0:T(8,128)(2,1)}, f32[13,1024]{1,0:T(8,128)}) custom-call(bf16[2048,1024]{1,0:T(8,128)(2,1)} %bitcast.53, bf16[1024,256]{1,0:T(8,128)(2,1)} %copy-done.1, bf16[1024,256]{1,0:T(8,128)(2,1)} %copy-done.2, f32[2048,1]{1,0:T(8,128)} %copy.31.cx_ref, f32[2048,1]{1,0:T(8,128)} %copy.32.cy_ref, f32[2048,1]{1,0:T(8,128)} %copy.33.cz_ref, ...), custom_call_target="tpu_custom_call" | custom-call | tf_op jit(solution)/shard_map/pallas_call | solution.py:177
  41.2 0.1 collective-permute-start.2
  41.3 1.4 %collective-permute-done.2 = f32[13,1024]{1,0:T(8,128)S(1)} collective-permute-done((f32[13,1024]{1,0:T(8,128)}, f32[13,1024]{1,0:T(8,128)S(1)}, u32[]{:S(2)}, u32[]{:S(2)}) %collective-permute-start.2) | collective-permute-done | bytes 53280 | tf_op jit(solution)/shard_map/ppermute | solution.py:253
  42.7 0.9 add.584
  43.7 3.1 %collective-permute-start.3 = (f32[16,3,256]{2,1,0:T(4,128)S(1)}, f32[16,3,256]{2,1,0:T(4,128)S(1)}, u32[]{:S(2)}, u32[]{:S(2)}) collective-permute-start(f32[16,3,256]{2,1,0:T(4,128)S(1)} %get-tuple-element.18), channel_id=1, source_target_pairs={{0,2},{2,4},{4,6},{6,8},{8,10},{10,12},{12,14},{14,16},{16,18},{18... | collective-permute-start | bytes 147464 | tf_op jit(solution)/shard_map/ppermute | solution.py:116
  46.8 2.7 %collective-permute-start.4 = (f32[16,3,256]{2,1,0:T(4,128)S(1)}, f32[16,3,256]{2,1,0:T(4,128)S(1)}, u32[]{:S(2)}, u32[]{:S(2)}) collective-permute-start(f32[16,3,256]{2,1,0:T(4,128)S(1)} %get-tuple-element.19), channel_id=1, source_target_pairs={{2,0},{4,2},{6,4},{8,6},{10,8},{12,10},{14,12},{16,14},{18,16},{20... | collective-permute-start | bytes 147464 | tf_op jit(solution)/shard_map/ppermute | solution.py:117
  49.5 0.6 fusion.48
  50.2 11.6 %psum.21 = f32[]{:T(128)} all-reduce(f32[]{:T(128)} %fusion.48), channel_id=1, replica_groups=mesh['sz'=8,'sy'=4,'sx'=4,'vel'=2] {'sx'}, use_global_device_ids=true, to_apply=%region_2.3 | all-reduce | flops 1 | bytes 8 | tf_op jit(solution)/shard_map/psum | solution.py:257
  61.8 9.6 %psum.22 = f32[]{:T(128)} all-reduce(f32[]{:T(128)} %psum.21), channel_id=1, replica_groups=mesh['sz'=8,'sy'=4,'sx'=4,'vel'=2] {'sy'}, use_global_device_ids=true, to_apply=%region_3.4 | all-reduce | flops 1 | bytes 8 | tf_op jit(solution)/shard_map/psum | solution.py:257
  71.3 1.1 copy.37
  72.4 24.0 %psum.23 = f32[]{:T(128)} all-reduce(f32[]{:T(128)} %psum.22), channel_id=1, replica_groups=mesh['sz'=8,'sy'=4,'sx'=4,'vel'=2] {'sz'}, use_global_device_ids=true, to_apply=%region_4.5 | all-reduce | flops 1 | bytes 8 | tf_op jit(solution)/shard_map/psum | solution.py:257
  97.2 0.1 broadcast_multiply_fusion.1
  97.3 0.3 reshape.296
  97.6 0.5 fusion.2
  98.1 0.4 reshape.297
  98.6 0.2 reshape.298
  98.8 0.4 fusion.5
  99.2 0.3 reshape.299
  99.5 0.1 fusion.11
  99.6 0.2 reshape.300
  99.8 0.3 fusion.8
  100.1 0.2 reshape.301
  100.3 0.7 broadcast_multiply_fusion.2
  101.0 0.6 copy.41
  101.7 10.1 %shard_map.60 = bf16[2048,4,256]{2,1,0:T(4,128)(2,1)} custom-call(bf16[2048,1024]{1,0:T(8,128)(2,1)} %get-tuple-element.4.star_ref, bf16[2048,13]{1,0:T(8,128)(2,1)} %bitcast.55, bf16[13,1024]{1,0:T(8,128)(2,1)} %bitcast.56, f32[1,1024]{1,0:T(1,128)} %bitcast.64), custom_call_target="tpu_custom_call" | custom-call | tf_op jit(solution)/shard_map/pallas_call | solution.py:209
  (39 shorter events, 0.4 us)
Async XLA Ops:
  3.9 2.0 %copy-start = (bf16[256,8,4,256]{3,1,2,0:T(8,128)(2,1)}, bf16[256,8,4,256]{3,1,2,0:T(8,128)(2,1)S(1)}, u32[]{:S(2)}) copy-start(bf16[256,8,4,256]{3,1,2,0:T(8,128)(2,1)S(1)} %copy.38) | copy-start | bytes 12582916
  3.9 11.4 %copy-start.4 = (s32[4,256]{1,0:T(4,128)S(1)}, s32[4,256]{1,0:T(4,128)}, u32[]{:S(2)}) copy-start(s32[4,256]{1,0:T(4,128)} %param.6) | copy-start | bytes 12292
  3.9 13.4 %copy-start.3 = (f32[4,256]{1,0:T(4,128)S(1)}, f32[4,256]{1,0:T(4,128)}, u32[]{:S(2)}) copy-start(f32[4,256]{1,0:T(4,128)} %param.5) | copy-start | bytes 12292
  6.0 15.6 %collective-permute-start = (bf16[1024,256]{1,0:T(8,128)(2,1)S(1)}, bf16[1024,256]{1,0:T(8,128)(2,1)S(1)}, u32[]{:S(2)}, u32[]{:S(2)}) collective-permute-start(bf16[1024,256]{1,0:T(8,128)(2,1)S(1)} %get-tuple-element.11), channel_id=1, source_target_pairs={{0,2},{2,4},{4,6},{6,8},{8,10},{10,12},{12,14},{14,16},{16,18},{18... | collective-permute-start | bytes 1572872 | tf_op jit(solution)/shard_map/ppermute | solution.py:239
  9.4 15.3 %collective-permute-start.1 = (bf16[1024,256]{1,0:T(8,128)(2,1)S(1)}, bf16[1024,256]{1,0:T(8,128)(2,1)S(1)}, u32[]{:S(2)}, u32[]{:S(2)}) collective-permute-start(bf16[1024,256]{1,0:T(8,128)(2,1)S(1)} %get-tuple-element.10), channel_id=1, source_target_pairs={{2,0},{4,2},{6,4},{8,6},{10,8},{12,10},{14,12},{16,14},{18,16},{20... | collective-permute-start | bytes 1572872 | tf_op jit(solution)/shard_map/ppermute | solution.py:240
  21.5 3.1 %copy-start.1 = (bf16[1024,256]{1,0:T(8,128)(2,1)}, bf16[1024,256]{1,0:T(8,128)(2,1)S(1)}, u32[]{:S(2)}) copy-start(bf16[1024,256]{1,0:T(8,128)(2,1)S(1)} %collective-permute-done.left_ref) | copy-start | bytes 1572868
  24.6 0.9 copy-start.2
  25.5 15.8 %copy-start.5 = (s32[4,256]{1,0:T(4,128)S(1)}, s32[4,256]{1,0:T(4,128)}, u32[]{:S(2)}) copy-start(s32[4,256]{1,0:T(4,128)} %param.7) | copy-start | bytes 12292
  41.2 1.6 %collective-permute-start.2 = (f32[13,1024]{1,0:T(8,128)}, f32[13,1024]{1,0:T(8,128)S(1)}, u32[]{:S(2)}, u32[]{:S(2)}) collective-permute-start(f32[13,1024]{1,0:T(8,128)} %get-tuple-element.5), channel_id=1, source_target_pairs={{0,1},{1,0},{2,3},{3,2},{4,5},{5,4},{6,7},{7,6},{8,9},{9,8},{10,11... | collective-permute-start | bytes 159752 | tf_op jit(solution)/shard_map/ppermute | solution.py:253
  43.7 53.4 %collective-permute-start.3 = (f32[16,3,256]{2,1,0:T(4,128)S(1)}, f32[16,3,256]{2,1,0:T(4,128)S(1)}, u32[]{:S(2)}, u32[]{:S(2)}) collective-permute-start(f32[16,3,256]{2,1,0:T(4,128)S(1)} %get-tuple-element.18), channel_id=1, source_target_pairs={{0,2},{2,4},{4,6},{6,8},{8,10},{10,12},{12,14},{14,16},{16,18},{18... | collective-permute-start | bytes 147464 | tf_op jit(solution)/shard_map/ppermute | solution.py:116
  46.8 50.3 %collective-permute-start.4 = (f32[16,3,256]{2,1,0:T(4,128)S(1)}, f32[16,3,256]{2,1,0:T(4,128)S(1)}, u32[]{:S(2)}, u32[]{:S(2)}) collective-permute-start(f32[16,3,256]{2,1,0:T(4,128)S(1)} %get-tuple-element.19), channel_id=1, source_target_pairs={{2,0},{4,2},{6,4},{8,6},{10,8},{12,10},{14,12},{16,14},{18,16},{20... | collective-permute-start | bytes 147464 | tf_op jit(solution)/shard_map/ppermute | solution.py:117
